TPU v7x, 512 devices: a whole 4x4x16 slice. The times are simulated.
512 devices in a mesh: tile: 64 (over z, x), image: 2 (over y_hi), tensor: 4 (over y_lo, core).
Axes of the slice: x: 4, y: 4 (y_hi: 2, y_lo: 2; y = y_hi * 2 + y_lo), z: 16, core: 2. Of those that a mesh axis runs over, the one named last changes fastest.
Arguments:
- latent: bfloat16 [2, 256, 640, 128], P('image', 'tile', 'tensor'), may hold values from -8 to 8
- tile_slot: int32 [2, 64], replicated, may hold values from 0 to 63, each once within a row
- tile_count: int32 [2], replicated, may hold values from 16 to 64, as said below
- merge_num: int32 [1], replicated, may hold values from 3 to 13
- conv_ema: bfloat16 [3, 3, 4, 2, 80, 640], P(None, None, 'tensor', 'image'), may hold values from -0.078125 to 0.078125
- conv_adjusted: bfloat16 [3, 3, 4, 2, 80, 640], P(None, None, 'tensor', 'image'), may hold values from -0.078125 to 0.078125
- query_ema: bfloat16 [640, 512], P('image', 'tensor'), may hold values from -4 to 4
- query_adjusted: bfloat16 [640, 512], P('image', 'tensor'), may hold values from -4 to 4
- kv_ema: bfloat16 [640, 2, 512], P('image', None, 'tensor'), may hold values from -4 to 4
- kv_adjusted: bfloat16 [640, 2, 512], P('image', None, 'tensor'), may hold values from -4 to 4
- out_ema: bfloat16 [640, 512], P('tensor', 'image'), may hold values from -0.25 to 0.25
- out_adjusted: bfloat16 [640, 512], P('tensor', 'image'), may hold values from -0.25 to 0.25
- norm_gain: bfloat16 [640], replicated, may hold values from 0.099609375 to 1.8984375
Outputs:
- denoised: bfloat16 [2, 256, 640, 128], P('image', 'tile', 'tensor')
Inputs may be any that keep to these rules, and one draw needn't show every extreme that they name: `tile_count`: the number of live tiles of each image; exactly one image has all 64 live, the others fewer. `tile_slot`: each row is a permutation of the tiles' vertical positions.
All inputs are finite; a program needn't handle non-finite values.
Results may differ from a plain program's by a relative error of at most 0.007.
The roundings to bfloat16 on the way count: a program that leaves them out, or rounds other values in their place, can miss the bound.
Values may be sent and summed in bfloat16 or wider, within the bound.
No kernel may reach another device: no remote copies, remote signals or barrier semaphores. Data moves between devices by JAX's collectives and lax.ppermute only.
A program may use at most 64 MiB of HBM per device.

v0:
```python
import jax
import jax.numpy as jnp
from jax import lax
from jax.sharding import PartitionSpec as P

HD = 64
POOL = 4


def blend(ema_part, adjusted_part, blend_ratio):
    base = ema_part.astype(jnp.float32)
    return (base + blend_ratio * (adjusted_part.astype(jnp.float32) - base)).astype(jnp.bfloat16)


def convolve(field, kernel, row_padding):
    return lax.conv_general_dilated(
        field[None],
        kernel,
        (1, 1),
        (row_padding, (1, 1)),
        dimension_numbers=("NHCW", "HWOI", "NHCW"),
        preferred_element_type=jnp.float32,
    )[0]


def slot_lookup(tile_ids, slot_row):
    tile_total = slot_row.shape[0]
    matches = tile_ids[:, None] == jnp.arange(tile_total, dtype=jnp.int32)[None, :]
    return jnp.sum(jnp.where(matches, slot_row[None, :], 0), axis=1)


def on_device(
    latent,
    tile_slot,
    tile_count,
    merge_num,
    conv_ema,
    conv_adjusted,
    query_ema,
    query_adjusted,
    kv_ema,
    kv_adjusted,
    out_ema,
    out_adjusted,
    norm_gain,
):
    image_index = lax.axis_index("image")
    tile_index = lax.axis_index("tile")
    slot_row = lax.dynamic_index_in_dim(tile_slot, image_index, 0, keepdims=False)
    live_count = lax.dynamic_index_in_dim(tile_count, image_index, 0, keepdims=False)
    my_slot = lax.dynamic_index_in_dim(slot_row, tile_index, 0, keepdims=False)
    live_flag = (my_slot < live_count).astype(jnp.float32)
    blend_ratio = merge_num[0].astype(jnp.float32) / 16.0
    gathered = (
        lax.all_gather(conv_ema, "image", axis=3, tiled=True),
        lax.all_gather(conv_adjusted, "image", axis=3, tiled=True),
        lax.all_gather(query_ema, "image", axis=0, tiled=True),
        lax.all_gather(query_adjusted, "image", axis=0, tiled=True),
        lax.all_gather(kv_ema, "image", axis=0, tiled=True),
        lax.all_gather(kv_adjusted, "image", axis=0, tiled=True),
        lax.all_gather(out_ema, "image", axis=1, tiled=True),
        lax.all_gather(out_adjusted, "image", axis=1, tiled=True),
    )
    conv_w = blend(gathered[0], gathered[1], blend_ratio)
    query_w = blend(gathered[2], gathered[3], blend_ratio)
    kv_w = blend(gathered[4], gathered[5], blend_ratio)
    out_w = blend(gathered[6], gathered[7], blend_ratio)
    conv_w = conv_w.reshape(3, 3, -1, conv_w.shape[-1])
    feats = latent[0]
    tile_rows, chan_shard, tile_cols = feats.shape
    activated = jax.nn.silu(feats.astype(jnp.float32)).astype(jnp.bfloat16)
    block_full = lax.all_gather(activated, "tensor", axis=1, tiled=True)
    rim_rows = jnp.stack([activated[0], activated[-1]])[None]
    shard_piece = lax.all_gather(rim_rows, "tile", axis=0, tiled=True)
    source = jnp.arange(shard_piece.shape[0], dtype=jnp.int32)
    source_slot = slot_lookup(source, slot_row)
    upper_w = (source_slot == my_slot - 1).astype(jnp.float32)
    lower_w = jnp.logical_and(source_slot == my_slot + 1, source_slot < live_count).astype(
        jnp.float32
    )
    piece_f = shard_piece.astype(jnp.float32)
    upper = jnp.einsum("n,ncw->cw", upper_w, piece_f[:, 1])
    lower = jnp.einsum("n,ncw->cw", lower_w, piece_f[:, 0])
    halo_rows = jnp.stack([upper, lower]).astype(jnp.bfloat16)
    halo_full = lax.all_gather(halo_rows, "tensor", axis=1, tiled=True)
    padded = jnp.concatenate([halo_full[0:1], block_full, halo_full[1:2]], axis=0)
    conv_out = convolve(padded, conv_w, (0, 0))
    section = (feats.astype(jnp.float32) + conv_out).astype(jnp.bfloat16)
    section_full = lax.all_gather(section, "tensor", axis=1, tiled=True)
    channels = section_full.shape[1]
    cells = tile_rows * tile_cols
    section_f = section_full.astype(jnp.float32)
    rows_f = jnp.transpose(section_f, (0, 2, 1)).reshape(cells, channels)
    root_mean = jnp.sqrt(jnp.mean(rows_f * rows_f, axis=-1) + 1e-06)
    normed = (rows_f * norm_gain.astype(jnp.float32) / root_mean[:, None]).astype(jnp.bfloat16)
    queries = (jnp.dot(normed, query_w, preferred_element_type=jnp.float32) * HD ** (-0.5)).astype(
        jnp.bfloat16
    )
    att_shard = queries.shape[1]
    head_count = att_shard // HD
    pooled = section_f.reshape(tile_rows // POOL, POOL, channels, tile_cols // POOL, POOL).mean(
        axis=(1, 4)
    )
    tok_count = pooled.shape[0] * pooled.shape[2]
    pooled = jnp.transpose(pooled, (0, 2, 1)).astype(jnp.bfloat16).reshape(tok_count, channels)
    kv_flat = kv_w.reshape(channels, 2 * att_shard)
    block_rows = min(512, cells)
    blocks = cells // block_rows
    query_blocks = queries.reshape(blocks, block_rows, head_count, HD)
    start_state = (
        jnp.full((blocks, block_rows, head_count), -1e30, jnp.float32),
        jnp.zeros((blocks, block_rows, head_count), jnp.float32),
        jnp.zeros((blocks, block_rows, head_count, HD), jnp.float32),
    )
    kv_rows = jnp.dot(
        lax.all_gather(pooled, "tile", axis=0, tiled=True),
        kv_flat,
        preferred_element_type=jnp.float32,
    ).astype(jnp.bfloat16)
    key_rows = kv_rows[:, :att_shard]
    key_total = key_rows.shape[0]
    key_tile = jnp.arange(key_total, dtype=jnp.int32) // tok_count
    key_live = slot_lookup(key_tile, slot_row) < live_count
    key_livef = key_live.astype(jnp.float32)
    key_heads = key_rows.reshape(key_total, head_count, HD)
    value_heads = kv_rows[:, att_shard:].reshape(key_total, head_count, HD)

    def per_block(inputs):
        query_part, max_part, total_part, accum_part = inputs
        max_list, total_list, accum_list = ([], [], [])
        for head_index in range(head_count):
            scores = lax.dot_general(
                query_part[:, head_index],
                key_heads[:, head_index],
                (((1,), (1,)), ((), ())),
                preferred_element_type=jnp.float32,
            )
            scores = jnp.where(key_live[None, :], scores, -1e30)
            max_new = jnp.maximum(max_part[:, head_index], jnp.max(scores, axis=1))
            expd = jnp.exp(scores - max_new[:, None]) * key_livef[None, :]
            shrink = jnp.exp(max_part[:, head_index] - max_new)
            max_list.append(max_new)
            total_list.append(total_part[:, head_index] * shrink + jnp.sum(expd, axis=1))
            accum_list.append(
                accum_part[:, head_index] * shrink[:, None]
                + jnp.dot(
                    expd.astype(jnp.bfloat16),
                    value_heads[:, head_index],
                    preferred_element_type=jnp.float32,
                )
            )
        return (
            jnp.stack(max_list, axis=1),
            jnp.stack(total_list, axis=1),
            jnp.stack(accum_list, axis=1),
        )

    final_state = lax.map(per_block, (query_blocks, start_state[0], start_state[1], start_state[2]))
    attended = (
        (final_state[2] / final_state[1][..., None]).astype(jnp.bfloat16).reshape(cells, att_shard)
    )
    shard_piece = jax.tree.map(
        lambda part: lax.all_gather(part, "tensor", axis=1, tiled=True), attended
    )
    weight_cols = lax.slice_in_dim(out_w, 0, shard_piece.shape[1], axis=1)
    projected = jnp.zeros((chan_shard, cells), jnp.float32) + lax.dot_general(
        weight_cols, shard_piece, (((1,), (1,)), ((), ())), preferred_element_type=jnp.float32
    )
    projected = jnp.transpose(projected.reshape(chan_shard, tile_rows, tile_cols), (1, 0, 2))
    final = (section.astype(jnp.float32) + projected) * live_flag
    return final.astype(jnp.bfloat16).reshape(1, tile_rows, chan_shard, tile_cols)


def solution(mesh):
    placed = (
        P("image", "tile", "tensor", None),
        P(),
        P(),
        P(),
        P(None, None, "tensor", "image", None, None),
        P(None, None, "tensor", "image", None, None),
        P("image", "tensor"),
        P("image", "tensor"),
        P("image", None, "tensor"),
        P("image", None, "tensor"),
        P("tensor", "image"),
        P("tensor", "image"),
        P(),
    )
    return jax.shard_map(
        on_device,
        mesh=mesh,
        in_specs=placed,
        out_specs=P("image", "tile", "tensor", None),
        check_vma=False,
    )
```

profile of v0, /device:TPU:1, one launch (start us, length us, event | category | flops | bytes accessed | tf_op | source)
XLA Modules:
  0.0 443.0 jit_solution(12450239543727953347)
XLA Ops:
  6.5 0.7 all-gather.7.cloned.1.call-update
  8.1 1.0 fusion.54
  13.0 13.6 %all_gather.44 = bf16[4,640,128]{2,0,1:T(4,128)(2,1)S(1)} all-gather(bf16[4,160,128]{2,0,1:T(4,128)(2,1)S(1)} %copy.107), channel_id=1, replica_groups=mesh['tile'=64,'image'=2,'tensor'=4] {'tensor'}, dimensions={1}, use_global_device_ids=true | all-gather | bytes 819200 | tf_op jit(solution)/shard_map/all_gather | solution.py:72
  26.6 30.2 %all-gather.7.cloned.1.call-done = bf16[3,3,1,2,80,640]{5,4,3,2,1,0:T(8,128)(2,1)} async-done(((bf16[3,3,1,1,80,640]{5,4,3,2,1,0:T(8,128)(2,1)}), bf16[3,3,1,2,80,640]{5,4,3,2,1,0:T(8,128)(2,1)}) %all-gather.7.cloned.1.call-update) | async-done | bytes 1843216 | tf_op jit(solution)/shard_map/all_gather | solution.py:55
  56.8 43.6 %all-gather.9.cloned.1.call-done = bf16[3,3,1,2,80,640]{5,4,3,2,1,0:T(8,128)(2,1)} async-done(((bf16[3,3,1,1,80,640]{5,4,3,2,1,0:T(8,128)(2,1)}), bf16[3,3,1,2,80,640]{5,4,3,2,1,0:T(8,128)(2,1)}) %all-gather.9.cloned.1.call-update) | async-done | bytes 1843216 | tf_op jit(solution)/shard_map/all_gather | solution.py:56
  100.4 4.0 fusion.1
  104.4 139.5 %all-gather.11.cloned.1.call-done = bf16[128,160,128]{2,1,0:T(8,128)(2,1)} async-done(((bf16[2,160,128]{2,1,0:T(8,128)(2,1)}), bf16[128,160,128]{2,1,0:T(8,128)(2,1)}) %all-gather.11.cloned.1.call-update) | async-done | bytes 5242896 | tf_op jit(solution)/shard_map/all_gather | solution.py:74
  243.9 2.9 slice_bitcast_fusion.1
  246.8 0.8 fusion.10
  247.6 1.4 fusion.8
  249.1 15.5 %all_gather.43 = bf16[2,640,128]{2,1,0:T(8,128)(2,1)S(1)} all-gather(bf16[2,160,128]{2,1,0:T(8,128)(2,1)S(1)} %pad_maximum_fusion.2), channel_id=1, replica_groups=mesh['tile'=64,'image'=2,'tensor'=4] {'tensor'}, dimensions={1}, use_global_device_ids=true | all-gather | bytes 409600 | tf_op jit(solution)/shard_map/all_gather | solution.py:85
  265.1 1.1 maximum_bitcast_fusion
  266.3 1.2 copy.129
  268.4 1.2 copy-done
  269.6 1.8 convolution_select_fusion
  272.6 8.1 %all_gather.49 = bf16[4,640,128]{2,0,1:T(4,128)(2,1)S(1)} all-gather(bf16[4,160,128]{2,0,1:T(4,128)(2,1)S(1)} %copy.115), channel_id=1, replica_groups=mesh['tile'=64,'image'=2,'tensor'=4] {'tensor'}, dimensions={1}, use_global_device_ids=true | all-gather | bytes 819200 | tf_op jit(solution)/shard_map/all_gather | solution.py:89
  280.7 0.9 copy.116
  283.9 6.1 %all_gather.50 = bf16[640,128]{1,0:T(8,128)(2,1)S(1)} all-gather(bf16[320,128]{1,0:T(8,128)(2,1)S(1)} %copy-done.4), channel_id=1, replica_groups=mesh['tile'=64,'image'=2,'tensor'=4] {'image'}, dimensions={0}, use_global_device_ids=true | all-gather | bytes 245760 | tf_op jit(solution)/shard_map/all_gather | solution.py:57
  289.9 5.5 %all_gather.51 = bf16[640,128]{1,0:T(8,128)(2,1)S(1)} all-gather(bf16[320,128]{1,0:T(8,128)(2,1)S(1)} %copy-done.5), channel_id=1, replica_groups=mesh['tile'=64,'image'=2,'tensor'=4] {'image'}, dimensions={0}, use_global_device_ids=true | all-gather | bytes 245760 | tf_op jit(solution)/shard_map/all_gather | solution.py:58
  295.4 5.5 %all_gather.47 = bf16[160,512]{1,0:T(8,128)(2,1)S(1)} all-gather(bf16[160,256]{1,0:T(8,128)(2,1)S(1)} %copy-done.6), channel_id=1, replica_groups=mesh['tile'=64,'image'=2,'tensor'=4] {'image'}, dimensions={1}, use_global_device_ids=true | all-gather | bytes 245760 | tf_op jit(solution)/shard_map/all_gather | solution.py:61
  300.9 5.5 %all_gather.48 = bf16[160,512]{1,0:T(8,128)(2,1)S(1)} all-gather(bf16[160,256]{1,0:T(8,128)(2,1)S(1)} %copy-done.7), channel_id=1, replica_groups=mesh['tile'=64,'image'=2,'tensor'=4] {'image'}, dimensions={1}, use_global_device_ids=true | all-gather | bytes 245760 | tf_op jit(solution)/shard_map/all_gather | solution.py:62
  306.3 6.4 %all_gather.53 = bf16[640,2,128]{2,1,0:T(2,128)(2,1)S(1)} all-gather(bf16[320,2,128]{2,1,0:T(2,128)(2,1)S(1)} %copy-done.2), channel_id=1, replica_groups=mesh['tile'=64,'image'=2,'tensor'=4] {'image'}, dimensions={0}, use_global_device_ids=true | all-gather | bytes 491520 | tf_op jit(solution)/shard_map/all_gather | solution.py:59
  312.7 6.9 %all_gather.54 = bf16[640,2,128]{2,1,0:T(2,128)(2,1)S(1)} all-gather(bf16[320,2,128]{2,1,0:T(2,128)(2,1)S(1)} %copy-done.3), channel_id=1, replica_groups=mesh['tile'=64,'image'=2,'tensor'=4] {'image'}, dimensions={0}, use_global_device_ids=true | all-gather | bytes 491520 | tf_op jit(solution)/shard_map/all_gather | solution.py:60
  321.7 88.4 %all-gather.13.cloned.1.call-done = bf16[1,2048,640]{2,1,0:T(8,128)(2,1)} async-done(((bf16[1,32,640]{2,1,0:T(8,128)(2,1)}), bf16[1,2048,640]{2,1,0:T(8,128)(2,1)}) %all-gather.13.cloned.1.call-update) | async-done | bytes 2621456 | tf_op jit(solution)/shard_map/all_gather | solution.py:116
  410.2 2.8 fusion.12
  413.0 0.7 fusion.61
  413.7 1.1 select_reduce_fusion.1
  414.8 2.1 fusion.2
  417.0 1.0 fusion.35
  418.1 1.0 fusion.41
  419.2 16.3 %all_gather.55 = bf16[512,512]{0,1:T(8,128)(2,1)S(1)} all-gather(bf16[512,128]{0,1:T(8,128)(2,1)S(1)} %fusion.63), channel_id=1, replica_groups=mesh['tile'=64,'image'=2,'tensor'=4] {'tensor'}, dimensions={1}, use_global_device_ids=true | all-gather | bytes 655360 | tf_op jit(solution)/shard_map/all_gather | solution.py:163
  435.7 0.7 fusion.64
  (73 shorter events, 8.8 us)
Async XLA Ops:
  6.5 3.4 copy-start.9
  6.5 4.5 %copy-start.10 = (s32[2]{0:T(128)S(1)}, s32[2]{0:T(128)}, u32[]{:S(2)}) copy-start(s32[2]{0:T(128)} %param.15) | copy-start | bytes 28
  6.5 50.2 %all-gather.7.cloned.1.call-start = ((), (), s32[]{:S(2)}) async-start(), calls=%async_computation | async-start | bytes 2764800 | tf_op jit(solution)/shard_map/all_gather | solution.py:55
  7.3 93.1 %all-gather.9.cloned.1.call-start = ((), (), s32[]{:S(2)}) async-start(), calls=%async_computation.1 | async-start | bytes 2764800 | tf_op jit(solution)/shard_map/all_gather | solution.py:56
  8.0 235.9 %all-gather.11.cloned.1.call-start = ((), (), s32[]{:S(2)}) async-start(), calls=%async_computation.2 | async-start | bytes 5324800 | tf_op jit(solution)/shard_map/all_gather | solution.py:74
  9.8 400.4 %all-gather.13.cloned.1.call-start = ((), (), s32[]{:S(2)}) async-start(), calls=%async_computation.3 | async-start | bytes 2662400 | tf_op jit(solution)/shard_map/all_gather | solution.py:116
  267.7 0.7 copy-start.11
  268.1 1.5 copy-start
  271.5 0.9 copy-start.1
  272.4 11.4 %copy-start.8 = (bf16[640]{0:T(1024)(128)(2,1)S(1)}, bf16[640]{0:T(1024)(128)(2,1)}, u32[]{:S(2)}) copy-start(bf16[640]{0:T(1024)(128)(2,1)} %param.25) | copy-start | bytes 3844
  272.4 11.4 %copy-start.4 = (bf16[320,128]{1,0:T(8,128)(2,1)S(1)}, bf16[320,128]{1,0:T(8,128)(2,1)}, u32[]{:S(2)}) copy-start(bf16[320,128]{1,0:T(8,128)(2,1)} %param.19) | copy-start | bytes 245764
  272.5 17.5 %copy-start.5 = (bf16[320,128]{1,0:T(8,128)(2,1)S(1)}, bf16[320,128]{1,0:T(8,128)(2,1)}, u32[]{:S(2)}) copy-start(bf16[320,128]{1,0:T(8,128)(2,1)} %param.20) | copy-start | bytes 245764
  272.5 22.9 %copy-start.6 = (bf16[160,256]{1,0:T(8,128)(2,1)S(1)}, bf16[160,256]{1,0:T(8,128)(2,1)}, u32[]{:S(2)}) copy-start(bf16[160,256]{1,0:T(8,128)(2,1)} %param.23) | copy-start | bytes 245764
  272.6 28.3 %copy-start.7 = (bf16[160,256]{1,0:T(8,128)(2,1)S(1)}, bf16[160,256]{1,0:T(8,128)(2,1)}, u32[]{:S(2)}) copy-start(bf16[160,256]{1,0:T(8,128)(2,1)} %param.24) | copy-start | bytes 245764
  272.6 33.7 %copy-start.2 = (bf16[320,2,128]{2,1,0:T(2,128)(2,1)S(1)}, bf16[320,2,128]{2,1,0:T(2,128)(2,1)}, u32[]{:S(2)}) copy-start(bf16[320,2,128]{2,1,0:T(2,128)(2,1)} %param.21) | copy-start | bytes 491524
  280.7 32.0 %copy-start.3 = (bf16[320,2,128]{2,1,0:T(2,128)(2,1)S(1)}, bf16[320,2,128]{2,1,0:T(2,128)(2,1)}, u32[]{:S(2)}) copy-start(bf16[320,2,128]{2,1,0:T(2,128)(2,1)} %param.22) | copy-start | bytes 491524
Sparse Core Ops, SparseCore 0:
  9.4 47.2 all-gather.6
  58.9 41.4 all-gather.8
  103.3 140.5 all-gather.10
  282.8 127.3 all-gather.12
where the time goes:
time: 443 us
  waiting for transfers between devices  303 us (68%)
  blocking collectives  89.3 us (20%)
  between operations  16.5 us (4%)
  other arithmetic  12.5 us (3%)
  matrix products  11.4 us (3%)
  local copies, waits for them, and re-layouts  10.1 us (2%)
    all_gather x1, waiting for transfers between devices, on_device(): shard_piece = lax.all_gather(rim_rows, 'tile', axis=0, tiled=True)  140 us
    all_gather x1, waiting for transfers between devices, on_device(): lax.all_gather(pooled, 'tile', axis=0, tiled=True)  88.4 us
    all_gather x1, waiting for transfers between devices, on_device(): lax.all_gather(conv_adjusted, 'image', axis=3, tiled=True)  43.6 us
    all_gather x1, waiting for transfers between devices, on_device(): lax.all_gather(conv_ema, 'image', axis=3, tiled=True)  30.2 us
    all_gather x1, blocking collectives, on_device(): lax.all_gather(part, 'tensor', axis=1, tiled=True)  16.3 us
    all_gather x1, blocking collectives, on_device(): halo_full = lax.all_gather(halo_rows, 'tensor', axis=1, tiled=True)  15.5 us
    all_gather x1, blocking collectives, on_device(): block_full = lax.all_gather(activated, 'tensor', axis=1, tiled=True)  13.6 us
  transfers between devices with their start and end apart: 4, of which 4 were waited for; matrix products, arithmetic and copies ran while one was open for 2% of the time, Pallas kernels for 0%

commit v1 on v0

v1 whole, which is shorter than its diff:
```python
import numpy as np
import jax
import jax.numpy as jnp
from jax import lax
from jax.sharding import Mesh
from jax.sharding import PartitionSpec as P

HD = 64
POOL = 4
TILE_AXES = ("tz", "tx")


def blend(ema_part, adjusted_part, blend_ratio):
    base = ema_part.astype(jnp.float32)
    return (base + blend_ratio * (adjusted_part.astype(jnp.float32) - base)).astype(jnp.bfloat16)


def convolve(field, kernel, row_padding):
    return lax.conv_general_dilated(
        field[None],
        kernel,
        (1, 1),
        (row_padding, (1, 1)),
        dimension_numbers=("NHCW", "HWOI", "NHCW"),
        preferred_element_type=jnp.float32,
    )[0]


def slot_lookup(tile_ids, slot_row):
    tile_total = slot_row.shape[0]
    matches = tile_ids[:, None] == jnp.arange(tile_total, dtype=jnp.int32)[None, :]
    return jnp.sum(jnp.where(matches, slot_row[None, :], 0), axis=1)


def image_pair(part, image_index, axis):
    other = lax.ppermute(part, "image", [(0, 1), (1, 0)])
    first = jnp.where(image_index == 0, part, other)
    second = jnp.where(image_index == 0, other, part)
    return jnp.concatenate([first, second], axis=axis)


def tile_gather(part):
    inner = lax.all_gather(part, "tx", axis=0, tiled=False)
    outer = lax.all_gather(inner, "tz", axis=0, tiled=False)
    return outer.reshape((-1,) + part.shape)


def on_device(
    latent,
    tile_slot,
    tile_count,
    merge_num,
    conv_ema,
    conv_adjusted,
    query_ema,
    query_adjusted,
    kv_ema,
    kv_adjusted,
    out_ema,
    out_adjusted,
    norm_gain,
):
    image_index = lax.axis_index("image")
    tile_index = lax.axis_index("tz") * lax.axis_size("tx") + lax.axis_index("tx")
    slot_row = lax.dynamic_index_in_dim(tile_slot, image_index, 0, keepdims=False)
    live_count = lax.dynamic_index_in_dim(tile_count, image_index, 0, keepdims=False)
    my_slot = lax.dynamic_index_in_dim(slot_row, tile_index, 0, keepdims=False)
    live_flag = (my_slot < live_count).astype(jnp.float32)
    blend_ratio = merge_num[0].astype(jnp.float32) / 16.0

    feats = latent[0]
    tile_rows, chan_shard, tile_cols = feats.shape
    activated = jax.nn.silu(feats.astype(jnp.float32)).astype(jnp.bfloat16)
    rim_rows = jnp.stack([activated[0], activated[-1]])
    shard_piece = tile_gather(rim_rows)

    conv_w = image_pair(blend(conv_ema, conv_adjusted, blend_ratio), image_index, 3)
    query_w = image_pair(blend(query_ema, query_adjusted, blend_ratio), image_index, 0)
    kv_w = image_pair(blend(kv_ema, kv_adjusted, blend_ratio), image_index, 0)
    out_w = image_pair(blend(out_ema, out_adjusted, blend_ratio), image_index, 1)
    conv_w = conv_w.reshape(3, 3, -1, conv_w.shape[-1])

    tile_total = shard_piece.shape[0]
    tiles = jnp.arange(tile_total, dtype=jnp.int32)
    upper_src = jnp.sum(jnp.where(slot_row == my_slot - 1, tiles, 0))
    lower_src = jnp.sum(jnp.where(slot_row == my_slot + 1, tiles, 0))
    has_upper = my_slot > 0
    has_lower = my_slot + 1 < live_count
    upper = lax.dynamic_index_in_dim(shard_piece, upper_src, 0, keepdims=False)[1]
    lower = lax.dynamic_index_in_dim(shard_piece, lower_src, 0, keepdims=False)[0]
    upper = jnp.where(has_upper, upper, jnp.zeros_like(upper))
    lower = jnp.where(has_lower, lower, jnp.zeros_like(lower))
    stacked = jnp.concatenate([upper[None], activated, lower[None]], axis=0)
    padded = lax.all_gather(stacked, "tensor", axis=1, tiled=True)
    conv_out = convolve(padded, conv_w, (0, 0))
    section = (feats.astype(jnp.float32) + conv_out).astype(jnp.bfloat16)
    section_full = lax.all_gather(section, "tensor", axis=1, tiled=True)
    channels = section_full.shape[1]
    cells = tile_rows * tile_cols
    section_f = section_full.astype(jnp.float32)
    rows_f = jnp.transpose(section_f, (0, 2, 1)).reshape(cells, channels)
    root_mean = jnp.sqrt(jnp.mean(rows_f * rows_f, axis=-1) + 1e-06)
    normed = (rows_f * norm_gain.astype(jnp.float32) / root_mean[:, None]).astype(jnp.bfloat16)
    queries = (jnp.dot(normed, query_w, preferred_element_type=jnp.float32) * HD ** (-0.5)).astype(
        jnp.bfloat16
    )
    att_shard = queries.shape[1]
    head_count = att_shard // HD
    pooled = section_f.reshape(tile_rows // POOL, POOL, channels, tile_cols // POOL, POOL).mean(
        axis=(1, 4)
    )
    tok_count = pooled.shape[0] * pooled.shape[2]
    pooled = jnp.transpose(pooled, (0, 2, 1)).astype(jnp.bfloat16).reshape(tok_count, channels)
    kv_flat = kv_w.reshape(channels, 2 * att_shard)
    kv_local = jnp.dot(pooled, kv_flat, preferred_element_type=jnp.float32).astype(jnp.bfloat16)
    kv_rows = tile_gather(kv_local).reshape(-1, 2 * att_shard)
    key_rows = kv_rows[:, :att_shard]
    key_total = key_rows.shape[0]
    key_tile = jnp.arange(key_total, dtype=jnp.int32) // tok_count
    key_live = slot_lookup(key_tile, slot_row) < live_count
    key_livef = key_live.astype(jnp.float32)
    key_heads = key_rows.reshape(key_total, head_count, HD)
    value_heads = kv_rows[:, att_shard:].reshape(key_total, head_count, HD)

    total_list, accum_list = [], []
    for head_index in range(head_count):
        scores = lax.dot_general(
            queries[:, head_index * HD:(head_index + 1) * HD],
            key_heads[:, head_index],
            (((1,), (1,)), ((), ())),
            preferred_element_type=jnp.float32,
        )
        scores = jnp.where(key_live[None, :], scores, -1e30)
        top = jnp.max(scores, axis=1)
        expd = jnp.exp(scores - top[:, None]) * key_livef[None, :]
        total_list.append(jnp.sum(expd, axis=1))
        accum_list.append(
            jnp.dot(
                expd.astype(jnp.bfloat16),
                value_heads[:, head_index],
                preferred_element_type=jnp.float32,
            )
        )
    totals = jnp.stack(total_list, axis=1)
    accum = jnp.stack(accum_list, axis=1)
    attended = (accum / totals[..., None]).astype(jnp.bfloat16).reshape(cells, att_shard)
    attended_full = lax.all_gather(attended, "tensor", axis=1, tiled=True)
    projected = lax.dot_general(
        out_w, attended_full, (((1,), (1,)), ((), ())), preferred_element_type=jnp.float32
    )
    projected = jnp.transpose(projected.reshape(chan_shard, tile_rows, tile_cols), (1, 0, 2))
    final = (section.astype(jnp.float32) + projected) * live_flag
    return final.astype(jnp.bfloat16).reshape(1, tile_rows, chan_shard, tile_cols)


def solution(mesh):
    tiles = mesh.shape["tile"]
    inner = 4 if tiles % 4 == 0 else 1
    devices = np.asarray(mesh.devices).reshape(
        (tiles // inner, inner, mesh.shape["image"], mesh.shape["tensor"])
    )
    split = Mesh(devices, ("tz", "tx", "image", "tensor"))
    placed = (
        P("image", TILE_AXES, "tensor", None),
        P(),
        P(),
        P(),
        P(None, None, "tensor", "image", None, None),
        P(None, None, "tensor", "image", None, None),
        P("image", "tensor"),
        P("image", "tensor"),
        P("image", None, "tensor"),
        P("image", None, "tensor"),
        P("tensor", "image"),
        P("tensor", "image"),
        P(),
    )
    return jax.shard_map(
        on_device,
        mesh=split,
        in_specs=placed,
        out_specs=P("image", TILE_AXES, "tensor", None),
        check_vma=False,
    )
```

time: 443 us -> 236 us (0.53)
  waiting for transfers between devices: 303 us -> 106 us
  blocking collectives: 89.3 us -> 63.3 us
  starting transfers between devices: 0.12 us -> 16.7 us
  between operations: 16.5 us -> 22.4 us
    all_gather x4 -> x2, waiting for transfers between devices: 302 us -> 103 us  [tile_gather(): outer = lax.all_gather(inner, 'tz', axis=0, tiled=False)]
    all_gather x9 -> x4, blocking collectives: 81.1 us -> 55.3 us  [the longest x2 21.6 us: tile_gather(): inner = lax.all_gather(part, 'tx', axis=0, tiled=False)]
    ppermute x0 -> x4, starting transfers between devices: none -> 16.6 us  [image_pair(): other = lax.ppermute(part, 'image', [(0, 1), (1, 0)])]
    dot_general x8 -> x6, matrix products: 9.17 us -> 4.27 us  [the longest x2 2.08 us: on_device(): jnp.dot(expd.astype(jnp.bfloat16), value_heads[:, head_index], preferred_...]
  transfers between devices with their start and end apart: 4 -> 6, of which waited for: 4 -> 3; matrix products, arithmetic and copies ran while one was open for 2% -> 8% of each run, Pallas kernels for 0% -> 0%
where the time goes in v1:
time: 236 us
  waiting for transfers between devices  106 us (45%)
  blocking collectives  63.3 us (27%)
  between operations  22.4 us (9%)
  starting transfers between devices  16.7 us (7%)
  other arithmetic  13.7 us (6%)
  matrix products  8.01 us (3%)
  local copies, waits for them, and re-layouts  6.01 us (3%)
    all_gather x2, waiting for transfers between devices, tile_gather(): outer = lax.all_gather(inner, 'tz', axis=0, tiled=False)  103 us
    all_gather x2, blocking collectives, tile_gather(): inner = lax.all_gather(part, 'tx', axis=0, tiled=False)  21.6 us
    all_gather x1, blocking collectives, on_device(): attended_full = lax.all_gather(attended, 'tensor', axis=1, tiled=True)  17.1 us
    all_gather x1, blocking collectives, on_device(): padded = lax.all_gather(stacked, 'tensor', axis=1, tiled=True)  16.6 us
    ppermute x4, starting transfers between devices, image_pair(): other = lax.ppermute(part, 'image', [(0, 1), (1, 0)])  16.6 us
    all_gather x1, blocking collectives, on_device(): section_full = lax.all_gather(section, 'tensor', axis=1, tiled=True)  8.01 us
  transfers between devices with their start and end apart: 6, of which 3 were waited for; matrix products, arithmetic and copies ran while one was open for 8% of the time, Pallas kernels for 0%

profile of v1, /device:TPU:1, one launch (start us, length us, event | category | flops | bytes accessed | tf_op | source)
XLA Modules:
  0.0 235.7 jit_solution(440670326737885075)
XLA Ops:
  6.6 1.1 fusion.35
  7.8 11.4 %all-gather = bf16[8,160,128]{2,1,0:T(8,128)(2,1)} all-gather(bf16[2,160,128]{2,1,0:T(8,128)(2,1)S(1)} %pad_maximum_fusion.3), channel_id=2, replica_groups=mesh['tz'=16,'tx'=4,'image'=2,'tensor'=4] {'tx'}, dimensions={0}, use_global_device_ids=true | all-gather | bytes 409600 | tf_op jit(solution)/shard_map/all_gather | solution.py:43
  19.9 1.8 fusion.12
  21.7 5.5 %collective-permute-start = (bf16[3,3,1,1,80,640]{5,4,3,2,1,0:T(8,128)(2,1)S(1)}, bf16[3,3,1,1,80,640]{5,4,3,2,1,0:T(8,128)(2,1)S(1)}, u32[]{:S(2)}, u32[]{:S(2)}) collective-permute-start(bf16[3,3,1,1,80,640]{5,4,3,2,1,0:T(8,128)(2,1)S(1)} %fusion.12), channel_id=1, source_target_pairs={{0,4},{4,0},{1,5},{5,1},{2,6},{6,2},{3,7},{7,3},{8,12},{12,8},{9,1... | collective-permute-start | bytes 2764808 | tf_op jit(solution)/shard_map/ppermute | solution.py:36
  27.5 1.9 collective-permute-start.3
  29.4 0.7 fusion.48
  30.1 4.9 %collective-permute-start.2 = (bf16[320,128]{1,0:T(8,128)(2,1)}, bf16[320,128]{1,0:T(8,128)(2,1)}, u32[]{:S(2)}, u32[]{:S(2)}) collective-permute-start(bf16[320,128]{1,0:T(8,128)(2,1)} %fusion.48), channel_id=1, source_target_pairs={{0,4},{4,0},{1,5},{5,1},{2,6},{6,2},{3,7},{7,3},{8,12},{12,8},{9,1... | collective-permute-start | bytes 245768 | tf_op jit(solution)/shard_map/ppermute | solution.py:36
  35.0 0.7 dynamic_slice.19
  37.0 0.7 fusion.67
  40.9 0.7 dynamic_slice.22
  43.5 2.2 collective-permute-done.3
  45.7 1.1 pad_maximum_fusion.1
  47.0 1.5 pad_maximum_fusion
  48.5 52.7 %all-gather.7.cloned.1.call-done = bf16[64,2,160,128]{3,2,1,0:T(8,128)(2,1)} async-done(((bf16[4,2,160,128]{3,2,1,0:T(8,128)(2,1)}), bf16[64,2,160,128]{3,2,1,0:T(8,128)(2,1)}) %all-gather.7.cloned.1.call-update) | async-done | bytes 5242896 | tf_op jit(solution)/shard_map/all_gather | solution.py:44
  101.2 0.8 fusion.61
  102.0 16.6 %all_gather.37 = bf16[6,640,128]{2,1,0:T(8,128)(2,1)S(1)} all-gather(bf16[6,160,128]{2,1,0:T(8,128)(2,1)S(1)} %pad_maximum_fusion.2), channel_id=1, replica_groups=mesh['tz'=16,'tx'=4,'image'=2,'tensor'=4] {'tensor'}, dimensions={1}, use_global_device_ids=true | all-gather | bytes 1228800 | tf_op jit(solution)/shard_map/all_gather | solution.py:94
  120.1 3.4 %convolution_select_fusion = f32[4,8,17,160]{3,1,2,0:T(8,128)S(1)} fusion(bf16[3,3,160,640]{3,2,1,0:T(8,128)(2,1)} %bitcast.115, bf16[6,640,1,7,2]{1,3,4,0,2:T(8,128)(2,1)S(1)} %slice.54, bf16[6,640,1,8,17]{1,3,4,0,2:T(8,128)(2,1)S(1)} %copy.96, pred[8,17]{0,1:T(8,128)(4,1)S(1)} %copy-done.11), kind=kOutput, calls=%fused_computation.24 | convolution fusion | flops 1006289920 | bytes 3343496 | tf_op jit(solution)/shard_map/conv_general_dilated | solution.py:19
  124.2 8.0 %all_gather.38 = bf16[4,640,128]{2,0,1:T(4,128)(2,1)S(1)} all-gather(bf16[4,160,128]{2,0,1:T(4,128)(2,1)S(1)} %copy.99), channel_id=1, replica_groups=mesh['tz'=16,'tx'=4,'image'=2,'tensor'=4] {'tensor'}, dimensions={1}, use_global_device_ids=true | all-gather | bytes 819200 | tf_op jit(solution)/shard_map/all_gather | solution.py:97
  132.2 0.9 copy.100
  133.6 10.1 %all-gather.2 = bf16[128,256]{1,0:T(8,128)(2,1)} all-gather(bf16[32,256]{1,0:T(8,128)(2,1)S(1)} %convolution_convert_fusion), channel_id=4, replica_groups=mesh['tz'=16,'tx'=4,'image'=2,'tensor'=4] {'tx'}, dimensions={0}, use_global_device_ids=true | all-gather | bytes 81920 | tf_op jit(solution)/shard_map/all_gather | solution.py:43
  143.9 4.4 %collective-permute-start.1 = (bf16[160,256]{1,0:T(8,128)(2,1)S(1)}, bf16[160,256]{1,0:T(8,128)(2,1)S(1)}, u32[]{:S(2)}, u32[]{:S(2)}) collective-permute-start(bf16[160,256]{1,0:T(8,128)(2,1)S(1)} %fusion.46), channel_id=1, source_target_pairs={{0,4},{4,0},{1,5},{5,1},{2,6},{6,2},{3,7},{7,3},{8,12},{12,8},{9,1... | collective-permute-start | bytes 245768 | tf_op jit(solution)/shard_map/ppermute | solution.py:36
  148.4 0.7 fusion.77
  150.5 0.9 broadcast_select_fusion.5
  152.3 50.7 %all-gather.9.cloned.1.call-done = bf16[64,32,256]{2,1,0:T(8,128)(2,1)} async-done(((bf16[4,32,256]{2,1,0:T(8,128)(2,1)}), bf16[64,32,256]{2,1,0:T(8,128)(2,1)}) %all-gather.9.cloned.1.call-update) | async-done | bytes 1048592 | tf_op jit(solution)/shard_map/all_gather | solution.py:44
  203.0 1.3 fusion.79
  204.7 0.7 fusion.42
  205.4 1.1 select_reduce_fusion.1
  206.5 2.1 fusion
  208.6 1.0 fusion.23
  209.7 1.0 fusion.26
  210.8 17.1 %all_gather.43 = bf16[512,512]{0,1:T(8,128)(2,1)S(1)} all-gather(bf16[512,128]{0,1:T(8,128)(2,1)S(1)} %bitcast.122), channel_id=1, replica_groups=mesh['tz'=16,'tx'=4,'image'=2,'tensor'=4] {'tensor'}, dimensions={1}, use_global_device_ids=true | all-gather | bytes 655360 | tf_op jit(solution)/shard_map/all_gather | solution.py:147
  228.2 0.7 fusion.49
  (65 shorter events, 4.9 us)
Async XLA Ops:
  6.5 20.7 %copy-start.2 = (bf16[320,2,128]{2,1,0:T(2,128)(2,1)S(1)}, bf16[320,2,128]{2,1,0:T(2,128)(2,1)}, u32[]{:S(2)}) copy-start(bf16[320,2,128]{2,1,0:T(2,128)(2,1)} %param.21) | copy-start | bytes 491524
  6.5 20.7 %copy-start.3 = (bf16[320,2,128]{2,1,0:T(2,128)(2,1)S(1)}, bf16[320,2,128]{2,1,0:T(2,128)(2,1)}, u32[]{:S(2)}) copy-start(bf16[320,2,128]{2,1,0:T(2,128)(2,1)} %param.22) | copy-start | bytes 491524
  6.5 22.9 %copy-start.4 = (bf16[320,128]{1,0:T(8,128)(2,1)S(1)}, bf16[320,128]{1,0:T(8,128)(2,1)}, u32[]{:S(2)}) copy-start(bf16[320,128]{1,0:T(8,128)(2,1)} %param.19) | copy-start | bytes 245764
  6.5 22.9 %copy-start.5 = (bf16[320,128]{1,0:T(8,128)(2,1)S(1)}, bf16[320,128]{1,0:T(8,128)(2,1)}, u32[]{:S(2)}) copy-start(bf16[320,128]{1,0:T(8,128)(2,1)} %param.20) | copy-start | bytes 245764
  6.5 28.4 %copy-start.9 = (s32[2,64]{1,0:T(2,128)S(1)}, s32[2,64]{1,0:T(2,128)}, u32[]{:S(2)}) copy-start(s32[2,64]{1,0:T(2,128)} %param.14) | copy-start | bytes 1540
  6.5 34.3 %copy-start.10 = (s32[2]{0:T(128)S(1)}, s32[2]{0:T(128)}, u32[]{:S(2)}) copy-start(s32[2]{0:T(128)} %param.15) | copy-start | bytes 28
  6.6 94.6 %all-gather.7.cloned.1.call-start = ((), (), s32[]{:S(2)}) async-start(), calls=%async_computation | async-start | bytes 5570560 | tf_op jit(solution)/shard_map/all_gather | solution.py:44
  19.2 183.8 %all-gather.9.cloned.1.call-start = ((), (), s32[]{:S(2)}) async-start(), calls=%async_computation.1 | async-start | bytes 1114112 | tf_op jit(solution)/shard_map/all_gather | solution.py:44
  21.7 25.1 %collective-permute-start = (bf16[3,3,1,1,80,640]{5,4,3,2,1,0:T(8,128)(2,1)S(1)}, bf16[3,3,1,1,80,640]{5,4,3,2,1,0:T(8,128)(2,1)S(1)}, u32[]{:S(2)}, u32[]{:S(2)}) collective-permute-start(bf16[3,3,1,1,80,640]{5,4,3,2,1,0:T(8,128)(2,1)S(1)} %fusion.12), channel_id=1, source_target_pairs={{0,4},{4,0},{1,5},{5,1},{2,6},{6,2},{3,7},{7,3},{8,12},{12,8},{9,1... | collective-permute-start | bytes 2764808 | tf_op jit(solution)/shard_map/ppermute | solution.py:36
  27.5 18.2 %collective-permute-start.3 = (bf16[320,2,128]{2,1,0:T(2,128)(2,1)S(1)}, bf16[320,2,128]{2,1,0:T(2,128)(2,1)S(1)}, u32[]{:S(2)}, u32[]{:S(2)}) collective-permute-start(bf16[320,2,128]{2,1,0:T(2,128)(2,1)S(1)} %fusion.31), channel_id=1, source_target_pairs={{0,4},{4,0},{1,5},{5,1},{2,6},{6,2},{3,7},{7,3},{8,12},{12,8},{9,1... | collective-permute-start | bytes 491528 | tf_op jit(solution)/shard_map/ppermute | solution.py:36
  30.1 120.4 %collective-permute-start.2 = (bf16[320,128]{1,0:T(8,128)(2,1)}, bf16[320,128]{1,0:T(8,128)(2,1)}, u32[]{:S(2)}, u32[]{:S(2)}) collective-permute-start(bf16[320,128]{1,0:T(8,128)(2,1)} %fusion.48), channel_id=1, source_target_pairs={{0,4},{4,0},{1,5},{5,1},{2,6},{6,2},{3,7},{7,3},{8,12},{12,8},{9,1... | collective-permute-start | bytes 245768 | tf_op jit(solution)/shard_map/ppermute | solution.py:36
  118.6 1.5 copy-start.11
  120.1 3.9 %copy-start.1 = (bf16[1,4,160,128]{3,2,1,0:T(8,128)(2,1)S(1)}, bf16[1,4,160,128]{3,2,1,0:T(8,128)(2,1)}, u32[]{:S(2)}) copy-start(bf16[1,4,160,128]{3,2,1,0:T(8,128)(2,1)} %param.13) | copy-start | bytes 491524
  123.5 10.0 %copy-start = (bf16[640,2,128]{2,1,0:T(2,128)(2,1)S(1)}, bf16[640,2,128]{2,1,0:T(2,128)(2,1)}, u32[]{:S(2)}) copy-start(bf16[640,2,128]{2,1,0:T(2,128)(2,1)} %pad_maximum_fusion.1) | copy-start | bytes 983044
  123.5 20.3 %copy-start.6 = (bf16[160,256]{1,0:T(8,128)(2,1)S(1)}, bf16[160,256]{1,0:T(8,128)(2,1)}, u32[]{:S(2)}) copy-start(bf16[160,256]{1,0:T(8,128)(2,1)} %param.23) | copy-start | bytes 245764
  123.5 20.3 %copy-start.7 = (bf16[160,256]{1,0:T(8,128)(2,1)S(1)}, bf16[160,256]{1,0:T(8,128)(2,1)}, u32[]{:S(2)}) copy-start(bf16[160,256]{1,0:T(8,128)(2,1)} %param.24) | copy-start | bytes 245764
  123.8 26.7 %copy-start.8 = (bf16[640]{0:T(1024)(128)(2,1)S(1)}, bf16[640]{0:T(1024)(128)(2,1)}, u32[]{:S(2)}) copy-start(bf16[640]{0:T(1024)(128)(2,1)} %param.25) | copy-start | bytes 3844
  143.9 7.6 %collective-permute-start.1 = (bf16[160,256]{1,0:T(8,128)(2,1)S(1)}, bf16[160,256]{1,0:T(8,128)(2,1)S(1)}, u32[]{:S(2)}, u32[]{:S(2)}) collective-permute-start(bf16[160,256]{1,0:T(8,128)(2,1)S(1)} %fusion.46), channel_id=1, source_target_pairs={{0,4},{4,0},{1,5},{5,1},{2,6},{6,2},{3,7},{7,3},{8,12},{12,8},{9,1... | collective-permute-start | bytes 245768 | tf_op jit(solution)/shard_map/ppermute | solution.py:36
Sparse Core Ops, SparseCore 0:
  19.3 81.7 all-gather.6
  143.9 59.0 all-gather.8

commit v2 on v1

--- a/solution.py
+++ b/solution.py
@@ -39,10 +39,36 @@
     return jnp.concatenate([first, second], axis=axis)
 
 
-def tile_gather(part):
-    inner = lax.all_gather(part, "tx", axis=0, tiled=False)
-    outer = lax.all_gather(inner, "tz", axis=0, tiled=False)
-    return outer.reshape((-1,) + part.shape)
+def owner_of(slot, slot_row):
+    tiles = jnp.arange(slot_row.shape[0], dtype=jnp.int32)
+    return jnp.sum(jnp.where(slot_row == slot, tiles, 0))
+
+
+def halo_rows(rims, slot_row, my_slot, tz_i, tx_i, n_x):
+    column = lax.all_gather(rims, "tz", axis=0, tiled=False)
+    received = [None]
+    for shift in range(1, n_x):
+        dest_tile = tz_i * n_x + (tx_i + shift) % n_x
+        dest_slot = lax.dynamic_index_in_dim(slot_row, dest_tile, 0, keepdims=False)
+        up_src = owner_of(dest_slot - 1, slot_row)
+        down_src = owner_of(dest_slot + 1, slot_row)
+        up_part = lax.dynamic_index_in_dim(column, up_src // n_x, 0, keepdims=False)[1]
+        down_part = lax.dynamic_index_in_dim(column, down_src // n_x, 0, keepdims=False)[0]
+        up_part = jnp.where(up_src % n_x == tx_i, up_part, jnp.zeros_like(up_part))
+        down_part = jnp.where(down_src % n_x == tx_i, down_part, jnp.zeros_like(down_part))
+        chunk = jnp.stack([up_part, down_part])
+        received.append(
+            lax.ppermute(chunk, "tx", [(i, (i + shift) % n_x) for i in range(n_x)])
+        )
+    up_src = owner_of(my_slot - 1, slot_row)
+    down_src = owner_of(my_slot + 1, slot_row)
+    up_shift = (tx_i - up_src % n_x) % n_x
+    down_shift = (tx_i - down_src % n_x) % n_x
+    up_own = lax.dynamic_index_in_dim(column, up_src // n_x, 0, keepdims=False)[1]
+    down_own = lax.dynamic_index_in_dim(column, down_src // n_x, 0, keepdims=False)[0]
+    upper = lax.select_n(up_shift, up_own, *[piece[0] for piece in received[1:]])
+    lower = lax.select_n(down_shift, down_own, *[piece[1] for piece in received[1:]])
+    return upper, lower
 
 
 def on_device(
@@ -72,7 +98,10 @@
     tile_rows, chan_shard, tile_cols = feats.shape
     activated = jax.nn.silu(feats.astype(jnp.float32)).astype(jnp.bfloat16)
     rim_rows = jnp.stack([activated[0], activated[-1]])
-    shard_piece = tile_gather(rim_rows)
+    n_x = lax.axis_size("tx")
+    upper, lower = halo_rows(
+        rim_rows, slot_row, my_slot, lax.axis_index("tz"), lax.axis_index("tx"), n_x
+    )
 
     conv_w = image_pair(blend(conv_ema, conv_adjusted, blend_ratio), image_index, 3)
     query_w = image_pair(blend(query_ema, query_adjusted, blend_ratio), image_index, 0)
@@ -80,14 +109,8 @@
     out_w = image_pair(blend(out_ema, out_adjusted, blend_ratio), image_index, 1)
     conv_w = conv_w.reshape(3, 3, -1, conv_w.shape[-1])
 
-    tile_total = shard_piece.shape[0]
-    tiles = jnp.arange(tile_total, dtype=jnp.int32)
-    upper_src = jnp.sum(jnp.where(slot_row == my_slot - 1, tiles, 0))
-    lower_src = jnp.sum(jnp.where(slot_row == my_slot + 1, tiles, 0))
     has_upper = my_slot > 0
     has_lower = my_slot + 1 < live_count
-    upper = lax.dynamic_index_in_dim(shard_piece, upper_src, 0, keepdims=False)[1]
-    lower = lax.dynamic_index_in_dim(shard_piece, lower_src, 0, keepdims=False)[0]
     upper = jnp.where(has_upper, upper, jnp.zeros_like(upper))
     lower = jnp.where(has_lower, lower, jnp.zeros_like(lower))
     stacked = jnp.concatenate([upper[None], activated, lower[None]], axis=0)
@@ -113,10 +136,17 @@
     pooled = jnp.transpose(pooled, (0, 2, 1)).astype(jnp.bfloat16).reshape(tok_count, channels)
     kv_flat = kv_w.reshape(channels, 2 * att_shard)
     kv_local = jnp.dot(pooled, kv_flat, preferred_element_type=jnp.float32).astype(jnp.bfloat16)
-    kv_rows = tile_gather(kv_local).reshape(-1, 2 * att_shard)
+    kv_column = lax.all_gather(kv_local, "tz", axis=0, tiled=False)
+    kv_all = lax.all_gather(kv_column, "tx", axis=0, tiled=False)
+    n_z = kv_all.shape[1]
+    kv_rows = kv_all.reshape(-1, 2 * att_shard)
     key_rows = kv_rows[:, :att_shard]
     key_total = key_rows.shape[0]
-    key_tile = jnp.arange(key_total, dtype=jnp.int32) // tok_count
+    key_tile = (
+        jnp.arange(n_x, dtype=jnp.int32)[:, None, None]
+        + n_x * jnp.arange(n_z, dtype=jnp.int32)[None, :, None]
+        + jnp.zeros((1, 1, tok_count), jnp.int32)
+    ).reshape(-1)
     key_live = slot_lookup(key_tile, slot_row) < live_count
     key_livef = key_live.astype(jnp.float32)
     key_heads = key_rows.reshape(key_total, head_count, HD)

time: 236 us -> 211 us (0.89)
  waiting for transfers between devices: 106 us -> 49.8 us
  between operations: 22.4 us -> 42.6 us
  starting transfers between devices: 16.7 us -> 24.5 us
  other arithmetic: 13.7 us -> 16.9 us
    all_gather x2, waiting for transfers between devices: 103 us -> 48.7 us  [the longest x1 29.2 us: on_device(): kv_all = lax.all_gather(kv_column, 'tx', axis=0, tiled=False)]
    ppermute x0 -> x3, starting transfers between devices: none -> 10 us  [halo_rows(): lax.ppermute(chunk, 'tx', [(i, (i + shift) % n_x) for i in range(n_x)])]
    all_gather x1, blocking collectives: 17.1 us -> 8.59 us  [on_device(): attended_full = lax.all_gather(attended, 'tensor', axis=1, tiled=True)]
    all_gather x1, blocking collectives: 16.6 us -> 20.6 us  [on_device(): padded = lax.all_gather(stacked, 'tensor', axis=1, tiled=True)]
    all_gather x2 -> x1, blocking collectives: 21.6 us -> 25.1 us  [on_device(): kv_column = lax.all_gather(kv_local, 'tz', axis=0, tiled=False)]
  transfers between devices with their start and end apart: 6 -> 9, of which waited for: 3 -> 3; matrix products, arithmetic and copies ran while one was open for 8% -> 10% of each run, Pallas kernels for 0% -> 0%
where the time goes in v2:
time: 211 us; the launch traced here: 210 us
  blocking collectives  62.3 us (30%)
  waiting for transfers between devices  49.8 us (24%)
  between operations  42.6 us (20%)
  starting transfers between devices  24.5 us (12%)
  other arithmetic  16.9 us (8%)
  matrix products  8 us (4%)
  local copies, waits for them, and re-layouts  6.11 us (3%)
    all_gather x1, waiting for transfers between devices, on_device(): kv_all = lax.all_gather(kv_column, 'tx', axis=0, tiled=False)  29.2 us
    all_gather x1, blocking collectives, on_device(): kv_column = lax.all_gather(kv_local, 'tz', axis=0, tiled=False)  25.1 us
    all_gather x1, blocking collectives, on_device(): padded = lax.all_gather(stacked, 'tensor', axis=1, tiled=True)  20.6 us
    all_gather x1, waiting for transfers between devices, halo_rows(): column = lax.all_gather(rims, 'tz', axis=0, tiled=False)  19.5 us
    ppermute x4, starting transfers between devices, image_pair(): other = lax.ppermute(part, 'image', [(0, 1), (1, 0)])  14.4 us
    ppermute x3, starting transfers between devices, halo_rows(): lax.ppermute(chunk, 'tx', [(i, (i + shift) % n_x) for i in range(n_x)])  10 us
    all_gather x1, blocking collectives, on_device(): attended_full = lax.all_gather(attended, 'tensor', axis=1, tiled=True)  8.59 us
    all_gather x1, blocking collectives, on_device(): section_full = lax.all_gather(section, 'tensor', axis=1, tiled=True)  8.01 us
  transfers between devices with their start and end apart: 9, of which 3 were waited for; matrix products, arithmetic and copies ran while one was open for 10% of the time, Pallas kernels for 0%

profile of v2, /device:TPU:1, one launch (start us, length us, event | category | flops | bytes accessed | tf_op | source)
XLA Modules:
  0.0 210.2 jit_solution(16405605177108303801)
XLA Ops:
  6.6 1.1 fusion.35
  9.0 1.8 fusion.12
  10.8 5.7 %collective-permute-start.3 = (bf16[3,3,1,1,80,640]{5,4,3,2,1,0:T(8,128)(2,1)S(1)}, bf16[3,3,1,1,80,640]{5,4,3,2,1,0:T(8,128)(2,1)}, u32[]{:S(2)}, u32[]{:S(2)}) collective-permute-start(bf16[3,3,1,1,80,640]{5,4,3,2,1,0:T(8,128)(2,1)S(1)} %fusion.12), channel_id=1, source_target_pairs={{0,4},{4,0},{1,5},{5,1},{2,6},{6,2},{3,7},{7,3},{8,12},{12,8},{9,1... | collective-permute-start | bytes 2764808 | tf_op jit(solution)/shard_map/ppermute | solution.py:36
  16.5 1.0 fusion.48
  17.5 1.9 collective-permute-start.5
  19.4 1.3 fusion.31
  20.7 4.9 %collective-permute-start.6 = (bf16[320,2,128]{2,1,0:T(2,128)(2,1)S(1)}, bf16[320,2,128]{2,1,0:T(2,128)(2,1)S(1)}, u32[]{:S(2)}, u32[]{:S(2)}) collective-permute-start(bf16[320,2,128]{2,1,0:T(2,128)(2,1)S(1)} %fusion.31), channel_id=1, source_target_pairs={{0,4},{4,0},{1,5},{5,1},{2,6},{6,2},{3,7},{7,3},{8,12},{12,8},{9,1... | collective-permute-start | bytes 491528 | tf_op jit(solution)/shard_map/ppermute | solution.py:36
  25.6 1.9 collective-permute-start.4
  33.2 0.8 fusion.71
  57.1 1.4 broadcast_select_fusion.1
  58.5 19.5 %all-gather.6.cloned.1.call-done = bf16[32,160,128]{2,1,0:T(8,128)(2,1)} async-done(((bf16[2,160,128]{2,1,0:T(8,128)(2,1)}), bf16[32,160,128]{2,1,0:T(8,128)(2,1)}) %all-gather.6.cloned.1.call-update) | async-done | bytes 1310736 | tf_op jit(solution)/shard_map/all_gather | solution.py:48
  78.0 0.9 fusion.69
  78.9 3.1 %collective-permute-start = (bf16[2,160,128]{2,1,0:T(8,128)(2,1)S(1)}, bf16[2,160,128]{2,1,0:T(8,128)(2,1)S(1)}, u32[]{:S(2)}, u32[]{:S(2)}) collective-permute-start(bf16[2,160,128]{2,1,0:T(8,128)(2,1)S(1)} %pad_maximum_fusion.4), channel_id=1, source_target_pairs={{0,8},{8,16},{16,24},{24,0},{1,9},{9,17},{17,25},{25,1},{2,10},{10... | collective-permute-start | bytes 245768 | tf_op jit(solution)/shard_map/ppermute | solution.py:61
  82.1 4.2 %collective-permute-start.1 = (bf16[2,160,128]{2,1,0:T(8,128)(2,1)S(1)}, bf16[2,160,128]{2,1,0:T(8,128)(2,1)S(1)}, u32[]{:S(2)}, u32[]{:S(2)}) collective-permute-start(bf16[2,160,128]{2,1,0:T(8,128)(2,1)S(1)} %pad_maximum_fusion.5), channel_id=1, source_target_pairs={{0,16},{8,24},{16,0},{24,8},{1,17},{9,25},{17,1},{25,9},{2,18},{10... | collective-permute-start | bytes 245768 | tf_op jit(solution)/shard_map/ppermute | solution.py:61
  86.3 2.6 %collective-permute-start.2 = (bf16[2,160,128]{2,1,0:T(8,128)(2,1)S(1)}, bf16[2,160,128]{2,1,0:T(8,128)(2,1)S(1)}, u32[]{:S(2)}, u32[]{:S(2)}) collective-permute-start(bf16[2,160,128]{2,1,0:T(8,128)(2,1)S(1)} %pad_maximum_fusion.6), channel_id=1, source_target_pairs={{0,24},{8,0},{16,8},{24,16},{1,25},{9,1},{17,9},{25,17},{2,26},{10... | collective-permute-start | bytes 245768 | tf_op jit(solution)/shard_map/ppermute | solution.py:61
  89.0 1.5 pad_maximum_fusion
  90.5 1.1 collective-permute-done.2
  91.5 0.8 fusion.63
  92.4 20.6 %all_gather.29 = bf16[6,640,128]{2,1,0:T(8,128)(2,1)S(1)} all-gather(bf16[6,160,128]{2,1,0:T(8,128)(2,1)S(1)} %pad_maximum_fusion.2), channel_id=1, replica_groups=mesh['tz'=16,'tx'=4,'image'=2,'tensor'=4] {'tensor'}, dimensions={1}, use_global_device_ids=true | all-gather | bytes 1228800 | tf_op jit(solution)/shard_map/all_gather | solution.py:117
  114.4 3.4 %convolution_select_fusion = f32[4,8,17,160]{3,1,2,0:T(8,128)S(1)} fusion(bf16[3,3,160,640]{3,2,1,0:T(8,128)(2,1)} %bitcast.137, bf16[6,640,1,7,2]{1,3,4,0,2:T(8,128)(2,1)S(1)} %slice.114, bf16[6,640,1,8,17]{1,3,4,0,2:T(8,128)(2,1)S(1)} %copy.100, pred[8,17]{0,1:T(8,128)(4,1)S(1)} %copy-done.6), kind=kOutput, calls=%fused_computation.24 | convolution fusion | flops 1006289920 | bytes 3343496 | tf_op jit(solution)/shard_map/conv_general_dilated | solution.py:19
  118.5 8.0 %all_gather.30 = bf16[4,640,128]{2,0,1:T(4,128)(2,1)S(1)} all-gather(bf16[4,160,128]{2,0,1:T(4,128)(2,1)S(1)} %copy.103), channel_id=1, replica_groups=mesh['tz'=16,'tx'=4,'image'=2,'tensor'=4] {'tensor'}, dimensions={1}, use_global_device_ids=true | all-gather | bytes 819200 | tf_op jit(solution)/shard_map/all_gather | solution.py:120
  126.5 0.9 copy.104
  127.9 25.1 %all-gather.1 = bf16[512,256]{1,0:T(8,128)(2,1)} all-gather(bf16[32,256]{1,0:T(8,128)(2,1)S(1)} %convolution_convert_fusion), channel_id=3, replica_groups=mesh['tz'=16,'tx'=4,'image'=2,'tensor'=4] {'tz'}, dimensions={0}, use_global_device_ids=true | all-gather | bytes 278528 | tf_op jit(solution)/shard_map/all_gather | solution.py:139
  155.1 0.9 broadcast_select_fusion.7
  156.8 29.2 %all-gather.8.cloned.1.call-done = bf16[64,32,256]{2,1,0:T(8,128)(2,1)} async-done(((bf16[16,32,256]{2,1,0:T(8,128)(2,1)}), bf16[64,32,256]{2,1,0:T(8,128)(2,1)}) %all-gather.8.cloned.1.call-update) | async-done | bytes 1048592 | tf_op jit(solution)/shard_map/all_gather | solution.py:140
  186.0 1.3 fusion.90
  187.7 0.7 fusion.42
  188.4 1.1 select_reduce_fusion.1
  189.5 2.1 %fusion = (f32[512]{0:T(512)S(1)}, f32[512]{0:T(512)S(1)}) fusion(f32[512,2048]{1,0:T(8,128)S(1)} %get-tuple-element.44, f32[2048]{0:T(1024)S(1)} %get-tuple-element.17, f32[512]{0:T(512)S(1)} %get-tuple-element.7, pred[2048]{0:T(1024)(128)(4,1)S(1)} %get-tuple-element.18, f32[512]{0:T(512)S(1)} %get-tuple-element.8, f32[512,2048]{1,0:T(8,128)S(1)} %fusion.42), kind=kLoop, calls=%fused_computation.4 | loop fusion | flops 8387584 | bytes 8407040 | tf_op jit(solution)/shard_map/reduce_sum | solution.py:166
  191.7 1.0 fusion.23
  192.7 1.0 fusion.26
  193.8 8.6 %all_gather.35 = bf16[512,512]{0,1:T(8,128)(2,1)S(1)} all-gather(bf16[512,128]{0,1:T(8,128)(2,1)S(1)} %bitcast.144), channel_id=1, replica_groups=mesh['tz'=16,'tx'=4,'image'=2,'tensor'=4] {'tensor'}, dimensions={1}, use_global_device_ids=true | all-gather | bytes 655360 | tf_op jit(solution)/shard_map/all_gather | solution.py:177
  (67 shorter events, 8.3 us)
Async XLA Ops:
  6.5 19.0 %copy-start.1 = (bf16[160,256]{1,0:T(8,128)(2,1)S(1)}, bf16[160,256]{1,0:T(8,128)(2,1)}, u32[]{:S(2)}) copy-start(bf16[160,256]{1,0:T(8,128)(2,1)} %param.23) | copy-start | bytes 245764
  6.5 19.0 %copy-start.2 = (bf16[160,256]{1,0:T(8,128)(2,1)S(1)}, bf16[160,256]{1,0:T(8,128)(2,1)}, u32[]{:S(2)}) copy-start(bf16[160,256]{1,0:T(8,128)(2,1)} %param.24) | copy-start | bytes 245764
  6.5 21.1 %copy-start.3 = (s32[2,64]{1,0:T(2,128)S(1)}, s32[2,64]{1,0:T(2,128)}, u32[]{:S(2)}) copy-start(s32[2,64]{1,0:T(2,128)} %param.14) | copy-start | bytes 1540
  6.5 48.7 %copy-start.5 = (s32[2]{0:T(128)S(1)}, s32[2]{0:T(128)}, u32[]{:S(2)}) copy-start(s32[2]{0:T(128)} %param.15) | copy-start | bytes 28
  6.5 71.5 %all-gather.6.cloned.1.call-start = ((), (), s32[]{:S(2)}) async-start(), calls=%async_computation | async-start | bytes 1392640 | tf_op jit(solution)/shard_map/all_gather | solution.py:48
  8.3 177.7 %all-gather.8.cloned.1.call-start = ((), (), s32[]{:S(2)}) async-start(), calls=%async_computation.1 | async-start | bytes 1310720 | tf_op jit(solution)/shard_map/all_gather | solution.py:140
  10.8 46.2 %collective-permute-start.3 = (bf16[3,3,1,1,80,640]{5,4,3,2,1,0:T(8,128)(2,1)S(1)}, bf16[3,3,1,1,80,640]{5,4,3,2,1,0:T(8,128)(2,1)}, u32[]{:S(2)}, u32[]{:S(2)}) collective-permute-start(bf16[3,3,1,1,80,640]{5,4,3,2,1,0:T(8,128)(2,1)S(1)} %fusion.12), channel_id=1, source_target_pairs={{0,4},{4,0},{1,5},{5,1},{2,6},{6,2},{3,7},{7,3},{8,12},{12,8},{9,1... | collective-permute-start | bytes 2764808 | tf_op jit(solution)/shard_map/ppermute | solution.py:36
  17.5 137.6 %collective-permute-start.5 = (bf16[320,128]{1,0:T(8,128)(2,1)S(1)}, bf16[320,128]{1,0:T(8,128)(2,1)S(1)}, u32[]{:S(2)}, u32[]{:S(2)}) collective-permute-start(bf16[320,128]{1,0:T(8,128)(2,1)S(1)} %fusion.48), channel_id=1, source_target_pairs={{0,4},{4,0},{1,5},{5,1},{2,6},{6,2},{3,7},{7,3},{8,12},{12,8},{9,1... | collective-permute-start | bytes 245768 | tf_op jit(solution)/shard_map/ppermute | solution.py:36
  20.7 35.9 %collective-permute-start.6 = (bf16[320,2,128]{2,1,0:T(2,128)(2,1)S(1)}, bf16[320,2,128]{2,1,0:T(2,128)(2,1)S(1)}, u32[]{:S(2)}, u32[]{:S(2)}) collective-permute-start(bf16[320,2,128]{2,1,0:T(2,128)(2,1)S(1)} %fusion.31), channel_id=1, source_target_pairs={{0,4},{4,0},{1,5},{5,1},{2,6},{6,2},{3,7},{7,3},{8,12},{12,8},{9,1... | collective-permute-start | bytes 491528 | tf_op jit(solution)/shard_map/ppermute | solution.py:36
  25.6 129.5 %collective-permute-start.4 = (bf16[160,256]{1,0:T(8,128)(2,1)S(1)}, bf16[160,256]{1,0:T(8,128)(2,1)}, u32[]{:S(2)}, u32[]{:S(2)}) collective-permute-start(bf16[160,256]{1,0:T(8,128)(2,1)S(1)} %fusion.46), channel_id=1, source_target_pairs={{0,4},{4,0},{1,5},{5,1},{2,6},{6,2},{3,7},{7,3},{8,12},{12,8},{9,1... | collective-permute-start | bytes 245768 | tf_op jit(solution)/shard_map/ppermute | solution.py:36
  78.9 11.5 %collective-permute-start = (bf16[2,160,128]{2,1,0:T(8,128)(2,1)S(1)}, bf16[2,160,128]{2,1,0:T(8,128)(2,1)S(1)}, u32[]{:S(2)}, u32[]{:S(2)}) collective-permute-start(bf16[2,160,128]{2,1,0:T(8,128)(2,1)S(1)} %pad_maximum_fusion.4), channel_id=1, source_target_pairs={{0,8},{8,16},{16,24},{24,0},{1,9},{9,17},{17,25},{25,1},{2,10},{10... | collective-permute-start | bytes 245768 | tf_op jit(solution)/shard_map/ppermute | solution.py:61
  82.1 8.4 %collective-permute-start.1 = (bf16[2,160,128]{2,1,0:T(8,128)(2,1)S(1)}, bf16[2,160,128]{2,1,0:T(8,128)(2,1)S(1)}, u32[]{:S(2)}, u32[]{:S(2)}) collective-permute-start(bf16[2,160,128]{2,1,0:T(8,128)(2,1)S(1)} %pad_maximum_fusion.5), channel_id=1, source_target_pairs={{0,16},{8,24},{16,0},{24,8},{1,17},{9,25},{17,1},{25,9},{2,18},{10... | collective-permute-start | bytes 245768 | tf_op jit(solution)/shard_map/ppermute | solution.py:61
  86.3 5.2 %collective-permute-start.2 = (bf16[2,160,128]{2,1,0:T(8,128)(2,1)S(1)}, bf16[2,160,128]{2,1,0:T(8,128)(2,1)S(1)}, u32[]{:S(2)}, u32[]{:S(2)}) collective-permute-start(bf16[2,160,128]{2,1,0:T(8,128)(2,1)S(1)} %pad_maximum_fusion.6), channel_id=1, source_target_pairs={{0,24},{8,0},{16,8},{24,16},{1,25},{9,1},{17,9},{25,17},{2,26},{10... | collective-permute-start | bytes 245768 | tf_op jit(solution)/shard_map/ppermute | solution.py:61
  112.9 1.5 copy-start.6
  114.4 3.9 %copy-start = (bf16[1,4,160,128]{3,2,1,0:T(8,128)(2,1)S(1)}, bf16[1,4,160,128]{3,2,1,0:T(8,128)(2,1)}, u32[]{:S(2)}) copy-start(bf16[1,4,160,128]{3,2,1,0:T(8,128)(2,1)} %param.13) | copy-start | bytes 491524
  118.0 37.0 %copy-start.4 = (bf16[640]{0:T(1024)(128)(2,1)S(1)}, bf16[640]{0:T(1024)(128)(2,1)}, u32[]{:S(2)}) copy-start(bf16[640]{0:T(1024)(128)(2,1)} %param.25) | copy-start | bytes 3844
Sparse Core Ops, SparseCore 0:
  9.5 68.4 all-gather.5
  153.2 32.7 all-gather.7

commit v3 on v2

--- a/solution.py
+++ b/solution.py
@@ -7,7 +7,8 @@
 
 HD = 64
 POOL = 4
-TILE_AXES = ("tz", "tx")
+TILE_AXES = ("zh", "zl", "tx")
+PIECE_BYTES = 900 * 1024
 
 
 def blend(ema_part, adjusted_part, blend_ratio):
@@ -39,13 +40,33 @@
     return jnp.concatenate([first, second], axis=axis)
 
 
+def staged_gather(part, axes):
+    out = part
+    for axis in axes:
+        size = lax.axis_size(axis)
+        total = out.size * out.dtype.itemsize * size
+        pieces = 1
+        while total > PIECE_BYTES * pieces or out.shape[0] % pieces:
+            pieces += 1
+        if pieces == 1:
+            out = lax.all_gather(out, axis, axis=0, tiled=False)
+        else:
+            step = out.shape[0] // pieces
+            parts = [
+                lax.all_gather(out[i * step:(i + 1) * step], axis, axis=1, tiled=False)
+                for i in range(pieces)
+            ]
+            out = jnp.swapaxes(jnp.concatenate(parts, axis=0), 0, 1)
+    return out
+
+
 def owner_of(slot, slot_row):
     tiles = jnp.arange(slot_row.shape[0], dtype=jnp.int32)
     return jnp.sum(jnp.where(slot_row == slot, tiles, 0))
 
 
 def halo_rows(rims, slot_row, my_slot, tz_i, tx_i, n_x):
-    column = lax.all_gather(rims, "tz", axis=0, tiled=False)
+    column = staged_gather(rims, ("zl", "zh")).reshape((-1,) + rims.shape)
     received = [None]
     for shift in range(1, n_x):
         dest_tile = tz_i * n_x + (tx_i + shift) % n_x
@@ -87,7 +108,8 @@
     norm_gain,
 ):
     image_index = lax.axis_index("image")
-    tile_index = lax.axis_index("tz") * lax.axis_size("tx") + lax.axis_index("tx")
+    z_index = lax.axis_index("zh") * lax.axis_size("zl") + lax.axis_index("zl")
+    tile_index = z_index * lax.axis_size("tx") + lax.axis_index("tx")
     slot_row = lax.dynamic_index_in_dim(tile_slot, image_index, 0, keepdims=False)
     live_count = lax.dynamic_index_in_dim(tile_count, image_index, 0, keepdims=False)
     my_slot = lax.dynamic_index_in_dim(slot_row, tile_index, 0, keepdims=False)
@@ -100,7 +122,7 @@
     rim_rows = jnp.stack([activated[0], activated[-1]])
     n_x = lax.axis_size("tx")
     upper, lower = halo_rows(
-        rim_rows, slot_row, my_slot, lax.axis_index("tz"), lax.axis_index("tx"), n_x
+        rim_rows, slot_row, my_slot, z_index, lax.axis_index("tx"), n_x
     )
 
     conv_w = image_pair(blend(conv_ema, conv_adjusted, blend_ratio), image_index, 3)
@@ -136,9 +158,8 @@
     pooled = jnp.transpose(pooled, (0, 2, 1)).astype(jnp.bfloat16).reshape(tok_count, channels)
     kv_flat = kv_w.reshape(channels, 2 * att_shard)
     kv_local = jnp.dot(pooled, kv_flat, preferred_element_type=jnp.float32).astype(jnp.bfloat16)
-    kv_column = lax.all_gather(kv_local, "tz", axis=0, tiled=False)
-    kv_all = lax.all_gather(kv_column, "tx", axis=0, tiled=False)
-    n_z = kv_all.shape[1]
+    kv_all = staged_gather(kv_local, ("zl", "zh", "tx"))
+    n_z = kv_all.shape[1] * kv_all.shape[2]
     kv_rows = kv_all.reshape(-1, 2 * att_shard)
     key_rows = kv_rows[:, :att_shard]
     key_total = key_rows.shape[0]
@@ -186,10 +207,11 @@
 def solution(mesh):
     tiles = mesh.shape["tile"]
     inner = 4 if tiles % 4 == 0 else 1
+    low = 4 if (tiles // inner) % 4 == 0 else 1
     devices = np.asarray(mesh.devices).reshape(
-        (tiles // inner, inner, mesh.shape["image"], mesh.shape["tensor"])
-    )
-    split = Mesh(devices, ("tz", "tx", "image", "tensor"))
+        (tiles // inner // low, low, inner, mesh.shape["image"], mesh.shape["tensor"])
+    )
+    split = Mesh(devices, ("zh", "zl", "tx", "image", "tensor"))
     placed = (
         P("image", TILE_AXES, "tensor", None),
         P(),

time: 211 us -> 251 us (1.19)
  blocking collectives: 62.3 us -> 162 us
  waiting for transfers between devices: 49.8 us -> 0.02 us
  between operations: 42.6 us -> 29 us
  other arithmetic: 16.9 us -> 21.4 us
    all_gather x1 -> x7, blocking collectives: 25.1 us -> 116 us  [the longest x4 74.5 us: staged_gather(): lax.all_gather(out[i * step:(i + 1) * step], axis, axis=1, tiled=False)]
    all_gather x2 -> x0, waiting for transfers between devices: 48.7 us -> none  [the longest x1 29.2 us: on_device(): kv_all = lax.all_gather(kv_column, 'tx', axis=0, tiled=False)]
    all_gather x1, blocking collectives: 8.59 us -> 18.1 us  [on_device(): attended_full = lax.all_gather(attended, 'tensor', axis=1, tiled=True)]
    select_n x4, other arithmetic: 2.31 us -> 5.49 us  [image_pair(): first = jnp.where(image_index == 0, part, other)]
  transfers between devices with their start and end apart: 9 -> 7, of which waited for: 3 -> 0; matrix products, arithmetic and copies ran while one was open for 10% -> 6% of each run, Pallas kernels for 0% -> 0%
where the time goes in v3:
time: 251 us; the launch traced here: 250 us
  blocking collectives  162 us (65%)
  between operations  29 us (12%)
  starting transfers between devices  24.1 us (10%)
  other arithmetic  21.4 us (9%)
  local copies, waits for them, and re-layouts  6.97 us (3%)
  matrix products  6.47 us (3%)
    all_gather x4, blocking collectives, staged_gather(): lax.all_gather(out[i * step:(i + 1) * step], axis, axis=1, tiled=False)  74.5 us
    all_gather x3, blocking collectives, staged_gather(): out = lax.all_gather(out, axis, axis=0, tiled=False)  41.9 us
    all_gather x1, blocking collectives, on_device(): padded = lax.all_gather(stacked, 'tensor', axis=1, tiled=True)  19.7 us
    all_gather x1, blocking collectives, on_device(): attended_full = lax.all_gather(attended, 'tensor', axis=1, tiled=True)  18.1 us
    ppermute x4, starting transfers between devices, image_pair(): other = lax.ppermute(part, 'image', [(0, 1), (1, 0)])  13.6 us
    ppermute x3, starting transfers between devices, halo_rows(): lax.ppermute(chunk, 'tx', [(i, (i + shift) % n_x) for i in range(n_x)])  10.5 us
    all_gather x1, blocking collectives, on_device(): section_full = lax.all_gather(section, 'tensor', axis=1, tiled=True)  8.01 us
    select_n x4, other arithmetic, image_pair(): first = jnp.where(image_index == 0, part, other)  5.49 us
  transfers between devices with their start and end apart: 7, of which 0 were waited for; matrix products, arithmetic and copies ran while one was open for 6% of the time, Pallas kernels for 0%

profile of v3, /device:TPU:1, one launch (start us, length us, event | category | flops | bytes accessed | tf_op | source)
XLA Modules:
  0.0 250.1 jit_solution(5000392623708061141)
XLA Ops:
  0.0 1.5 fusion.94
  6.3 1.5 fusion.71
  22.9 1.0 fusion.35
  24.0 14.0 %all-gather = bf16[8,160,128]{2,1,0:T(8,128)(2,1)S(1)} all-gather(bf16[2,160,128]{2,1,0:T(8,128)(2,1)S(1)} %pad_maximum_fusion.3), channel_id=2, replica_groups=mesh['zh'=4,'zl'=4,'tx'=4,'image'=2,'tensor'=4] {'zl'}, dimensions={0}, use_global_device_ids=true | all-gather | bytes 409600 | tf_op jit(solution)/shard_map/all_gather | solution.py:52
  37.9 32.4 %all-gather.1 = bf16[2,8,160,128]{3,2,1,0:T(8,128)(2,1)S(1)} all-gather(bf16[2,2,160,128]{3,2,1,0:T(8,128)(2,1)S(1)} %bitcast.161), channel_id=3, replica_groups=mesh['zh'=4,'zl'=4,'tx'=4,'image'=2,'tensor'=4] {'zh'}, dimensions={1}, use_global_device_ids=true | all-gather | bytes 819200 | tf_op jit(solution)/shard_map/all_gather | solution.py:56
  70.4 21.8 %all-gather.2 = bf16[2,8,160,128]{3,2,1,0:T(8,128)(2,1)S(1)} all-gather(bf16[2,2,160,128]{3,2,1,0:T(8,128)(2,1)S(1)} %bitcast.158), channel_id=4, replica_groups=mesh['zh'=4,'zl'=4,'tx'=4,'image'=2,'tensor'=4] {'zh'}, dimensions={1}, use_global_device_ids=true | all-gather | bytes 819200 | tf_op jit(solution)/shard_map/all_gather | solution.py:56
  93.2 3.1 %collective-permute-start = (bf16[2,160,128]{2,1,0:T(8,128)(2,1)}, bf16[2,160,128]{2,1,0:T(8,128)(2,1)S(1)}, u32[]{:S(2)}, u32[]{:S(2)}) collective-permute-start(bf16[2,160,128]{2,1,0:T(8,128)(2,1)} %pad_maximum_fusion.4), channel_id=1, source_target_pairs={{0,8},{8,16},{16,24},{24,0},{1,9},{9,17},{17,25},{25,1},{2,10},{10... | collective-permute-start | bytes 245768 | tf_op jit(solution)/shard_map/ppermute | solution.py:82
  96.9 4.3 %collective-permute-start.1 = (bf16[2,160,128]{2,1,0:T(8,128)(2,1)}, bf16[2,160,128]{2,1,0:T(8,128)(2,1)}, u32[]{:S(2)}, u32[]{:S(2)}) collective-permute-start(bf16[2,160,128]{2,1,0:T(8,128)(2,1)} %pad_maximum_fusion.5), channel_id=1, source_target_pairs={{0,16},{8,24},{16,0},{24,8},{1,17},{9,25},{17,1},{25,9},{2,18},{10... | collective-permute-start | bytes 245768 | tf_op jit(solution)/shard_map/ppermute | solution.py:82
  101.9 3.1 %collective-permute-start.2 = (bf16[2,160,128]{2,1,0:T(8,128)(2,1)}, bf16[2,160,128]{2,1,0:T(8,128)(2,1)}, u32[]{:S(2)}, u32[]{:S(2)}) collective-permute-start(bf16[2,160,128]{2,1,0:T(8,128)(2,1)} %pad_maximum_fusion.6), channel_id=1, source_target_pairs={{0,24},{8,0},{16,8},{24,16},{1,25},{9,1},{17,9},{25,17},{2,26},{10... | collective-permute-start | bytes 245768 | tf_op jit(solution)/shard_map/ppermute | solution.py:82
  105.6 1.5 fusion.12
  107.2 4.8 %collective-permute-start.3 = (bf16[3,3,1,1,80,640]{5,4,3,2,1,0:T(8,128)(2,1)S(1)}, bf16[3,3,1,1,80,640]{5,4,3,2,1,0:T(8,128)(2,1)}, u32[]{:S(2)}, u32[]{:S(2)}) collective-permute-start(bf16[3,3,1,1,80,640]{5,4,3,2,1,0:T(8,128)(2,1)S(1)} %fusion.12), channel_id=1, source_target_pairs={{0,4},{4,0},{1,5},{5,1},{2,6},{6,2},{3,7},{7,3},{8,12},{12,8},{9,1... | collective-permute-start | bytes 2764808 | tf_op jit(solution)/shard_map/ppermute | solution.py:37
  112.9 2.0 collective-permute-start.5
  115.7 1.9 fusion.31
  117.8 1.0 fusion.46
  127.2 4.8 %collective-permute-start.6 = (bf16[320,2,128]{2,1,0:T(2,128)(2,1)}, bf16[320,2,128]{2,1,0:T(2,128)(2,1)}, u32[]{:S(2)}, u32[]{:S(2)}) collective-permute-start(bf16[320,2,128]{2,1,0:T(2,128)(2,1)} %fusion.31), channel_id=1, source_target_pairs={{0,4},{4,0},{1,5},{5,1},{2,6},{6,2},{3,7},{7,3},{8,12},{12,8},{9,1... | collective-permute-start | bytes 491528 | tf_op jit(solution)/shard_map/ppermute | solution.py:37
  132.1 2.0 collective-permute-start.4
  135.0 19.7 %all_gather.57 = bf16[6,640,128]{2,1,0:T(8,128)(2,1)S(1)} all-gather(bf16[6,160,128]{2,1,0:T(8,128)(2,1)S(1)} %pad_maximum_fusion.2), channel_id=1, replica_groups=mesh['zh'=4,'zl'=4,'tx'=4,'image'=2,'tensor'=4] {'tensor'}, dimensions={1}, use_global_device_ids=true | all-gather | bytes 1228800 | tf_op jit(solution)/shard_map/all_gather | solution.py:139
  154.6 1.6 broadcast_select_fusion.5
  157.7 1.5 broadcast_select_fusion.7
  159.2 1.0 broadcast_select_fusion.3
  160.7 1.4 broadcast_select_fusion.1
  162.7 1.8 convolution_select_fusion
  165.6 8.0 %all_gather.58 = bf16[4,640,128]{2,0,1:T(4,128)(2,1)S(1)} all-gather(bf16[4,160,128]{2,0,1:T(4,128)(2,1)S(1)} %copy.117), channel_id=1, replica_groups=mesh['zh'=4,'zl'=4,'tx'=4,'image'=2,'tensor'=4] {'tensor'}, dimensions={1}, use_global_device_ids=true | all-gather | bytes 819200 | tf_op jit(solution)/shard_map/all_gather | solution.py:142
  175.3 11.5 %all-gather.3 = bf16[128,256]{1,0:T(8,128)(2,1)S(1)} all-gather(bf16[32,256]{1,0:T(8,128)(2,1)S(1)} %convolution_convert_fusion), channel_id=5, replica_groups=mesh['zh'=4,'zl'=4,'tx'=4,'image'=2,'tensor'=4] {'zl'}, dimensions={0}, use_global_device_ids=true | all-gather | bytes 81920 | tf_op jit(solution)/shard_map/all_gather | solution.py:52
  186.8 16.4 %all-gather.4 = bf16[16,32,256]{2,1,0:T(8,128)(2,1)S(1)} all-gather(bf16[4,32,256]{2,1,0:T(8,128)(2,1)S(1)} %bitcast.167), channel_id=6, replica_groups=mesh['zh'=4,'zl'=4,'tx'=4,'image'=2,'tensor'=4] {'zh'}, dimensions={0}, use_global_device_ids=true | all-gather | bytes 327680 | tf_op jit(solution)/shard_map/all_gather | solution.py:52
  203.2 10.2 %all-gather.5 = bf16[2,16,32,256]{3,2,1,0:T(8,128)(2,1)S(1)} all-gather(bf16[2,4,32,256]{3,2,1,0:T(8,128)(2,1)S(1)} %bitcast.166), channel_id=7, replica_groups=mesh['zh'=4,'zl'=4,'tx'=4,'image'=2,'tensor'=4] {'tx'}, dimensions={1}, use_global_device_ids=true | all-gather | bytes 655360 | tf_op jit(solution)/shard_map/all_gather | solution.py:56
  213.4 10.1 %all-gather.6 = bf16[2,16,32,256]{3,2,1,0:T(8,128)(2,1)S(1)} all-gather(bf16[2,4,32,256]{3,2,1,0:T(8,128)(2,1)S(1)} %bitcast.165), channel_id=8, replica_groups=mesh['zh'=4,'zl'=4,'tx'=4,'image'=2,'tensor'=4] {'tx'}, dimensions={1}, use_global_device_ids=true | all-gather | bytes 655360 | tf_op jit(solution)/shard_map/all_gather | solution.py:56
  225.7 1.1 select_reduce_fusion.1
  226.8 2.1 fusion
  228.9 1.0 fusion.23
  230.0 1.0 fusion.26
  231.1 18.1 %all_gather.67 = bf16[512,512]{0,1:T(8,128)(2,1)S(1)} all-gather(bf16[512,128]{0,1:T(8,128)(2,1)S(1)} %bitcast.162), channel_id=1, replica_groups=mesh['zh'=4,'zl'=4,'tx'=4,'image'=2,'tensor'=4] {'tensor'}, dimensions={1}, use_global_device_ids=true | all-gather | bytes 655360 | tf_op jit(solution)/shard_map/all_gather | solution.py:198
  (77 shorter events, 13.9 us)
Async XLA Ops:
  92.3 13.3 %copy-start = (bf16[3,3,1,1,80,640]{5,4,3,2,1,0:T(8,128)(2,1)S(1)}, bf16[3,3,1,1,80,640]{5,4,3,2,1,0:T(8,128)(2,1)}, u32[]{:S(2)}) copy-start(bf16[3,3,1,1,80,640]{5,4,3,2,1,0:T(8,128)(2,1)} %param.17) | copy-start | bytes 2764804
  92.4 19.6 %copy-start.5 = (bf16[320,128]{1,0:T(8,128)(2,1)S(1)}, bf16[320,128]{1,0:T(8,128)(2,1)}, u32[]{:S(2)}) copy-start(bf16[320,128]{1,0:T(8,128)(2,1)} %param.19) | copy-start | bytes 245764
  92.4 22.5 %copy-start.7 = (s32[2]{0:T(128)S(1)}, s32[2]{0:T(128)}, u32[]{:S(2)}) copy-start(s32[2]{0:T(128)} %param.15) | copy-start | bytes 28
  92.5 34.6 %copy-start.6 = (bf16[640]{0:T(1024)(128)(2,1)S(1)}, bf16[640]{0:T(1024)(128)(2,1)}, u32[]{:S(2)}) copy-start(bf16[640]{0:T(1024)(128)(2,1)} %param.25) | copy-start | bytes 3844
  93.2 34.0 %collective-permute-start = (bf16[2,160,128]{2,1,0:T(8,128)(2,1)}, bf16[2,160,128]{2,1,0:T(8,128)(2,1)S(1)}, u32[]{:S(2)}, u32[]{:S(2)}) collective-permute-start(bf16[2,160,128]{2,1,0:T(8,128)(2,1)} %pad_maximum_fusion.4), channel_id=1, source_target_pairs={{0,8},{8,16},{16,24},{24,0},{1,9},{9,17},{17,25},{25,1},{2,10},{10... | collective-permute-start | bytes 245768 | tf_op jit(solution)/shard_map/ppermute | solution.py:82
  96.9 35.1 %collective-permute-start.1 = (bf16[2,160,128]{2,1,0:T(8,128)(2,1)}, bf16[2,160,128]{2,1,0:T(8,128)(2,1)}, u32[]{:S(2)}, u32[]{:S(2)}) collective-permute-start(bf16[2,160,128]{2,1,0:T(8,128)(2,1)} %pad_maximum_fusion.5), channel_id=1, source_target_pairs={{0,16},{8,24},{16,0},{24,8},{1,17},{9,25},{17,1},{25,9},{2,18},{10... | collective-permute-start | bytes 245768 | tf_op jit(solution)/shard_map/ppermute | solution.py:82
  101.9 32.1 %collective-permute-start.2 = (bf16[2,160,128]{2,1,0:T(8,128)(2,1)}, bf16[2,160,128]{2,1,0:T(8,128)(2,1)}, u32[]{:S(2)}, u32[]{:S(2)}) collective-permute-start(bf16[2,160,128]{2,1,0:T(8,128)(2,1)} %pad_maximum_fusion.6), channel_id=1, source_target_pairs={{0,24},{8,0},{16,8},{24,16},{1,25},{9,1},{17,9},{25,17},{2,26},{10... | collective-permute-start | bytes 245768 | tf_op jit(solution)/shard_map/ppermute | solution.py:82
  107.2 53.5 %collective-permute-start.3 = (bf16[3,3,1,1,80,640]{5,4,3,2,1,0:T(8,128)(2,1)S(1)}, bf16[3,3,1,1,80,640]{5,4,3,2,1,0:T(8,128)(2,1)}, u32[]{:S(2)}, u32[]{:S(2)}) collective-permute-start(bf16[3,3,1,1,80,640]{5,4,3,2,1,0:T(8,128)(2,1)S(1)} %fusion.12), channel_id=1, source_target_pairs={{0,4},{4,0},{1,5},{5,1},{2,6},{6,2},{3,7},{7,3},{8,12},{12,8},{9,1... | collective-permute-start | bytes 2764808 | tf_op jit(solution)/shard_map/ppermute | solution.py:37
  112.9 41.7 %collective-permute-start.5 = (bf16[320,128]{1,0:T(8,128)(2,1)S(1)}, bf16[320,128]{1,0:T(8,128)(2,1)}, u32[]{:S(2)}, u32[]{:S(2)}) collective-permute-start(bf16[320,128]{1,0:T(8,128)(2,1)S(1)} %fusion.48), channel_id=1, source_target_pairs={{0,4},{4,0},{1,5},{5,1},{2,6},{6,2},{3,7},{7,3},{8,12},{12,8},{9,1... | collective-permute-start | bytes 245768 | tf_op jit(solution)/shard_map/ppermute | solution.py:37
  127.2 32.0 %collective-permute-start.6 = (bf16[320,2,128]{2,1,0:T(2,128)(2,1)}, bf16[320,2,128]{2,1,0:T(2,128)(2,1)}, u32[]{:S(2)}, u32[]{:S(2)}) collective-permute-start(bf16[320,2,128]{2,1,0:T(2,128)(2,1)} %fusion.31), channel_id=1, source_target_pairs={{0,4},{4,0},{1,5},{5,1},{2,6},{6,2},{3,7},{7,3},{8,12},{12,8},{9,1... | collective-permute-start | bytes 491528 | tf_op jit(solution)/shard_map/ppermute | solution.py:37
  132.1 25.6 %collective-permute-start.4 = (bf16[160,256]{1,0:T(8,128)(2,1)S(1)}, bf16[160,256]{1,0:T(8,128)(2,1)}, u32[]{:S(2)}, u32[]{:S(2)}) collective-permute-start(bf16[160,256]{1,0:T(8,128)(2,1)S(1)} %fusion.46), channel_id=1, source_target_pairs={{0,4},{4,0},{1,5},{5,1},{2,6},{6,2},{3,7},{7,3},{8,12},{12,8},{9,1... | collective-permute-start | bytes 245768 | tf_op jit(solution)/shard_map/ppermute | solution.py:37
  162.0 0.7 copy-start.8
  164.6 0.9 copy-start.1
  223.7 0.9 copy-start.3
  223.7 0.9 copy-start.4
  230.0 19.2 %copy-start.2 = (bf16[160,256]{1,0:T(8,128)(2,1)S(1)}, bf16[160,256]{1,0:T(8,128)(2,1)}, u32[]{:S(2)}) copy-start(bf16[160,256]{1,0:T(8,128)(2,1)} %get-tuple-element.39) | copy-start | bytes 245764

commit v4 on v2

--- a/solution.py
+++ b/solution.py
@@ -113,8 +113,9 @@
     has_lower = my_slot + 1 < live_count
     upper = jnp.where(has_upper, upper, jnp.zeros_like(upper))
     lower = jnp.where(has_lower, lower, jnp.zeros_like(lower))
-    stacked = jnp.concatenate([upper[None], activated, lower[None]], axis=0)
-    padded = lax.all_gather(stacked, "tensor", axis=1, tiled=True)
+    block_full = lax.all_gather(activated, "tensor", axis=1, tiled=True)
+    halo_full = lax.all_gather(jnp.stack([upper, lower]), "tensor", axis=1, tiled=True)
+    padded = jnp.concatenate([halo_full[0:1], block_full, halo_full[1:2]], axis=0)
     conv_out = convolve(padded, conv_w, (0, 0))
     section = (feats.astype(jnp.float32) + conv_out).astype(jnp.bfloat16)
     section_full = lax.all_gather(section, "tensor", axis=1, tiled=True)
@@ -129,11 +130,12 @@
     )
     att_shard = queries.shape[1]
     head_count = att_shard // HD
-    pooled = section_f.reshape(tile_rows // POOL, POOL, channels, tile_cols // POOL, POOL).mean(
-        axis=(1, 4)
-    )
+    pooled = section.astype(jnp.float32).reshape(
+        tile_rows // POOL, POOL, chan_shard, tile_cols // POOL, POOL
+    ).mean(axis=(1, 4))
     tok_count = pooled.shape[0] * pooled.shape[2]
-    pooled = jnp.transpose(pooled, (0, 2, 1)).astype(jnp.bfloat16).reshape(tok_count, channels)
+    pooled = jnp.transpose(pooled, (0, 2, 1)).astype(jnp.bfloat16).reshape(tok_count, chan_shard)
+    pooled = lax.all_gather(pooled, "tensor", axis=1, tiled=True)
     kv_flat = kv_w.reshape(channels, 2 * att_shard)
     kv_local = jnp.dot(pooled, kv_flat, preferred_element_type=jnp.float32).astype(jnp.bfloat16)
     kv_column = lax.all_gather(kv_local, "tz", axis=0, tiled=False)

time: 211 us -> 207 us (0.981)
  waiting for transfers between devices: 49.8 us -> 17.6 us
  blocking collectives: 62.3 us -> 87.7 us
  local copies, waits for them, and re-layouts: 6.11 us -> 9.43 us
    all_gather x1 -> x3, blocking collectives: 20.6 us -> 38.8 us  [the longest x1 16.9 us: on_device(): lax.all_gather(jnp.stack([upper, lower]), 'tensor', axis=1, tiled=True)]
    all_gather x1, waiting for transfers between devices: 19.5 us -> 1.79 us  [halo_rows(): column = lax.all_gather(rims, 'tz', axis=0, tiled=False)]
    all_gather x1, waiting for transfers between devices: 29.2 us -> 15 us  [on_device(): kv_all = lax.all_gather(kv_column, 'tx', axis=0, tiled=False)]
    all_gather x1, blocking collectives: 8.01 us -> 15.2 us  [on_device(): section_full = lax.all_gather(section, 'tensor', axis=1, tiled=True)]
    unnamed x16 -> x32, local copies, waits for them, and re-layouts: 0.85 us -> 3.18 us
  transfers between devices with their start and end apart: 9 -> 9, of which waited for: 3 -> 3; matrix products, arithmetic and copies ran while one was open for 10% -> 11% of each run, Pallas kernels for 0% -> 0%
where the time goes in v4:
time: 207 us; the launch traced here: 206 us
  blocking collectives  87.7 us (42%)
  between operations  42.2 us (20%)
  starting transfers between devices  24.7 us (12%)
  other arithmetic  18.2 us (9%)
  waiting for transfers between devices  17.6 us (9%)
  local copies, waits for them, and re-layouts  9.43 us (5%)
  matrix products  6.46 us (3%)
    all_gather x1, blocking collectives, on_device(): kv_column = lax.all_gather(kv_local, 'tz', axis=0, tiled=False)  25.1 us
    all_gather x1, blocking collectives, on_device(): lax.all_gather(jnp.stack([upper, lower]), 'tensor', axis=1, tiled=True)  16.9 us
    all_gather x1, blocking collectives, on_device(): block_full = lax.all_gather(activated, 'tensor', axis=1, tiled=True)  15.7 us
    all_gather x1, blocking collectives, on_device(): section_full = lax.all_gather(section, 'tensor', axis=1, tiled=True)  15.2 us
    all_gather x1, waiting for transfers between devices, on_device(): kv_all = lax.all_gather(kv_column, 'tx', axis=0, tiled=False)  15 us
    ppermute x4, starting transfers between devices, image_pair(): other = lax.ppermute(part, 'image', [(0, 1), (1, 0)])  14.3 us
    ppermute x3, starting transfers between devices, halo_rows(): lax.ppermute(chunk, 'tx', [(i, (i + shift) % n_x) for i in range(n_x)])  10.2 us
    all_gather x1, blocking collectives, on_device(): attended_full = lax.all_gather(attended, 'tensor', axis=1, tiled=True)  8.59 us
  transfers between devices with their start and end apart: 9, of which 3 were waited for; matrix products, arithmetic and copies ran while one was open for 11% of the time, Pallas kernels for 0%

profile of v4, /device:TPU:1, one launch (start us, length us, event | category | flops | bytes accessed | tf_op | source)
XLA Modules:
  0.0 206.3 jit_solution(7347867011601662339)
XLA Ops:
  6.6 1.1 fusion.38
  9.2 1.8 fusion.12
  11.0 5.7 %collective-permute-start.3 = (bf16[3,3,1,1,80,640]{5,4,3,2,1,0:T(8,128)(2,1)S(1)}, bf16[3,3,1,1,80,640]{5,4,3,2,1,0:T(8,128)(2,1)}, u32[]{:S(2)}, u32[]{:S(2)}) collective-permute-start(bf16[3,3,1,1,80,640]{5,4,3,2,1,0:T(8,128)(2,1)S(1)} %fusion.12), channel_id=1, source_target_pairs={{0,4},{4,0},{1,5},{5,1},{2,6},{6,2},{3,7},{7,3},{8,12},{12,8},{9,1... | collective-permute-start | bytes 2764808 | tf_op jit(solution)/shard_map/ppermute | solution.py:36
  16.7 1.9 collective-permute-start.5
  18.9 4.9 %collective-permute-start.6 = (bf16[320,2,128]{2,1,0:T(2,128)(2,1)S(1)}, bf16[320,2,128]{2,1,0:T(2,128)(2,1)S(1)}, u32[]{:S(2)}, u32[]{:S(2)}) collective-permute-start(bf16[320,2,128]{2,1,0:T(2,128)(2,1)S(1)} %fusion.34), channel_id=1, source_target_pairs={{0,4},{4,0},{1,5},{5,1},{2,6},{6,2},{3,7},{7,3},{8,12},{12,8},{9,1... | collective-permute-start | bytes 491528 | tf_op jit(solution)/shard_map/ppermute | solution.py:36
  24.5 1.9 collective-permute-start.4
  34.0 15.7 %all_gather.36 = bf16[4,640,128]{2,0,1:T(4,128)(2,1)S(1)} all-gather(bf16[4,160,128]{2,0,1:T(4,128)(2,1)S(1)} %copy.165), channel_id=1, replica_groups=mesh['tz'=16,'tx'=4,'image'=2,'tensor'=4] {'tensor'}, dimensions={1}, use_global_device_ids=true | all-gather | bytes 819200 | tf_op jit(solution)/shard_map/all_gather | solution.py:116
  73.7 1.1 pad_maximum_fusion.1
  74.9 1.4 broadcast_select_fusion.1
  76.2 1.8 all-gather.7.cloned.1.call-done
  78.0 0.9 fusion.71
  78.9 3.0 %collective-permute-start = (bf16[2,160,128]{2,1,0:T(8,128)(2,1)S(1)}, bf16[2,160,128]{2,1,0:T(8,128)(2,1)S(1)}, u32[]{:S(2)}, u32[]{:S(2)}) collective-permute-start(bf16[2,160,128]{2,1,0:T(8,128)(2,1)S(1)} %pad_maximum_fusion.3), channel_id=1, source_target_pairs={{0,8},{8,16},{16,24},{24,0},{1,9},{9,17},{17,25},{25,1},{2,10},{10... | collective-permute-start | bytes 245768 | tf_op jit(solution)/shard_map/ppermute | solution.py:61
  82.0 4.3 %collective-permute-start.1 = (bf16[2,160,128]{2,1,0:T(8,128)(2,1)S(1)}, bf16[2,160,128]{2,1,0:T(8,128)(2,1)S(1)}, u32[]{:S(2)}, u32[]{:S(2)}) collective-permute-start(bf16[2,160,128]{2,1,0:T(8,128)(2,1)S(1)} %pad_maximum_fusion.4), channel_id=1, source_target_pairs={{0,16},{8,24},{16,0},{24,8},{1,17},{9,25},{17,1},{25,9},{2,18},{10... | collective-permute-start | bytes 245768 | tf_op jit(solution)/shard_map/ppermute | solution.py:61
  86.3 2.9 %collective-permute-start.2 = (bf16[2,160,128]{2,1,0:T(8,128)(2,1)S(1)}, bf16[2,160,128]{2,1,0:T(8,128)(2,1)S(1)}, u32[]{:S(2)}, u32[]{:S(2)}) collective-permute-start(bf16[2,160,128]{2,1,0:T(8,128)(2,1)S(1)} %pad_maximum_fusion.5), channel_id=1, source_target_pairs={{0,24},{8,0},{16,8},{24,16},{1,25},{9,1},{17,9},{25,17},{2,26},{10... | collective-permute-start | bytes 245768 | tf_op jit(solution)/shard_map/ppermute | solution.py:61
  89.2 1.5 pad_maximum_fusion
  92.4 16.9 %all_gather.35 = bf16[2,640,128]{2,1,0:T(8,128)(2,1)S(1)} all-gather(bf16[2,160,128]{2,1,0:T(8,128)(2,1)S(1)} %pad_maximum_fusion.6), channel_id=1, replica_groups=mesh['tz'=16,'tx'=4,'image'=2,'tensor'=4] {'tensor'}, dimensions={1}, use_global_device_ids=true | all-gather | bytes 409600 | tf_op jit(solution)/shard_map/all_gather | solution.py:117
  109.9 1.1 maximum_bitcast_fusion
  111.0 1.2 copy.185
  113.1 1.2 copy-done
  114.4 1.8 convolution_select_fusion
  117.5 6.2 %all-gather.1 = bf16[1,32,640]{1,0,2:T(2,128)(2,1)S(1)} all-gather(bf16[1,32,160]{1,0,2:T(2,128)(2,1)S(1)} %copy.178), channel_id=3, replica_groups=mesh['tz'=16,'tx'=4,'image'=2,'tensor'=4] {'tensor'}, dimensions={2}, use_global_device_ids=true | all-gather | bytes 51200 | tf_op jit(solution)/shard_map/all_gather | solution.py:138
  124.1 25.1 %all-gather.2 = bf16[512,256]{1,0:T(8,128)(2,1)} all-gather(bf16[32,256]{1,0:T(8,128)(2,1)S(1)} %convolution_convert_fusion), channel_id=4, replica_groups=mesh['tz'=16,'tx'=4,'image'=2,'tensor'=4] {'tz'}, dimensions={0}, use_global_device_ids=true | all-gather | bytes 278528 | tf_op jit(solution)/shard_map/all_gather | solution.py:141
  149.2 0.9 broadcast_select_fusion.7
  150.3 15.2 %all_gather.37 = bf16[4,640,128]{2,0,1:T(4,128)(2,1)S(1)} all-gather(bf16[4,160,128]{2,0,1:T(4,128)(2,1)S(1)} %copy.173), channel_id=1, replica_groups=mesh['tz'=16,'tx'=4,'image'=2,'tensor'=4] {'tensor'}, dimensions={1}, use_global_device_ids=true | all-gather | bytes 819200 | tf_op jit(solution)/shard_map/all_gather | solution.py:121
  165.4 0.9 copy.174
  167.1 15.0 %all-gather.9.cloned.1.call-done = bf16[64,32,256]{2,1,0:T(8,128)(2,1)} async-done(((bf16[16,32,256]{2,1,0:T(8,128)(2,1)}), bf16[64,32,256]{2,1,0:T(8,128)(2,1)}) %all-gather.9.cloned.1.call-update) | async-done | bytes 1048592 | tf_op jit(solution)/shard_map/all_gather | solution.py:142
  182.1 1.3 fusion.92
  184.6 1.1 select_reduce_fusion.1
  185.6 2.1 %fusion = (f32[512]{0:T(512)S(1)}, f32[512]{0:T(512)S(1)}) fusion(f32[512,2048]{1,0:T(8,128)S(1)} %get-tuple-element.46, f32[2048]{0:T(1024)S(1)} %get-tuple-element.17, f32[512]{0:T(512)S(1)} %get-tuple-element.7, pred[2048]{0:T(1024)(128)(4,1)S(1)} %get-tuple-element.18, f32[512]{0:T(512)S(1)} %get-tuple-element.8, f32[512,2048]{1,0:T(8,128)S(1)} %fusion.46), kind=kLoop, calls=%fused_computation.4 | loop fusion | flops 8387584 | bytes 8407040 | tf_op jit(solution)/shard_map/reduce_sum | solution.py:168
  187.8 1.0 fusion.23
  188.8 1.0 fusion.26
  189.9 8.6 %all_gather.43 = bf16[512,512]{0,1:T(8,128)(2,1)S(1)} all-gather(bf16[512,128]{0,1:T(8,128)(2,1)S(1)} %bitcast.163), channel_id=1, replica_groups=mesh['tz'=16,'tx'=4,'image'=2,'tensor'=4] {'tensor'}, dimensions={1}, use_global_device_ids=true | all-gather | bytes 655360 | tf_op jit(solution)/shard_map/all_gather | solution.py:179
  (94 shorter events, 13.4 us)
Async XLA Ops:
  6.5 10.1 %copy-start.7 = (bf16[320,128]{1,0:T(8,128)(2,1)S(1)}, bf16[320,128]{1,0:T(8,128)(2,1)}, u32[]{:S(2)}) copy-start(bf16[320,128]{1,0:T(8,128)(2,1)} %param.19) | copy-start | bytes 245764
  6.5 10.1 %copy-start.8 = (bf16[320,128]{1,0:T(8,128)(2,1)S(1)}, bf16[320,128]{1,0:T(8,128)(2,1)}, u32[]{:S(2)}) copy-start(bf16[320,128]{1,0:T(8,128)(2,1)} %param.20) | copy-start | bytes 245764
  6.5 12.1 %copy-start.5 = (bf16[320,2,128]{2,1,0:T(2,128)(2,1)S(1)}, bf16[320,2,128]{2,1,0:T(2,128)(2,1)}, u32[]{:S(2)}) copy-start(bf16[320,2,128]{2,1,0:T(2,128)(2,1)} %param.21) | copy-start | bytes 491524
  6.5 12.1 %copy-start.6 = (bf16[320,2,128]{2,1,0:T(2,128)(2,1)S(1)}, bf16[320,2,128]{2,1,0:T(2,128)(2,1)}, u32[]{:S(2)}) copy-start(bf16[320,2,128]{2,1,0:T(2,128)(2,1)} %param.22) | copy-start | bytes 491524
  6.5 17.2 %copy-start.9 = (bf16[160,256]{1,0:T(8,128)(2,1)S(1)}, bf16[160,256]{1,0:T(8,128)(2,1)}, u32[]{:S(2)}) copy-start(bf16[160,256]{1,0:T(8,128)(2,1)} %param.23) | copy-start | bytes 245764
  6.5 17.3 %copy-start.10 = (bf16[160,256]{1,0:T(8,128)(2,1)S(1)}, bf16[160,256]{1,0:T(8,128)(2,1)}, u32[]{:S(2)}) copy-start(bf16[160,256]{1,0:T(8,128)(2,1)} %param.24) | copy-start | bytes 245764
  6.6 19.9 %copy-start.11 = (s32[2,64]{1,0:T(2,128)S(1)}, s32[2,64]{1,0:T(2,128)}, u32[]{:S(2)}) copy-start(s32[2,64]{1,0:T(2,128)} %param.14) | copy-start | bytes 1540
  6.6 25.8 %copy-start.13 = (s32[2]{0:T(128)S(1)}, s32[2]{0:T(128)}, u32[]{:S(2)}) copy-start(s32[2]{0:T(128)} %param.15) | copy-start | bytes 28
  6.6 71.4 %all-gather.7.cloned.1.call-start = ((), (), s32[]{:S(2)}) async-start(), calls=%async_computation | async-start | bytes 1392640 | tf_op jit(solution)/shard_map/all_gather | solution.py:48
  8.5 173.7 %all-gather.9.cloned.1.call-start = ((), (), s32[]{:S(2)}) async-start(), calls=%async_computation.1 | async-start | bytes 1310720 | tf_op jit(solution)/shard_map/all_gather | solution.py:142
  9.2 63.8 %copy-start.12 = (bf16[640]{0:T(1024)(128)(2,1)S(1)}, bf16[640]{0:T(1024)(128)(2,1)}, u32[]{:S(2)}) copy-start(bf16[640]{0:T(1024)(128)(2,1)} %param.25) | copy-start | bytes 3844
  11.0 63.9 %collective-permute-start.3 = (bf16[3,3,1,1,80,640]{5,4,3,2,1,0:T(8,128)(2,1)S(1)}, bf16[3,3,1,1,80,640]{5,4,3,2,1,0:T(8,128)(2,1)}, u32[]{:S(2)}, u32[]{:S(2)}) collective-permute-start(bf16[3,3,1,1,80,640]{5,4,3,2,1,0:T(8,128)(2,1)S(1)} %fusion.12), channel_id=1, source_target_pairs={{0,4},{4,0},{1,5},{5,1},{2,6},{6,2},{3,7},{7,3},{8,12},{12,8},{9,1... | collective-permute-start | bytes 2764808 | tf_op jit(solution)/shard_map/ppermute | solution.py:36
  16.7 56.3 %collective-permute-start.5 = (bf16[320,128]{1,0:T(8,128)(2,1)S(1)}, bf16[320,128]{1,0:T(8,128)(2,1)S(1)}, u32[]{:S(2)}, u32[]{:S(2)}) collective-permute-start(bf16[320,128]{1,0:T(8,128)(2,1)S(1)} %fusion.52), channel_id=1, source_target_pairs={{0,4},{4,0},{1,5},{5,1},{2,6},{6,2},{3,7},{7,3},{8,12},{12,8},{9,1... | collective-permute-start | bytes 245768 | tf_op jit(solution)/shard_map/ppermute | solution.py:36
  18.9 54.8 %collective-permute-start.6 = (bf16[320,2,128]{2,1,0:T(2,128)(2,1)S(1)}, bf16[320,2,128]{2,1,0:T(2,128)(2,1)S(1)}, u32[]{:S(2)}, u32[]{:S(2)}) collective-permute-start(bf16[320,2,128]{2,1,0:T(2,128)(2,1)S(1)} %fusion.34), channel_id=1, source_target_pairs={{0,4},{4,0},{1,5},{5,1},{2,6},{6,2},{3,7},{7,3},{8,12},{12,8},{9,1... | collective-permute-start | bytes 491528 | tf_op jit(solution)/shard_map/ppermute | solution.py:36
  24.5 124.7 %collective-permute-start.4 = (bf16[160,256]{1,0:T(8,128)(2,1)}, bf16[160,256]{1,0:T(8,128)(2,1)}, u32[]{:S(2)}, u32[]{:S(2)}) collective-permute-start(bf16[160,256]{1,0:T(8,128)(2,1)} %fusion.50), channel_id=1, source_target_pairs={{0,4},{4,0},{1,5},{5,1},{2,6},{6,2},{3,7},{7,3},{8,12},{12,8},{9,1... | collective-permute-start | bytes 245768 | tf_op jit(solution)/shard_map/ppermute | solution.py:36
  78.9 11.8 %collective-permute-start = (bf16[2,160,128]{2,1,0:T(8,128)(2,1)S(1)}, bf16[2,160,128]{2,1,0:T(8,128)(2,1)S(1)}, u32[]{:S(2)}, u32[]{:S(2)}) collective-permute-start(bf16[2,160,128]{2,1,0:T(8,128)(2,1)S(1)} %pad_maximum_fusion.3), channel_id=1, source_target_pairs={{0,8},{8,16},{16,24},{24,0},{1,9},{9,17},{17,25},{25,1},{2,10},{10... | collective-permute-start | bytes 245768 | tf_op jit(solution)/shard_map/ppermute | solution.py:61
  82.0 8.7 %collective-permute-start.1 = (bf16[2,160,128]{2,1,0:T(8,128)(2,1)S(1)}, bf16[2,160,128]{2,1,0:T(8,128)(2,1)S(1)}, u32[]{:S(2)}, u32[]{:S(2)}) collective-permute-start(bf16[2,160,128]{2,1,0:T(8,128)(2,1)S(1)} %pad_maximum_fusion.4), channel_id=1, source_target_pairs={{0,16},{8,24},{16,0},{24,8},{1,17},{9,25},{17,1},{25,9},{2,18},{10... | collective-permute-start | bytes 245768 | tf_op jit(solution)/shard_map/ppermute | solution.py:61
  86.3 5.2 %collective-permute-start.2 = (bf16[2,160,128]{2,1,0:T(8,128)(2,1)S(1)}, bf16[2,160,128]{2,1,0:T(8,128)(2,1)S(1)}, u32[]{:S(2)}, u32[]{:S(2)}) collective-permute-start(bf16[2,160,128]{2,1,0:T(8,128)(2,1)S(1)} %pad_maximum_fusion.5), channel_id=1, source_target_pairs={{0,24},{8,0},{16,8},{24,16},{1,25},{9,1},{17,9},{25,17},{2,26},{10... | collective-permute-start | bytes 245768 | tf_op jit(solution)/shard_map/ppermute | solution.py:61
  112.4 0.7 copy-start.14
  112.9 1.5 copy-start
  116.2 0.9 copy-start.1
  116.2 7.7 %copy-start.2 = (bf16[640,2,128]{2,1,0:T(2,128)(2,1)S(1)}, bf16[640,2,128]{2,1,0:T(2,128)(2,1)}, u32[]{:S(2)}) copy-start(bf16[640,2,128]{2,1,0:T(2,128)(2,1)} %pad_maximum_fusion.1) | copy-start | bytes 983044
  150.1 16.6 %copy-start.3 = (bf16[320,128]{1,0:T(8,128)(2,1)S(1)}, bf16[320,128]{1,0:T(8,128)(2,1)}, u32[]{:S(2)}) copy-start(bf16[320,128]{1,0:T(8,128)(2,1)} %get-tuple-element.38) | copy-start | bytes 245764
  150.1 16.6 %copy-start.4 = (bf16[320,128]{1,0:T(8,128)(2,1)S(1)}, bf16[320,128]{1,0:T(8,128)(2,1)}, u32[]{:S(2)}) copy-start(bf16[320,128]{1,0:T(8,128)(2,1)} %get-tuple-element.39) | copy-start | bytes 245764
Sparse Core Ops, SparseCore 0:
  9.5 68.4 all-gather.6
  149.3 32.7 all-gather.8

commit v5 on v4

--- a/solution.py
+++ b/solution.py
@@ -117,7 +117,8 @@
     halo_full = lax.all_gather(jnp.stack([upper, lower]), "tensor", axis=1, tiled=True)
     padded = jnp.concatenate([halo_full[0:1], block_full, halo_full[1:2]], axis=0)
     conv_out = convolve(padded, conv_w, (0, 0))
-    section = (feats.astype(jnp.float32) + conv_out).astype(jnp.bfloat16)
+    section_r = lax.reduce_precision(feats.astype(jnp.float32) + conv_out, exponent_bits=8, mantissa_bits=7)
+    section = section_r.astype(jnp.bfloat16)
     section_full = lax.all_gather(section, "tensor", axis=1, tiled=True)
     channels = section_full.shape[1]
     cells = tile_rows * tile_cols
@@ -130,7 +131,7 @@
     )
     att_shard = queries.shape[1]
     head_count = att_shard // HD
-    pooled = section.astype(jnp.float32).reshape(
+    pooled = section_r.reshape(
         tile_rows // POOL, POOL, chan_shard, tile_cols // POOL, POOL
     ).mean(axis=(1, 4))
     tok_count = pooled.shape[0] * pooled.shape[2]
@@ -181,7 +182,7 @@
         out_w, attended_full, (((1,), (1,)), ((), ())), preferred_element_type=jnp.float32
     )
     projected = jnp.transpose(projected.reshape(chan_shard, tile_rows, tile_cols), (1, 0, 2))
-    final = (section.astype(jnp.float32) + projected) * live_flag
+    final = (section_r + projected) * live_flag
     return final.astype(jnp.bfloat16).reshape(1, tile_rows, chan_shard, tile_cols)
 
 

time: 207 us -> 207 us (level)
  no operation moved by 1% of the time
where the time goes in v5:
time: 207 us; the launch traced here: 206 us
  blocking collectives  87.6 us (42%)
  between operations  42.2 us (20%)
  starting transfers between devices  24.7 us (12%)
  other arithmetic  18.2 us (9%)
  waiting for transfers between devices  17.6 us (9%)
  local copies, waits for them, and re-layouts  9.43 us (5%)
  matrix products  6.48 us (3%)
    all_gather x1, blocking collectives, on_device(): kv_column = lax.all_gather(kv_local, 'tz', axis=0, tiled=False)  25.1 us
    all_gather x1, blocking collectives, on_device(): lax.all_gather(jnp.stack([upper, lower]), 'tensor', axis=1, tiled=True)  16.9 us
    all_gather x1, blocking collectives, on_device(): block_full = lax.all_gather(activated, 'tensor', axis=1, tiled=True)  15.7 us
    all_gather x1, blocking collectives, on_device(): section_full = lax.all_gather(section, 'tensor', axis=1, tiled=True)  15.2 us
    all_gather x1, waiting for transfers between devices, on_device(): kv_all = lax.all_gather(kv_column, 'tx', axis=0, tiled=False)  15 us
    ppermute x4, starting transfers between devices, image_pair(): other = lax.ppermute(part, 'image', [(0, 1), (1, 0)])  14.3 us
    ppermute x3, starting transfers between devices, halo_rows(): lax.ppermute(chunk, 'tx', [(i, (i + shift) % n_x) for i in range(n_x)])  10.3 us
    all_gather x1, blocking collectives, on_device(): attended_full = lax.all_gather(attended, 'tensor', axis=1, tiled=True)  8.57 us
  transfers between devices with their start and end apart: 9, of which 3 were waited for; matrix products, arithmetic and copies ran while one was open for 11% of the time, Pallas kernels for 0%

profile of v5, /device:TPU:1, one launch (start us, length us, event | category | flops | bytes accessed | tf_op | source)
XLA Modules:
  0.0 206.3 jit_solution(7356651788305153388)
XLA Ops:
  6.6 1.1 fusion.38
  9.2 1.8 fusion.12
  11.0 5.7 %collective-permute-start.3 = (bf16[3,3,1,1,80,640]{5,4,3,2,1,0:T(8,128)(2,1)S(1)}, bf16[3,3,1,1,80,640]{5,4,3,2,1,0:T(8,128)(2,1)}, u32[]{:S(2)}, u32[]{:S(2)}) collective-permute-start(bf16[3,3,1,1,80,640]{5,4,3,2,1,0:T(8,128)(2,1)S(1)} %fusion.12), channel_id=1, source_target_pairs={{0,4},{4,0},{1,5},{5,1},{2,6},{6,2},{3,7},{7,3},{8,12},{12,8},{9,1... | collective-permute-start | bytes 2764808 | tf_op jit(solution)/shard_map/ppermute | solution.py:36
  16.7 1.9 collective-permute-start.5
  18.9 4.9 %collective-permute-start.6 = (bf16[320,2,128]{2,1,0:T(2,128)(2,1)S(1)}, bf16[320,2,128]{2,1,0:T(2,128)(2,1)S(1)}, u32[]{:S(2)}, u32[]{:S(2)}) collective-permute-start(bf16[320,2,128]{2,1,0:T(2,128)(2,1)S(1)} %fusion.34), channel_id=1, source_target_pairs={{0,4},{4,0},{1,5},{5,1},{2,6},{6,2},{3,7},{7,3},{8,12},{12,8},{9,1... | collective-permute-start | bytes 491528 | tf_op jit(solution)/shard_map/ppermute | solution.py:36
  24.5 1.9 collective-permute-start.4
  34.0 15.7 %all_gather.36 = bf16[4,640,128]{2,0,1:T(4,128)(2,1)S(1)} all-gather(bf16[4,160,128]{2,0,1:T(4,128)(2,1)S(1)} %copy.165), channel_id=1, replica_groups=mesh['tz'=16,'tx'=4,'image'=2,'tensor'=4] {'tensor'}, dimensions={1}, use_global_device_ids=true | all-gather | bytes 819200 | tf_op jit(solution)/shard_map/all_gather | solution.py:116
  73.7 1.1 pad_maximum_fusion.1
  74.9 1.4 broadcast_select_fusion.1
  76.2 1.8 all-gather.7.cloned.1.call-done
  78.0 0.9 fusion.73
  78.9 3.1 %collective-permute-start = (bf16[2,160,128]{2,1,0:T(8,128)(2,1)S(1)}, bf16[2,160,128]{2,1,0:T(8,128)(2,1)S(1)}, u32[]{:S(2)}, u32[]{:S(2)}) collective-permute-start(bf16[2,160,128]{2,1,0:T(8,128)(2,1)S(1)} %pad_maximum_fusion.3), channel_id=1, source_target_pairs={{0,8},{8,16},{16,24},{24,0},{1,9},{9,17},{17,25},{25,1},{2,10},{10... | collective-permute-start | bytes 245768 | tf_op jit(solution)/shard_map/ppermute | solution.py:61
  82.0 4.3 %collective-permute-start.1 = (bf16[2,160,128]{2,1,0:T(8,128)(2,1)S(1)}, bf16[2,160,128]{2,1,0:T(8,128)(2,1)S(1)}, u32[]{:S(2)}, u32[]{:S(2)}) collective-permute-start(bf16[2,160,128]{2,1,0:T(8,128)(2,1)S(1)} %pad_maximum_fusion.4), channel_id=1, source_target_pairs={{0,16},{8,24},{16,0},{24,8},{1,17},{9,25},{17,1},{25,9},{2,18},{10... | collective-permute-start | bytes 245768 | tf_op jit(solution)/shard_map/ppermute | solution.py:61
  86.3 2.9 %collective-permute-start.2 = (bf16[2,160,128]{2,1,0:T(8,128)(2,1)S(1)}, bf16[2,160,128]{2,1,0:T(8,128)(2,1)S(1)}, u32[]{:S(2)}, u32[]{:S(2)}) collective-permute-start(bf16[2,160,128]{2,1,0:T(8,128)(2,1)S(1)} %pad_maximum_fusion.5), channel_id=1, source_target_pairs={{0,24},{8,0},{16,8},{24,16},{1,25},{9,1},{17,9},{25,17},{2,26},{10... | collective-permute-start | bytes 245768 | tf_op jit(solution)/shard_map/ppermute | solution.py:61
  89.3 1.5 pad_maximum_fusion
  92.4 16.9 %all_gather.35 = bf16[2,640,128]{2,1,0:T(8,128)(2,1)S(1)} all-gather(bf16[2,160,128]{2,1,0:T(8,128)(2,1)S(1)} %pad_maximum_fusion.6), channel_id=1, replica_groups=mesh['tz'=16,'tx'=4,'image'=2,'tensor'=4] {'tensor'}, dimensions={1}, use_global_device_ids=true | all-gather | bytes 409600 | tf_op jit(solution)/shard_map/all_gather | solution.py:117
  109.9 1.1 maximum_bitcast_fusion
  111.0 1.2 copy.185
  113.1 1.2 copy-done.1
  114.4 1.8 convolution_select_fusion
  117.6 6.2 %all-gather.1 = bf16[1,32,640]{1,0,2:T(2,128)(2,1)S(1)} all-gather(bf16[1,32,160]{1,0,2:T(2,128)(2,1)S(1)} %copy.178), channel_id=3, replica_groups=mesh['tz'=16,'tx'=4,'image'=2,'tensor'=4] {'tensor'}, dimensions={2}, use_global_device_ids=true | all-gather | bytes 51200 | tf_op jit(solution)/shard_map/all_gather | solution.py:139
  124.1 25.1 %all-gather.2 = bf16[512,256]{1,0:T(8,128)(2,1)} all-gather(bf16[32,256]{1,0:T(8,128)(2,1)S(1)} %convolution_convert_fusion), channel_id=4, replica_groups=mesh['tz'=16,'tx'=4,'image'=2,'tensor'=4] {'tz'}, dimensions={0}, use_global_device_ids=true | all-gather | bytes 278528 | tf_op jit(solution)/shard_map/all_gather | solution.py:142
  149.2 0.9 broadcast_select_fusion.7
  150.3 15.2 %all_gather.37 = bf16[4,640,128]{2,0,1:T(4,128)(2,1)S(1)} all-gather(bf16[4,160,128]{2,0,1:T(4,128)(2,1)S(1)} %copy.173), channel_id=1, replica_groups=mesh['tz'=16,'tx'=4,'image'=2,'tensor'=4] {'tensor'}, dimensions={1}, use_global_device_ids=true | all-gather | bytes 819200 | tf_op jit(solution)/shard_map/all_gather | solution.py:122
  165.5 0.9 copy.174
  167.1 15.0 %all-gather.9.cloned.1.call-done = bf16[64,32,256]{2,1,0:T(8,128)(2,1)} async-done(((bf16[16,32,256]{2,1,0:T(8,128)(2,1)}), bf16[64,32,256]{2,1,0:T(8,128)(2,1)}) %all-gather.9.cloned.1.call-update) | async-done | bytes 1048592 | tf_op jit(solution)/shard_map/all_gather | solution.py:143
  182.1 1.3 fusion.94
  184.6 1.1 select_reduce_fusion.1
  185.6 2.1 %fusion = (f32[512]{0:T(512)S(1)}, f32[512]{0:T(512)S(1)}) fusion(f32[512,2048]{1,0:T(8,128)S(1)} %get-tuple-element.46, f32[2048]{0:T(1024)S(1)} %get-tuple-element.17, f32[512]{0:T(512)S(1)} %get-tuple-element.7, pred[2048]{0:T(1024)(128)(4,1)S(1)} %get-tuple-element.18, f32[512]{0:T(512)S(1)} %get-tuple-element.8, f32[512,2048]{1,0:T(8,128)S(1)} %fusion.47), kind=kLoop, calls=%fused_computation.4 | loop fusion | flops 8387584 | bytes 8407040 | tf_op jit(solution)/shard_map/reduce_sum | solution.py:169
  187.8 1.0 fusion.23
  188.8 1.0 fusion.26
  189.9 8.6 %all_gather.43 = bf16[512,512]{0,1:T(8,128)(2,1)S(1)} all-gather(bf16[512,128]{0,1:T(8,128)(2,1)S(1)} %bitcast.173), channel_id=1, replica_groups=mesh['tz'=16,'tx'=4,'image'=2,'tensor'=4] {'tensor'}, dimensions={1}, use_global_device_ids=true | all-gather | bytes 655360 | tf_op jit(solution)/shard_map/all_gather | solution.py:180
  (94 shorter events, 13.5 us)
Async XLA Ops:
  6.5 10.1 %copy-start.7 = (bf16[320,128]{1,0:T(8,128)(2,1)S(1)}, bf16[320,128]{1,0:T(8,128)(2,1)}, u32[]{:S(2)}) copy-start(bf16[320,128]{1,0:T(8,128)(2,1)} %param.19) | copy-start | bytes 245764
  6.5 10.1 %copy-start.8 = (bf16[320,128]{1,0:T(8,128)(2,1)S(1)}, bf16[320,128]{1,0:T(8,128)(2,1)}, u32[]{:S(2)}) copy-start(bf16[320,128]{1,0:T(8,128)(2,1)} %param.20) | copy-start | bytes 245764
  6.5 12.1 %copy-start.5 = (bf16[320,2,128]{2,1,0:T(2,128)(2,1)S(1)}, bf16[320,2,128]{2,1,0:T(2,128)(2,1)}, u32[]{:S(2)}) copy-start(bf16[320,2,128]{2,1,0:T(2,128)(2,1)} %param.21) | copy-start | bytes 491524
  6.5 12.1 %copy-start.6 = (bf16[320,2,128]{2,1,0:T(2,128)(2,1)S(1)}, bf16[320,2,128]{2,1,0:T(2,128)(2,1)}, u32[]{:S(2)}) copy-start(bf16[320,2,128]{2,1,0:T(2,128)(2,1)} %param.22) | copy-start | bytes 491524
  6.5 17.2 %copy-start.9 = (bf16[160,256]{1,0:T(8,128)(2,1)S(1)}, bf16[160,256]{1,0:T(8,128)(2,1)}, u32[]{:S(2)}) copy-start(bf16[160,256]{1,0:T(8,128)(2,1)} %param.23) | copy-start | bytes 245764
  6.5 17.3 %copy-start.10 = (bf16[160,256]{1,0:T(8,128)(2,1)S(1)}, bf16[160,256]{1,0:T(8,128)(2,1)}, u32[]{:S(2)}) copy-start(bf16[160,256]{1,0:T(8,128)(2,1)} %param.24) | copy-start | bytes 245764
  6.6 19.9 %copy-start.11 = (s32[2,64]{1,0:T(2,128)S(1)}, s32[2,64]{1,0:T(2,128)}, u32[]{:S(2)}) copy-start(s32[2,64]{1,0:T(2,128)} %param.14) | copy-start | bytes 1540
  6.6 25.8 %copy-start.13 = (s32[2]{0:T(128)S(1)}, s32[2]{0:T(128)}, u32[]{:S(2)}) copy-start(s32[2]{0:T(128)} %param.15) | copy-start | bytes 28
  6.6 71.4 %all-gather.7.cloned.1.call-start = ((), (), s32[]{:S(2)}) async-start(), calls=%async_computation | async-start | bytes 1392640 | tf_op jit(solution)/shard_map/all_gather | solution.py:48
  8.5 173.7 %all-gather.9.cloned.1.call-start = ((), (), s32[]{:S(2)}) async-start(), calls=%async_computation.1 | async-start | bytes 1310720 | tf_op jit(solution)/shard_map/all_gather | solution.py:143
  9.2 63.8 %copy-start.12 = (bf16[640]{0:T(1024)(128)(2,1)S(1)}, bf16[640]{0:T(1024)(128)(2,1)}, u32[]{:S(2)}) copy-start(bf16[640]{0:T(1024)(128)(2,1)} %param.25) | copy-start | bytes 3844
  11.0 63.9 %collective-permute-start.3 = (bf16[3,3,1,1,80,640]{5,4,3,2,1,0:T(8,128)(2,1)S(1)}, bf16[3,3,1,1,80,640]{5,4,3,2,1,0:T(8,128)(2,1)}, u32[]{:S(2)}, u32[]{:S(2)}) collective-permute-start(bf16[3,3,1,1,80,640]{5,4,3,2,1,0:T(8,128)(2,1)S(1)} %fusion.12), channel_id=1, source_target_pairs={{0,4},{4,0},{1,5},{5,1},{2,6},{6,2},{3,7},{7,3},{8,12},{12,8},{9,1... | collective-permute-start | bytes 2764808 | tf_op jit(solution)/shard_map/ppermute | solution.py:36
  16.7 56.3 %collective-permute-start.5 = (bf16[320,128]{1,0:T(8,128)(2,1)S(1)}, bf16[320,128]{1,0:T(8,128)(2,1)S(1)}, u32[]{:S(2)}, u32[]{:S(2)}) collective-permute-start(bf16[320,128]{1,0:T(8,128)(2,1)S(1)} %fusion.54), channel_id=1, source_target_pairs={{0,4},{4,0},{1,5},{5,1},{2,6},{6,2},{3,7},{7,3},{8,12},{12,8},{9,1... | collective-permute-start | bytes 245768 | tf_op jit(solution)/shard_map/ppermute | solution.py:36
  18.9 54.8 %collective-permute-start.6 = (bf16[320,2,128]{2,1,0:T(2,128)(2,1)S(1)}, bf16[320,2,128]{2,1,0:T(2,128)(2,1)S(1)}, u32[]{:S(2)}, u32[]{:S(2)}) collective-permute-start(bf16[320,2,128]{2,1,0:T(2,128)(2,1)S(1)} %fusion.34), channel_id=1, source_target_pairs={{0,4},{4,0},{1,5},{5,1},{2,6},{6,2},{3,7},{7,3},{8,12},{12,8},{9,1... | collective-permute-start | bytes 491528 | tf_op jit(solution)/shard_map/ppermute | solution.py:36
  24.5 124.7 %collective-permute-start.4 = (bf16[160,256]{1,0:T(8,128)(2,1)}, bf16[160,256]{1,0:T(8,128)(2,1)}, u32[]{:S(2)}, u32[]{:S(2)}) collective-permute-start(bf16[160,256]{1,0:T(8,128)(2,1)} %fusion.52), channel_id=1, source_target_pairs={{0,4},{4,0},{1,5},{5,1},{2,6},{6,2},{3,7},{7,3},{8,12},{12,8},{9,1... | collective-permute-start | bytes 245768 | tf_op jit(solution)/shard_map/ppermute | solution.py:36
  78.9 11.8 %collective-permute-start = (bf16[2,160,128]{2,1,0:T(8,128)(2,1)S(1)}, bf16[2,160,128]{2,1,0:T(8,128)(2,1)S(1)}, u32[]{:S(2)}, u32[]{:S(2)}) collective-permute-start(bf16[2,160,128]{2,1,0:T(8,128)(2,1)S(1)} %pad_maximum_fusion.3), channel_id=1, source_target_pairs={{0,8},{8,16},{16,24},{24,0},{1,9},{9,17},{17,25},{25,1},{2,10},{10... | collective-permute-start | bytes 245768 | tf_op jit(solution)/shard_map/ppermute | solution.py:61
  82.0 8.7 %collective-permute-start.1 = (bf16[2,160,128]{2,1,0:T(8,128)(2,1)S(1)}, bf16[2,160,128]{2,1,0:T(8,128)(2,1)S(1)}, u32[]{:S(2)}, u32[]{:S(2)}) collective-permute-start(bf16[2,160,128]{2,1,0:T(8,128)(2,1)S(1)} %pad_maximum_fusion.4), channel_id=1, source_target_pairs={{0,16},{8,24},{16,0},{24,8},{1,17},{9,25},{17,1},{25,9},{2,18},{10... | collective-permute-start | bytes 245768 | tf_op jit(solution)/shard_map/ppermute | solution.py:61
  86.3 5.2 %collective-permute-start.2 = (bf16[2,160,128]{2,1,0:T(8,128)(2,1)S(1)}, bf16[2,160,128]{2,1,0:T(8,128)(2,1)S(1)}, u32[]{:S(2)}, u32[]{:S(2)}) collective-permute-start(bf16[2,160,128]{2,1,0:T(8,128)(2,1)S(1)} %pad_maximum_fusion.5), channel_id=1, source_target_pairs={{0,24},{8,0},{16,8},{24,16},{1,25},{9,1},{17,9},{25,17},{2,26},{10... | collective-permute-start | bytes 245768 | tf_op jit(solution)/shard_map/ppermute | solution.py:61
  112.4 0.7 copy-start.14
  112.9 1.5 copy-start.1
  116.2 0.9 copy-start
  116.2 7.7 %copy-start.2 = (bf16[640,2,128]{2,1,0:T(2,128)(2,1)S(1)}, bf16[640,2,128]{2,1,0:T(2,128)(2,1)}, u32[]{:S(2)}) copy-start(bf16[640,2,128]{2,1,0:T(2,128)(2,1)} %pad_maximum_fusion.1) | copy-start | bytes 983044
  150.1 16.6 %copy-start.3 = (bf16[320,128]{1,0:T(8,128)(2,1)S(1)}, bf16[320,128]{1,0:T(8,128)(2,1)}, u32[]{:S(2)}) copy-start(bf16[320,128]{1,0:T(8,128)(2,1)} %get-tuple-element.38) | copy-start | bytes 245764
  150.1 16.6 %copy-start.4 = (bf16[320,128]{1,0:T(8,128)(2,1)S(1)}, bf16[320,128]{1,0:T(8,128)(2,1)}, u32[]{:S(2)}) copy-start(bf16[320,128]{1,0:T(8,128)(2,1)} %get-tuple-element.39) | copy-start | bytes 245764
Sparse Core Ops, SparseCore 0:
  9.5 68.4 all-gather.6
  149.3 32.7 all-gather.8

commit v6 on v5

--- a/solution.py
+++ b/solution.py
@@ -7,7 +7,8 @@
 
 HD = 64
 POOL = 4
-TILE_AXES = ("tz", "tx")
+TILE_AXES = ("zh", "zl", "tx")
+Z_AXES = ("zh", "zl")
 
 
 def blend(ema_part, adjusted_part, blend_ratio):
@@ -45,7 +46,8 @@
 
 
 def halo_rows(rims, slot_row, my_slot, tz_i, tx_i, n_x):
-    column = lax.all_gather(rims, "tz", axis=0, tiled=False)
+    near = lax.all_gather(rims, "zl", axis=0, tiled=False)
+    column = lax.all_gather(near, "zh", axis=0, tiled=False).reshape((-1,) + rims.shape)
     received = [None]
     for shift in range(1, n_x):
         dest_tile = tz_i * n_x + (tx_i + shift) % n_x
@@ -87,7 +89,8 @@
     norm_gain,
 ):
     image_index = lax.axis_index("image")
-    tile_index = lax.axis_index("tz") * lax.axis_size("tx") + lax.axis_index("tx")
+    z_index = lax.axis_index("zh") * lax.axis_size("zl") + lax.axis_index("zl")
+    tile_index = z_index * lax.axis_size("tx") + lax.axis_index("tx")
     slot_row = lax.dynamic_index_in_dim(tile_slot, image_index, 0, keepdims=False)
     live_count = lax.dynamic_index_in_dim(tile_count, image_index, 0, keepdims=False)
     my_slot = lax.dynamic_index_in_dim(slot_row, tile_index, 0, keepdims=False)
@@ -100,7 +103,7 @@
     rim_rows = jnp.stack([activated[0], activated[-1]])
     n_x = lax.axis_size("tx")
     upper, lower = halo_rows(
-        rim_rows, slot_row, my_slot, lax.axis_index("tz"), lax.axis_index("tx"), n_x
+        rim_rows, slot_row, my_slot, z_index, lax.axis_index("tx"), n_x
     )
 
     conv_w = image_pair(blend(conv_ema, conv_adjusted, blend_ratio), image_index, 3)
@@ -139,7 +142,7 @@
     pooled = lax.all_gather(pooled, "tensor", axis=1, tiled=True)
     kv_flat = kv_w.reshape(channels, 2 * att_shard)
     kv_local = jnp.dot(pooled, kv_flat, preferred_element_type=jnp.float32).astype(jnp.bfloat16)
-    kv_column = lax.all_gather(kv_local, "tz", axis=0, tiled=False)
+    kv_column = lax.all_gather(kv_local, Z_AXES, axis=0, tiled=False)
     kv_all = lax.all_gather(kv_column, "tx", axis=0, tiled=False)
     n_z = kv_all.shape[1]
     kv_rows = kv_all.reshape(-1, 2 * att_shard)
@@ -189,10 +192,11 @@
 def solution(mesh):
     tiles = mesh.shape["tile"]
     inner = 4 if tiles % 4 == 0 else 1
+    low = 4 if (tiles // inner) % 4 == 0 else 1
     devices = np.asarray(mesh.devices).reshape(
-        (tiles // inner, inner, mesh.shape["image"], mesh.shape["tensor"])
-    )
-    split = Mesh(devices, ("tz", "tx", "image", "tensor"))
+        (tiles // inner // low, low, inner, mesh.shape["image"], mesh.shape["tensor"])
+    )
+    split = Mesh(devices, ("zh", "zl", "tx", "image", "tensor"))
     placed = (
         P("image", TILE_AXES, "tensor", None),
         P(),

time: 207 us -> 218 us (1.053)
  waiting for transfers between devices: 17.6 us -> 24.9 us
  blocking collectives: 87.6 us -> 91.2 us
    all_gather x1 -> x2, blocking collectives: 25.1 us -> 37.6 us  [the longest x1 23.1 us: on_device(): kv_column = lax.all_gather(kv_local, Z_AXES, axis=0, tiled=False)]
    all_gather x1, blocking collectives: 16.9 us -> 8.86 us  [on_device(): lax.all_gather(jnp.stack([upper, lower]), 'tensor', axis=1, tiled=True)]
    all_gather x1, waiting for transfers between devices: 1.79 us -> 8.84 us  [halo_rows(): lax.all_gather(near, 'zh', axis=0, tiled=False).reshape((-1,) + rims.shape)]
  transfers between devices with their start and end apart: 9 -> 9, of which waited for: 3 -> 2; matrix products, arithmetic and copies ran while one was open for 11% -> 10% of each run, Pallas kernels for 0% -> 0%
where the time goes in v6:
time: 218 us; the launch traced here: 217 us
  blocking collectives  91.2 us (42%)
  between operations  42.4 us (19%)
  starting transfers between devices  25 us (11%)
  waiting for transfers between devices  24.9 us (11%)
  other arithmetic  17.6 us (8%)
  local copies, waits for them, and re-layouts  9.43 us (4%)
  matrix products  6.46 us (3%)
    all_gather x1, blocking collectives, on_device(): kv_column = lax.all_gather(kv_local, Z_AXES, axis=0, tiled=False)  23.1 us
    all_gather x1, waiting for transfers between devices, on_device(): kv_all = lax.all_gather(kv_column, 'tx', axis=0, tiled=False)  16 us
    all_gather x1, blocking collectives, on_device(): block_full = lax.all_gather(activated, 'tensor', axis=1, tiled=True)  15.5 us
    all_gather x1, blocking collectives, on_device(): section_full = lax.all_gather(section, 'tensor', axis=1, tiled=True)  14.5 us
    all_gather x1, blocking collectives, halo_rows(): near = lax.all_gather(rims, 'zl', axis=0, tiled=False)  14.5 us
    ppermute x4, starting transfers between devices, image_pair(): other = lax.ppermute(part, 'image', [(0, 1), (1, 0)])  14.1 us
    ppermute x3, starting transfers between devices, halo_rows(): lax.ppermute(chunk, 'tx', [(i, (i + shift) % n_x) for i in range(n_x)])  10.9 us
    all_gather x1, blocking collectives, on_device(): lax.all_gather(jnp.stack([upper, lower]), 'tensor', axis=1, tiled=True)  8.86 us
  transfers between devices with their start and end apart: 9, of which 2 were waited for; matrix products, arithmetic and copies ran while one was open for 10% of the time, Pallas kernels for 0%

profile of v6, /device:TPU:1, one launch (start us, length us, event | category | flops | bytes accessed | tf_op | source)
XLA Modules:
  0.0 217.0 jit_solution(8112966900079000190)
XLA Ops:
  6.6 1.1 fusion.38
  7.8 14.5 %all-gather = bf16[8,160,128]{2,1,0:T(8,128)(2,1)} all-gather(bf16[2,160,128]{2,1,0:T(8,128)(2,1)S(1)} %pad_maximum_fusion.2), channel_id=2, replica_groups=mesh['zh'=4,'zl'=4,'tx'=4,'image'=2,'tensor'=4] {'zl'}, dimensions={0}, use_global_device_ids=true | all-gather | bytes 409600 | tf_op jit(solution)/shard_map/all_gather | solution.py:49
  23.0 1.8 fusion.12
  24.8 5.4 %collective-permute-start.3 = (bf16[3,3,1,1,80,640]{5,4,3,2,1,0:T(8,128)(2,1)S(1)}, bf16[3,3,1,1,80,640]{5,4,3,2,1,0:T(8,128)(2,1)}, u32[]{:S(2)}, u32[]{:S(2)}) collective-permute-start(bf16[3,3,1,1,80,640]{5,4,3,2,1,0:T(8,128)(2,1)S(1)} %fusion.12), channel_id=1, source_target_pairs={{0,4},{4,0},{1,5},{5,1},{2,6},{6,2},{3,7},{7,3},{8,12},{12,8},{9,1... | collective-permute-start | bytes 2764808 | tf_op jit(solution)/shard_map/ppermute | solution.py:37
  30.2 1.9 collective-permute-start.5
  32.4 4.9 %collective-permute-start.6 = (bf16[320,2,128]{2,1,0:T(2,128)(2,1)S(1)}, bf16[320,2,128]{2,1,0:T(2,128)(2,1)S(1)}, u32[]{:S(2)}, u32[]{:S(2)}) collective-permute-start(bf16[320,2,128]{2,1,0:T(2,128)(2,1)S(1)} %fusion.34), channel_id=1, source_target_pairs={{0,4},{4,0},{1,5},{5,1},{2,6},{6,2},{3,7},{7,3},{8,12},{12,8},{9,1... | collective-permute-start | bytes 491528 | tf_op jit(solution)/shard_map/ppermute | solution.py:37
  38.0 1.9 collective-permute-start.4
  47.7 15.5 %all_gather.44 = bf16[4,640,128]{2,0,1:T(4,128)(2,1)S(1)} all-gather(bf16[4,160,128]{2,0,1:T(4,128)(2,1)S(1)} %copy.165), channel_id=1, replica_groups=mesh['zh'=4,'zl'=4,'tx'=4,'image'=2,'tensor'=4] {'tensor'}, dimensions={1}, use_global_device_ids=true | all-gather | bytes 819200 | tf_op jit(solution)/shard_map/all_gather | solution.py:119
  87.2 1.1 pad_maximum_fusion.1
  88.4 1.4 broadcast_select_fusion.1
  89.8 8.8 %all-gather.8.cloned.1.call-done = bf16[16,2,160,128]{3,2,1,0:T(8,128)(2,1)} async-done(((bf16[4,2,160,128]{3,2,1,0:T(8,128)(2,1)}), bf16[16,2,160,128]{3,2,1,0:T(8,128)(2,1)}) %all-gather.8.cloned.1.call-update) | async-done | bytes 1310736 | tf_op jit(solution)/shard_map/all_gather | solution.py:50
  98.6 0.9 fusion.73
  99.5 2.8 %collective-permute-start = (bf16[2,160,128]{2,1,0:T(8,128)(2,1)S(1)}, bf16[2,160,128]{2,1,0:T(8,128)(2,1)S(1)}, u32[]{:S(2)}, u32[]{:S(2)}) collective-permute-start(bf16[2,160,128]{2,1,0:T(8,128)(2,1)S(1)} %pad_maximum_fusion.3), channel_id=1, source_target_pairs={{0,8},{8,16},{16,24},{24,0},{1,9},{9,17},{17,25},{25,1},{2,10},{10... | collective-permute-start | bytes 245768 | tf_op jit(solution)/shard_map/ppermute | solution.py:63
  102.4 4.4 %collective-permute-start.1 = (bf16[2,160,128]{2,1,0:T(8,128)(2,1)S(1)}, bf16[2,160,128]{2,1,0:T(8,128)(2,1)S(1)}, u32[]{:S(2)}, u32[]{:S(2)}) collective-permute-start(bf16[2,160,128]{2,1,0:T(8,128)(2,1)S(1)} %pad_maximum_fusion.4), channel_id=1, source_target_pairs={{0,16},{8,24},{16,0},{24,8},{1,17},{9,25},{17,1},{25,9},{2,18},{10... | collective-permute-start | bytes 245768 | tf_op jit(solution)/shard_map/ppermute | solution.py:63
  106.8 3.7 %collective-permute-start.2 = (bf16[2,160,128]{2,1,0:T(8,128)(2,1)S(1)}, bf16[2,160,128]{2,1,0:T(8,128)(2,1)S(1)}, u32[]{:S(2)}, u32[]{:S(2)}) collective-permute-start(bf16[2,160,128]{2,1,0:T(8,128)(2,1)S(1)} %pad_maximum_fusion.5), channel_id=1, source_target_pairs={{0,24},{8,0},{16,8},{24,16},{1,25},{9,1},{17,9},{25,17},{2,26},{10... | collective-permute-start | bytes 245768 | tf_op jit(solution)/shard_map/ppermute | solution.py:63
  110.5 1.5 pad_maximum_fusion
  112.8 8.9 %all_gather.43 = bf16[2,640,128]{2,1,0:T(8,128)(2,1)S(1)} all-gather(bf16[2,160,128]{2,1,0:T(8,128)(2,1)S(1)} %pad_maximum_fusion.6), channel_id=1, replica_groups=mesh['zh'=4,'zl'=4,'tx'=4,'image'=2,'tensor'=4] {'tensor'}, dimensions={1}, use_global_device_ids=true | all-gather | bytes 409600 | tf_op jit(solution)/shard_map/all_gather | solution.py:120
  122.2 1.1 maximum_bitcast_fusion
  123.4 1.2 copy.185
  125.5 1.2 copy-done.1
  126.7 1.8 convolution_select_fusion
  129.9 6.2 %all-gather.2 = bf16[1,32,640]{1,0,2:T(2,128)(2,1)S(1)} all-gather(bf16[1,32,160]{1,0,2:T(2,128)(2,1)S(1)} %copy.178), channel_id=4, replica_groups=mesh['zh'=4,'zl'=4,'tx'=4,'image'=2,'tensor'=4] {'tensor'}, dimensions={2}, use_global_device_ids=true | all-gather | bytes 51200 | tf_op jit(solution)/shard_map/all_gather | solution.py:142
  136.5 23.1 %all-gather.3 = bf16[512,256]{1,0:T(8,128)(2,1)} all-gather(bf16[32,256]{1,0:T(8,128)(2,1)S(1)} %convolution_convert_fusion), channel_id=5, replica_groups=mesh['zh'=4,'zl'=4,'tx'=4,'image'=2,'tensor'=4] {'zh','zl'}, dimensions={0}, use_global_device_ids=true | all-gather | bytes 278528 | tf_op jit(solution)/shard_map/all_gather | solution.py:145
  159.6 0.9 broadcast_select_fusion.7
  160.7 14.5 %all_gather.45 = bf16[4,640,128]{2,0,1:T(4,128)(2,1)S(1)} all-gather(bf16[4,160,128]{2,0,1:T(4,128)(2,1)S(1)} %copy.173), channel_id=1, replica_groups=mesh['zh'=4,'zl'=4,'tx'=4,'image'=2,'tensor'=4] {'tensor'}, dimensions={1}, use_global_device_ids=true | all-gather | bytes 819200 | tf_op jit(solution)/shard_map/all_gather | solution.py:125
  176.9 16.0 %all-gather.10.cloned.1.call-done = bf16[64,32,256]{2,1,0:T(8,128)(2,1)} async-done(((bf16[16,32,256]{2,1,0:T(8,128)(2,1)}), bf16[64,32,256]{2,1,0:T(8,128)(2,1)}) %all-gather.10.cloned.1.call-update) | async-done | bytes 1048592 | tf_op jit(solution)/shard_map/all_gather | solution.py:146
  192.8 1.3 fusion.94
  195.3 1.1 select_reduce_fusion.1
  196.3 2.1 fusion
  198.5 1.0 fusion.23
  199.5 1.0 fusion.26
  200.6 8.6 %all_gather.51 = bf16[512,512]{0,1:T(8,128)(2,1)S(1)} all-gather(bf16[512,128]{0,1:T(8,128)(2,1)S(1)} %bitcast.174), channel_id=1, replica_groups=mesh['zh'=4,'zl'=4,'tx'=4,'image'=2,'tensor'=4] {'tensor'}, dimensions={1}, use_global_device_ids=true | all-gather | bytes 655360 | tf_op jit(solution)/shard_map/all_gather | solution.py:183
  (95 shorter events, 12.9 us)
Async XLA Ops:
  6.5 23.6 %copy-start.7 = (bf16[320,128]{1,0:T(8,128)(2,1)S(1)}, bf16[320,128]{1,0:T(8,128)(2,1)}, u32[]{:S(2)}) copy-start(bf16[320,128]{1,0:T(8,128)(2,1)} %param.19) | copy-start | bytes 245764
  6.5 23.6 %copy-start.8 = (bf16[320,128]{1,0:T(8,128)(2,1)S(1)}, bf16[320,128]{1,0:T(8,128)(2,1)}, u32[]{:S(2)}) copy-start(bf16[320,128]{1,0:T(8,128)(2,1)} %param.20) | copy-start | bytes 245764
  6.5 25.6 %copy-start.5 = (bf16[320,2,128]{2,1,0:T(2,128)(2,1)S(1)}, bf16[320,2,128]{2,1,0:T(2,128)(2,1)}, u32[]{:S(2)}) copy-start(bf16[320,2,128]{2,1,0:T(2,128)(2,1)} %param.21) | copy-start | bytes 491524
  6.5 25.6 %copy-start.6 = (bf16[320,2,128]{2,1,0:T(2,128)(2,1)S(1)}, bf16[320,2,128]{2,1,0:T(2,128)(2,1)}, u32[]{:S(2)}) copy-start(bf16[320,2,128]{2,1,0:T(2,128)(2,1)} %param.22) | copy-start | bytes 491524
  6.5 30.8 %copy-start.9 = (bf16[160,256]{1,0:T(8,128)(2,1)S(1)}, bf16[160,256]{1,0:T(8,128)(2,1)}, u32[]{:S(2)}) copy-start(bf16[160,256]{1,0:T(8,128)(2,1)} %param.23) | copy-start | bytes 245764
  6.5 30.8 %copy-start.10 = (bf16[160,256]{1,0:T(8,128)(2,1)S(1)}, bf16[160,256]{1,0:T(8,128)(2,1)}, u32[]{:S(2)}) copy-start(bf16[160,256]{1,0:T(8,128)(2,1)} %param.24) | copy-start | bytes 245764
  6.6 33.4 %copy-start.11 = (s32[2,64]{1,0:T(2,128)S(1)}, s32[2,64]{1,0:T(2,128)}, u32[]{:S(2)}) copy-start(s32[2,64]{1,0:T(2,128)} %param.14) | copy-start | bytes 1540
  6.6 92.0 %all-gather.8.cloned.1.call-start = ((), (), s32[]{:S(2)}) async-start(), calls=%async_computation | async-start | bytes 1638400 | tf_op jit(solution)/shard_map/all_gather | solution.py:50
  7.8 38.3 %copy-start.13 = (s32[2]{0:T(128)S(1)}, s32[2]{0:T(128)}, u32[]{:S(2)}) copy-start(s32[2]{0:T(128)} %param.15) | copy-start | bytes 28
  22.3 170.5 %all-gather.10.cloned.1.call-start = ((), (), s32[]{:S(2)}) async-start(), calls=%async_computation.1 | async-start | bytes 1310720 | tf_op jit(solution)/shard_map/all_gather | solution.py:146
  23.0 63.5 %copy-start.12 = (bf16[640]{0:T(1024)(128)(2,1)S(1)}, bf16[640]{0:T(1024)(128)(2,1)}, u32[]{:S(2)}) copy-start(bf16[640]{0:T(1024)(128)(2,1)} %param.25) | copy-start | bytes 3844
  24.8 63.6 %collective-permute-start.3 = (bf16[3,3,1,1,80,640]{5,4,3,2,1,0:T(8,128)(2,1)S(1)}, bf16[3,3,1,1,80,640]{5,4,3,2,1,0:T(8,128)(2,1)}, u32[]{:S(2)}, u32[]{:S(2)}) collective-permute-start(bf16[3,3,1,1,80,640]{5,4,3,2,1,0:T(8,128)(2,1)S(1)} %fusion.12), channel_id=1, source_target_pairs={{0,4},{4,0},{1,5},{5,1},{2,6},{6,2},{3,7},{7,3},{8,12},{12,8},{9,1... | collective-permute-start | bytes 2764808 | tf_op jit(solution)/shard_map/ppermute | solution.py:37
  30.2 56.3 %collective-permute-start.5 = (bf16[320,128]{1,0:T(8,128)(2,1)S(1)}, bf16[320,128]{1,0:T(8,128)(2,1)S(1)}, u32[]{:S(2)}, u32[]{:S(2)}) collective-permute-start(bf16[320,128]{1,0:T(8,128)(2,1)S(1)} %fusion.54), channel_id=1, source_target_pairs={{0,4},{4,0},{1,5},{5,1},{2,6},{6,2},{3,7},{7,3},{8,12},{12,8},{9,1... | collective-permute-start | bytes 245768 | tf_op jit(solution)/shard_map/ppermute | solution.py:37
  32.4 54.8 %collective-permute-start.6 = (bf16[320,2,128]{2,1,0:T(2,128)(2,1)S(1)}, bf16[320,2,128]{2,1,0:T(2,128)(2,1)S(1)}, u32[]{:S(2)}, u32[]{:S(2)}) collective-permute-start(bf16[320,2,128]{2,1,0:T(2,128)(2,1)S(1)} %fusion.34), channel_id=1, source_target_pairs={{0,4},{4,0},{1,5},{5,1},{2,6},{6,2},{3,7},{7,3},{8,12},{12,8},{9,1... | collective-permute-start | bytes 491528 | tf_op jit(solution)/shard_map/ppermute | solution.py:37
  38.0 121.6 %collective-permute-start.4 = (bf16[160,256]{1,0:T(8,128)(2,1)}, bf16[160,256]{1,0:T(8,128)(2,1)}, u32[]{:S(2)}, u32[]{:S(2)}) collective-permute-start(bf16[160,256]{1,0:T(8,128)(2,1)} %fusion.52), channel_id=1, source_target_pairs={{0,4},{4,0},{1,5},{5,1},{2,6},{6,2},{3,7},{7,3},{8,12},{12,8},{9,1... | collective-permute-start | bytes 245768 | tf_op jit(solution)/shard_map/ppermute | solution.py:37
  99.5 12.4 %collective-permute-start = (bf16[2,160,128]{2,1,0:T(8,128)(2,1)S(1)}, bf16[2,160,128]{2,1,0:T(8,128)(2,1)S(1)}, u32[]{:S(2)}, u32[]{:S(2)}) collective-permute-start(bf16[2,160,128]{2,1,0:T(8,128)(2,1)S(1)} %pad_maximum_fusion.3), channel_id=1, source_target_pairs={{0,8},{8,16},{16,24},{24,0},{1,9},{9,17},{17,25},{25,1},{2,10},{10... | collective-permute-start | bytes 245768 | tf_op jit(solution)/shard_map/ppermute | solution.py:63
  102.4 9.6 %collective-permute-start.1 = (bf16[2,160,128]{2,1,0:T(8,128)(2,1)S(1)}, bf16[2,160,128]{2,1,0:T(8,128)(2,1)S(1)}, u32[]{:S(2)}, u32[]{:S(2)}) collective-permute-start(bf16[2,160,128]{2,1,0:T(8,128)(2,1)S(1)} %pad_maximum_fusion.4), channel_id=1, source_target_pairs={{0,16},{8,24},{16,0},{24,8},{1,17},{9,25},{17,1},{25,9},{2,18},{10... | collective-permute-start | bytes 245768 | tf_op jit(solution)/shard_map/ppermute | solution.py:63
  106.8 5.2 %collective-permute-start.2 = (bf16[2,160,128]{2,1,0:T(8,128)(2,1)S(1)}, bf16[2,160,128]{2,1,0:T(8,128)(2,1)S(1)}, u32[]{:S(2)}, u32[]{:S(2)}) collective-permute-start(bf16[2,160,128]{2,1,0:T(8,128)(2,1)S(1)} %pad_maximum_fusion.5), channel_id=1, source_target_pairs={{0,24},{8,0},{16,8},{24,16},{1,25},{9,1},{17,9},{25,17},{2,26},{10... | collective-permute-start | bytes 245768 | tf_op jit(solution)/shard_map/ppermute | solution.py:63
  124.8 0.7 copy-start.14
  125.2 1.5 copy-start.1
  128.6 0.9 copy-start
  128.6 7.7 %copy-start.2 = (bf16[640,2,128]{2,1,0:T(2,128)(2,1)S(1)}, bf16[640,2,128]{2,1,0:T(2,128)(2,1)}, u32[]{:S(2)}) copy-start(bf16[640,2,128]{2,1,0:T(2,128)(2,1)} %pad_maximum_fusion.1) | copy-start | bytes 983044
  160.6 15.9 %copy-start.3 = (bf16[320,128]{1,0:T(8,128)(2,1)S(1)}, bf16[320,128]{1,0:T(8,128)(2,1)}, u32[]{:S(2)}) copy-start(bf16[320,128]{1,0:T(8,128)(2,1)} %get-tuple-element.38) | copy-start | bytes 245764
  160.6 15.9 %copy-start.4 = (bf16[320,128]{1,0:T(8,128)(2,1)S(1)}, bf16[320,128]{1,0:T(8,128)(2,1)}, u32[]{:S(2)}) copy-start(bf16[320,128]{1,0:T(8,128)(2,1)} %get-tuple-element.39) | copy-start | bytes 245764
Sparse Core Ops, SparseCore 0:
  22.4 76.1 all-gather.7
  159.7 33.0 all-gather.9

commit v7 on v5

--- a/solution.py
+++ b/solution.py
@@ -114,9 +114,12 @@
     upper = jnp.where(has_upper, upper, jnp.zeros_like(upper))
     lower = jnp.where(has_lower, lower, jnp.zeros_like(lower))
     block_full = lax.all_gather(activated, "tensor", axis=1, tiled=True)
+    conv_inner = convolve(block_full, conv_w, (1, 1))
     halo_full = lax.all_gather(jnp.stack([upper, lower]), "tensor", axis=1, tiled=True)
-    padded = jnp.concatenate([halo_full[0:1], block_full, halo_full[1:2]], axis=0)
-    conv_out = convolve(padded, conv_w, (0, 0))
+    up_term = convolve(halo_full[0:1], conv_w[0:1], (0, 0))
+    down_term = convolve(halo_full[1:2], conv_w[2:3], (0, 0))
+    middle = jnp.zeros((tile_rows - 2,) + up_term.shape[1:], jnp.float32)
+    conv_out = conv_inner + jnp.concatenate([up_term, middle, down_term], axis=0)
     section_r = lax.reduce_precision(feats.astype(jnp.float32) + conv_out, exponent_bits=8, mantissa_bits=7)
     section = section_r.astype(jnp.bfloat16)
     section_full = lax.all_gather(section, "tensor", axis=1, tiled=True)

time: 207 us -> 203 us (0.981)
  blocking collectives: 87.6 us -> 83.9 us
    all_gather x1, blocking collectives: 16.9 us -> 14.2 us  [on_device(): lax.all_gather(jnp.stack([upper, lower]), 'tensor', axis=1, tiled=True)]
    select_n x4 -> x3, other arithmetic: 3.03 us -> 0.95 us  [image_pair(): first = jnp.where(image_index == 0, part, other)]
  transfers between devices with their start and end apart: 9 -> 9, of which waited for: 3 -> 2; matrix products, arithmetic and copies ran while one was open for 11% -> 11% of each run, Pallas kernels for 0% -> 0%
where the time goes in v7:
time: 203 us; the launch traced here: 202 us
  blocking collectives  83.9 us (41%)
  between operations  42.3 us (21%)
  starting transfers between devices  25 us (12%)
  other arithmetic  17 us (8%)
  waiting for transfers between devices  16.3 us (8%)
  local copies, waits for them, and re-layouts  9.22 us (5%)
  matrix products  8.24 us (4%)
    all_gather x1, blocking collectives, on_device(): kv_column = lax.all_gather(kv_local, 'tz', axis=0, tiled=False)  25.3 us
    all_gather x1, blocking collectives, on_device(): section_full = lax.all_gather(section, 'tensor', axis=1, tiled=True)  15 us
    all_gather x1, waiting for transfers between devices, on_device(): kv_all = lax.all_gather(kv_column, 'tx', axis=0, tiled=False)  15 us
    all_gather x1, blocking collectives, on_device(): block_full = lax.all_gather(activated, 'tensor', axis=1, tiled=True)  14.7 us
    ppermute x4, starting transfers between devices, image_pair(): other = lax.ppermute(part, 'image', [(0, 1), (1, 0)])  14.4 us
    all_gather x1, blocking collectives, on_device(): lax.all_gather(jnp.stack([upper, lower]), 'tensor', axis=1, tiled=True)  14.2 us
    ppermute x3, starting transfers between devices, halo_rows(): lax.ppermute(chunk, 'tx', [(i, (i + shift) % n_x) for i in range(n_x)])  10.5 us
    all_gather x1, blocking collectives, on_device(): attended_full = lax.all_gather(attended, 'tensor', axis=1, tiled=True)  8.38 us
  transfers between devices with their start and end apart: 9, of which 2 were waited for; matrix products, arithmetic and copies ran while one was open for 11% of the time, Pallas kernels for 0%

profile of v7, /device:TPU:1, one launch (start us, length us, event | category | flops | bytes accessed | tf_op | source)
XLA Modules:
  0.0 201.9 jit_solution(6211034707098917592)
XLA Ops:
  6.6 1.1 fusion.42
  9.0 1.8 fusion.11
  10.9 5.7 %collective-permute-start = (bf16[3,3,1,1,80,640]{5,4,3,2,1,0:T(8,128)(2,1)S(1)}, bf16[3,3,1,1,80,640]{5,4,3,2,1,0:T(8,128)(2,1)}, u32[]{:S(2)}, u32[]{:S(2)}) collective-permute-start(bf16[3,3,1,1,80,640]{5,4,3,2,1,0:T(8,128)(2,1)S(1)} %fusion.11), channel_id=1, source_target_pairs={{0,4},{4,0},{1,5},{5,1},{2,6},{6,2},{3,7},{7,3},{8,12},{12,8},{9,1... | collective-permute-start | bytes 2764808 | tf_op jit(solution)/shard_map/ppermute | solution.py:36
  16.5 1.0 fusion.69
  17.5 1.9 collective-permute-start.5
  19.4 1.3 fusion.38
  20.7 4.9 %collective-permute-start.6 = (bf16[320,2,128]{2,1,0:T(2,128)(2,1)S(1)}, bf16[320,2,128]{2,1,0:T(2,128)(2,1)S(1)}, u32[]{:S(2)}, u32[]{:S(2)}) collective-permute-start(bf16[320,2,128]{2,1,0:T(2,128)(2,1)S(1)} %fusion.38), channel_id=1, source_target_pairs={{0,4},{4,0},{1,5},{5,1},{2,6},{6,2},{3,7},{7,3},{8,12},{12,8},{9,1... | collective-permute-start | bytes 491528 | tf_op jit(solution)/shard_map/ppermute | solution.py:36
  25.6 1.9 collective-permute-start.4
  34.8 14.7 %all_gather.33 = bf16[4,640,128]{2,0,1:T(4,128)(2,1)S(1)} all-gather(bf16[4,160,128]{2,0,1:T(4,128)(2,1)S(1)} %copy.251), channel_id=1, replica_groups=mesh['tz'=16,'tx'=4,'image'=2,'tensor'=4] {'tensor'}, dimensions={1}, use_global_device_ids=true | all-gather | bytes 819200 | tf_op jit(solution)/shard_map/all_gather | solution.py:116
  73.0 1.0 copy.281
  76.5 1.4 broadcast_select_fusion
  78.1 1.8 convolution_select_fusion
  80.5 0.9 fusion.90
  81.4 3.1 %collective-permute-start.1 = (bf16[2,160,128]{2,1,0:T(8,128)(2,1)S(1)}, bf16[2,160,128]{2,1,0:T(8,128)(2,1)S(1)}, u32[]{:S(2)}, u32[]{:S(2)}) collective-permute-start(bf16[2,160,128]{2,1,0:T(8,128)(2,1)S(1)} %pad_maximum_fusion.3), channel_id=1, source_target_pairs={{0,8},{8,16},{16,24},{24,0},{1,9},{9,17},{17,25},{25,1},{2,10},{10... | collective-permute-start | bytes 245768 | tf_op jit(solution)/shard_map/ppermute | solution.py:61
  84.6 4.4 %collective-permute-start.2 = (bf16[2,160,128]{2,1,0:T(8,128)(2,1)S(1)}, bf16[2,160,128]{2,1,0:T(8,128)(2,1)S(1)}, u32[]{:S(2)}, u32[]{:S(2)}) collective-permute-start(bf16[2,160,128]{2,1,0:T(8,128)(2,1)S(1)} %pad_maximum_fusion.4), channel_id=1, source_target_pairs={{0,16},{8,24},{16,0},{24,8},{1,17},{9,25},{17,1},{25,9},{2,18},{10... | collective-permute-start | bytes 245768 | tf_op jit(solution)/shard_map/ppermute | solution.py:61
  88.9 3.1 %collective-permute-start.3 = (bf16[2,160,128]{2,1,0:T(8,128)(2,1)S(1)}, bf16[2,160,128]{2,1,0:T(8,128)(2,1)S(1)}, u32[]{:S(2)}, u32[]{:S(2)}) collective-permute-start(bf16[2,160,128]{2,1,0:T(8,128)(2,1)S(1)} %pad_maximum_fusion.5), channel_id=1, source_target_pairs={{0,24},{8,0},{16,8},{24,16},{1,25},{9,1},{17,9},{25,17},{2,26},{10... | collective-permute-start | bytes 245768 | tf_op jit(solution)/shard_map/ppermute | solution.py:61
  92.0 1.2 fusion.29
  93.2 1.2 collective-permute-done.3
  95.3 14.2 %all_gather.36 = bf16[2,640,128]{2,1,0:T(8,128)(2,1)S(1)} all-gather(bf16[2,160,128]{2,1,0:T(8,128)(2,1)S(1)} %pad_maximum_fusion.6), channel_id=1, replica_groups=mesh['tz'=16,'tx'=4,'image'=2,'tensor'=4] {'tensor'}, dimensions={1}, use_global_device_ids=true | all-gather | bytes 409600 | tf_op jit(solution)/shard_map/all_gather | solution.py:118
  109.9 1.4 convolution_select_fusion.2
  113.1 6.2 %all-gather.1 = bf16[1,32,640]{1,0,2:T(2,128)(2,1)S(1)} all-gather(bf16[1,32,160]{1,0,2:T(2,128)(2,1)S(1)} %copy.272), channel_id=3, replica_groups=mesh['tz'=16,'tx'=4,'image'=2,'tensor'=4] {'tensor'}, dimensions={2}, use_global_device_ids=true | all-gather | bytes 51200 | tf_op jit(solution)/shard_map/all_gather | solution.py:142
  119.6 25.3 %all-gather.2 = bf16[512,256]{1,0:T(8,128)(2,1)} all-gather(bf16[32,256]{1,0:T(8,128)(2,1)S(1)} %convolution_convert_fusion), channel_id=4, replica_groups=mesh['tz'=16,'tx'=4,'image'=2,'tensor'=4] {'tz'}, dimensions={0}, use_global_device_ids=true | all-gather | bytes 278528 | tf_op jit(solution)/shard_map/all_gather | solution.py:145
  144.9 0.9 broadcast_select_fusion.7
  146.1 15.0 %all_gather.37 = bf16[4,640,128]{2,0,1:T(4,128)(2,1)S(1)} all-gather(bf16[4,160,128]{2,0,1:T(4,128)(2,1)S(1)} %copy.267), channel_id=1, replica_groups=mesh['tz'=16,'tx'=4,'image'=2,'tensor'=4] {'tensor'}, dimensions={1}, use_global_device_ids=true | all-gather | bytes 819200 | tf_op jit(solution)/shard_map/all_gather | solution.py:125
  161.1 0.9 copy.268
  162.8 15.0 %all-gather.9.cloned.1.call-done = bf16[64,32,256]{2,1,0:T(8,128)(2,1)} async-done(((bf16[16,32,256]{2,1,0:T(8,128)(2,1)}), bf16[64,32,256]{2,1,0:T(8,128)(2,1)}) %all-gather.9.cloned.1.call-update) | async-done | bytes 1048592 | tf_op jit(solution)/shard_map/all_gather | solution.py:146
  177.8 1.3 fusion.118
  180.2 1.1 select_reduce_fusion.1
  181.3 2.1 %fusion = (f32[512]{0:T(512)S(1)}, f32[512]{0:T(512)S(1)}) fusion(f32[512,2048]{1,0:T(8,128)S(1)} %get-tuple-element.48, f32[2048]{0:T(1024)S(1)} %get-tuple-element.17, f32[512]{0:T(512)S(1)} %get-tuple-element.7, pred[2048]{0:T(1024)(128)(4,1)S(1)} %get-tuple-element.18, f32[512]{0:T(512)S(1)} %get-tuple-element.8, f32[512,2048]{1,0:T(8,128)S(1)} %fusion.51), kind=kLoop, calls=%fused_computation.4 | loop fusion | flops 8387584 | bytes 8407040 | tf_op jit(solution)/shard_map/reduce_sum | solution.py:172
  183.4 1.0 fusion.17
  184.5 1.0 fusion.20
  185.6 8.4 %all_gather.43 = bf16[512,512]{0,1:T(8,128)(2,1)S(1)} all-gather(bf16[512,128]{0,1:T(8,128)(2,1)S(1)} %bitcast.207), channel_id=1, replica_groups=mesh['tz'=16,'tx'=4,'image'=2,'tensor'=4] {'tensor'}, dimensions={1}, use_global_device_ids=true | all-gather | bytes 655360 | tf_op jit(solution)/shard_map/all_gather | solution.py:183
  (103 shorter events, 13.5 us)
Async XLA Ops:
  6.5 19.0 %copy-start.5 = (bf16[160,256]{1,0:T(8,128)(2,1)S(1)}, bf16[160,256]{1,0:T(8,128)(2,1)}, u32[]{:S(2)}) copy-start(bf16[160,256]{1,0:T(8,128)(2,1)} %param.23) | copy-start | bytes 245764
  6.5 19.0 %copy-start.6 = (bf16[160,256]{1,0:T(8,128)(2,1)S(1)}, bf16[160,256]{1,0:T(8,128)(2,1)}, u32[]{:S(2)}) copy-start(bf16[160,256]{1,0:T(8,128)(2,1)} %param.24) | copy-start | bytes 245764
  6.5 21.1 %copy-start.7 = (s32[2,64]{1,0:T(2,128)S(1)}, s32[2,64]{1,0:T(2,128)}, u32[]{:S(2)}) copy-start(s32[2,64]{1,0:T(2,128)} %param.14) | copy-start | bytes 1540
  6.5 26.6 %copy-start.9 = (s32[2]{0:T(128)S(1)}, s32[2]{0:T(128)}, u32[]{:S(2)}) copy-start(s32[2]{0:T(128)} %param.15) | copy-start | bytes 28
  6.5 73.9 %all-gather.7.cloned.1.call-start = ((), (), s32[]{:S(2)}) async-start(), calls=%async_computation | async-start | bytes 1392640 | tf_op jit(solution)/shard_map/all_gather | solution.py:48
  8.3 169.4 %all-gather.9.cloned.1.call-start = ((), (), s32[]{:S(2)}) async-start(), calls=%async_computation.1 | async-start | bytes 1310720 | tf_op jit(solution)/shard_map/all_gather | solution.py:146
  10.8 65.0 %copy-start.8 = (bf16[640]{0:T(1024)(128)(2,1)S(1)}, bf16[640]{0:T(1024)(128)(2,1)}, u32[]{:S(2)}) copy-start(bf16[640]{0:T(1024)(128)(2,1)} %param.25) | copy-start | bytes 3844
  10.9 65.6 %collective-permute-start = (bf16[3,3,1,1,80,640]{5,4,3,2,1,0:T(8,128)(2,1)S(1)}, bf16[3,3,1,1,80,640]{5,4,3,2,1,0:T(8,128)(2,1)}, u32[]{:S(2)}, u32[]{:S(2)}) collective-permute-start(bf16[3,3,1,1,80,640]{5,4,3,2,1,0:T(8,128)(2,1)S(1)} %fusion.11), channel_id=1, source_target_pairs={{0,4},{4,0},{1,5},{5,1},{2,6},{6,2},{3,7},{7,3},{8,12},{12,8},{9,1... | collective-permute-start | bytes 2764808 | tf_op jit(solution)/shard_map/ppermute | solution.py:36
  17.5 58.5 %collective-permute-start.5 = (bf16[320,128]{1,0:T(8,128)(2,1)S(1)}, bf16[320,128]{1,0:T(8,128)(2,1)S(1)}, u32[]{:S(2)}, u32[]{:S(2)}) collective-permute-start(bf16[320,128]{1,0:T(8,128)(2,1)S(1)} %fusion.69), channel_id=1, source_target_pairs={{0,4},{4,0},{1,5},{5,1},{2,6},{6,2},{3,7},{7,3},{8,12},{12,8},{9,1... | collective-permute-start | bytes 245768 | tf_op jit(solution)/shard_map/ppermute | solution.py:36
  20.7 55.3 %collective-permute-start.6 = (bf16[320,2,128]{2,1,0:T(2,128)(2,1)S(1)}, bf16[320,2,128]{2,1,0:T(2,128)(2,1)S(1)}, u32[]{:S(2)}, u32[]{:S(2)}) collective-permute-start(bf16[320,2,128]{2,1,0:T(2,128)(2,1)S(1)} %fusion.38), channel_id=1, source_target_pairs={{0,4},{4,0},{1,5},{5,1},{2,6},{6,2},{3,7},{7,3},{8,12},{12,8},{9,1... | collective-permute-start | bytes 491528 | tf_op jit(solution)/shard_map/ppermute | solution.py:36
  25.6 119.3 %collective-permute-start.4 = (bf16[160,256]{1,0:T(8,128)(2,1)S(1)}, bf16[160,256]{1,0:T(8,128)(2,1)}, u32[]{:S(2)}, u32[]{:S(2)}) collective-permute-start(bf16[160,256]{1,0:T(8,128)(2,1)S(1)} %fusion.67), channel_id=1, source_target_pairs={{0,4},{4,0},{1,5},{5,1},{2,6},{6,2},{3,7},{7,3},{8,12},{12,8},{9,1... | collective-permute-start | bytes 245768 | tf_op jit(solution)/shard_map/ppermute | solution.py:36
  74.4 0.9 copy-start.1
  76.0 2.1 %copy-start.2 = (bf16[4,640,1,8,17]{1,3,4,0,2:T(8,128)(2,1)S(1)}, bf16[4,640,1,8,17]{1,3,4,0,2:T(8,128)(2,1)}, u32[]{:S(2)}) copy-start(bf16[4,640,1,8,17]{1,3,4,0,2:T(8,128)(2,1)} %copy-done.1) | copy-start | bytes 2088964
  76.0 2.1 %copy-start.4 = (bf16[4,640,1,7,2]{1,3,4,0,2:T(8,128)(2,1)S(1)}, bf16[4,640,1,7,2]{1,3,4,0,2:T(8,128)(2,1)}, u32[]{:S(2)}) copy-start(bf16[4,640,1,7,2]{1,3,4,0,2:T(8,128)(2,1)} %slice.134) | copy-start | bytes 215044
  76.0 2.1 %copy-start.10 = (pred[8,17]{0,1:T(8,128)(4,1)S(1)}, pred[8,17]{0,1:T(8,128)(4,1)}, u32[]{:S(2)}) copy-start(pred[8,17]{0,1:T(8,128)(4,1)} %constant.280) | copy-start | bytes 412
  81.4 11.8 %collective-permute-start.1 = (bf16[2,160,128]{2,1,0:T(8,128)(2,1)S(1)}, bf16[2,160,128]{2,1,0:T(8,128)(2,1)S(1)}, u32[]{:S(2)}, u32[]{:S(2)}) collective-permute-start(bf16[2,160,128]{2,1,0:T(8,128)(2,1)S(1)} %pad_maximum_fusion.3), channel_id=1, source_target_pairs={{0,8},{8,16},{16,24},{24,0},{1,9},{9,17},{17,25},{25,1},{2,10},{10... | collective-permute-start | bytes 245768 | tf_op jit(solution)/shard_map/ppermute | solution.py:61
  84.6 8.6 %collective-permute-start.2 = (bf16[2,160,128]{2,1,0:T(8,128)(2,1)S(1)}, bf16[2,160,128]{2,1,0:T(8,128)(2,1)S(1)}, u32[]{:S(2)}, u32[]{:S(2)}) collective-permute-start(bf16[2,160,128]{2,1,0:T(8,128)(2,1)S(1)} %pad_maximum_fusion.4), channel_id=1, source_target_pairs={{0,16},{8,24},{16,0},{24,8},{1,17},{9,25},{17,1},{25,9},{2,18},{10... | collective-permute-start | bytes 245768 | tf_op jit(solution)/shard_map/ppermute | solution.py:61
  88.9 5.5 %collective-permute-start.3 = (bf16[2,160,128]{2,1,0:T(8,128)(2,1)S(1)}, bf16[2,160,128]{2,1,0:T(8,128)(2,1)S(1)}, u32[]{:S(2)}, u32[]{:S(2)}) collective-permute-start(bf16[2,160,128]{2,1,0:T(8,128)(2,1)S(1)} %pad_maximum_fusion.5), channel_id=1, source_target_pairs={{0,24},{8,0},{16,8},{24,16},{1,25},{9,1},{17,9},{25,17},{2,26},{10... | collective-permute-start | bytes 245768 | tf_op jit(solution)/shard_map/ppermute | solution.py:61
  93.2 18.7 %copy-start.3 = (bf16[1,3,1,2,80,640]{5,4,3,2,1,0:T(8,128)(2,1)S(1)}, bf16[1,3,1,2,80,640]{5,4,3,2,1,0:T(8,128)(2,1)}, u32[]{:S(2)}) copy-start(bf16[1,3,1,2,80,640]{5,4,3,2,1,0:T(8,128)(2,1)} %get-tuple-element.21) | copy-start | bytes 1843204
  95.3 17.3 %copy-start = (bf16[1,4,160,128]{3,2,1,0:T(8,128)(2,1)S(1)}, bf16[1,4,160,128]{3,2,1,0:T(8,128)(2,1)}, u32[]{:S(2)}) copy-start(bf16[1,4,160,128]{3,2,1,0:T(8,128)(2,1)} %param.13) | copy-start | bytes 491524
Sparse Core Ops, SparseCore 0:
  9.5 68.4 all-gather.6
  145.1 32.6 all-gather.8

commit v8 on v7

--- a/solution.py
+++ b/solution.py
@@ -46,9 +46,9 @@
 
 def halo_rows(rims, slot_row, my_slot, tz_i, tx_i, n_x):
     column = lax.all_gather(rims, "tz", axis=0, tiled=False)
-    received = [None]
-    for shift in range(1, n_x):
-        dest_tile = tz_i * n_x + (tx_i + shift) % n_x
+    chunks = []
+    for dest_x in range(n_x):
+        dest_tile = tz_i * n_x + dest_x
         dest_slot = lax.dynamic_index_in_dim(slot_row, dest_tile, 0, keepdims=False)
         up_src = owner_of(dest_slot - 1, slot_row)
         down_src = owner_of(dest_slot + 1, slot_row)
@@ -56,18 +56,12 @@
         down_part = lax.dynamic_index_in_dim(column, down_src // n_x, 0, keepdims=False)[0]
         up_part = jnp.where(up_src % n_x == tx_i, up_part, jnp.zeros_like(up_part))
         down_part = jnp.where(down_src % n_x == tx_i, down_part, jnp.zeros_like(down_part))
-        chunk = jnp.stack([up_part, down_part])
-        received.append(
-            lax.ppermute(chunk, "tx", [(i, (i + shift) % n_x) for i in range(n_x)])
-        )
+        chunks.append(jnp.stack([up_part, down_part]))
+    received = lax.all_to_all(jnp.stack(chunks), "tx", 0, 0, tiled=False)
     up_src = owner_of(my_slot - 1, slot_row)
     down_src = owner_of(my_slot + 1, slot_row)
-    up_shift = (tx_i - up_src % n_x) % n_x
-    down_shift = (tx_i - down_src % n_x) % n_x
-    up_own = lax.dynamic_index_in_dim(column, up_src // n_x, 0, keepdims=False)[1]
-    down_own = lax.dynamic_index_in_dim(column, down_src // n_x, 0, keepdims=False)[0]
-    upper = lax.select_n(up_shift, up_own, *[piece[0] for piece in received[1:]])
-    lower = lax.select_n(down_shift, down_own, *[piece[1] for piece in received[1:]])
+    upper = lax.dynamic_index_in_dim(received, up_src % n_x, 0, keepdims=False)[0]
+    lower = lax.dynamic_index_in_dim(received, down_src % n_x, 0, keepdims=False)[1]
     return upper, lower
 
 

time: 203 us -> 204 us (level)
  starting transfers between devices: 25 us -> 17.9 us
  between operations: 42.3 us -> 47.2 us
  other arithmetic: 17 us -> 20.8 us
  waiting for transfers between devices: 16.3 us -> 13.4 us
    ppermute x3 -> x0, starting transfers between devices: 10.5 us -> none  [halo_rows(): lax.ppermute(chunk, 'tx', [(i, (i + shift) % n_x) for i in range(n_x)])]
    all_gather x1, blocking collectives: 25.3 us -> 31.1 us  [on_device(): kv_column = lax.all_gather(kv_local, 'tz', axis=0, tiled=False)]
    all_gather x1, blocking collectives: 14.2 us -> 9.32 us  [on_device(): lax.all_gather(jnp.stack([upper, lower]), 'tensor', axis=1, tiled=True)]
    all_to_all x0 -> x1, starting transfers between devices: none -> 3.46 us  [halo_rows(): received = lax.all_to_all(jnp.stack(chunks), 'tx', 0, 0, tiled=False)]
    all_gather x1, waiting for transfers between devices: 15 us -> 12.4 us  [on_device(): kv_all = lax.all_gather(kv_column, 'tx', axis=0, tiled=False)]
  transfers between devices with their start and end apart: 9 -> 7, of which waited for: 2 -> 2; matrix products, arithmetic and copies ran while one was open for 11% -> 14% of each run, Pallas kernels for 0% -> 0%
where the time goes in v8:
time: 204 us; the launch traced here: 203 us
  blocking collectives  84.4 us (41%)
  between operations  47.2 us (23%)
  other arithmetic  20.8 us (10%)
  starting transfers between devices  17.9 us (9%)
  waiting for transfers between devices  13.4 us (7%)
  matrix products  9.84 us (5%)
  local copies, waits for them, and re-layouts  9.01 us (4%)
    all_gather x1, blocking collectives, on_device(): kv_column = lax.all_gather(kv_local, 'tz', axis=0, tiled=False)  31.1 us
    all_gather x1, blocking collectives, on_device(): section_full = lax.all_gather(section, 'tensor', axis=1, tiled=True)  15 us
    ppermute x4, starting transfers between devices, image_pair(): other = lax.ppermute(part, 'image', [(0, 1), (1, 0)])  14.4 us
    all_gather x1, blocking collectives, on_device(): block_full = lax.all_gather(activated, 'tensor', axis=1, tiled=True)  13.9 us
    all_gather x1, waiting for transfers between devices, on_device(): kv_all = lax.all_gather(kv_column, 'tx', axis=0, tiled=False)  12.4 us
    all_gather x1, blocking collectives, on_device(): lax.all_gather(jnp.stack([upper, lower]), 'tensor', axis=1, tiled=True)  9.32 us
    all_gather x1, blocking collectives, on_device(): attended_full = lax.all_gather(attended, 'tensor', axis=1, tiled=True)  8.83 us
    all_gather x1, blocking collectives, on_device(): pooled = lax.all_gather(pooled, 'tensor', axis=1, tiled=True)  6.22 us
  transfers between devices with their start and end apart: 7, of which 2 were waited for; matrix products, arithmetic and copies ran while one was open for 14% of the time, Pallas kernels for 0%

profile of v8, /device:TPU:1, one launch (start us, length us, event | category | flops | bytes accessed | tf_op | source)
XLA Modules:
  0.0 202.6 jit_solution(3040867425351560170)
XLA Ops:
  6.6 1.1 fusion.42
  9.0 1.8 fusion.11
  10.8 5.7 %collective-permute-start = (bf16[3,3,1,1,80,640]{5,4,3,2,1,0:T(8,128)(2,1)S(1)}, bf16[3,3,1,1,80,640]{5,4,3,2,1,0:T(8,128)(2,1)}, u32[]{:S(2)}, u32[]{:S(2)}) collective-permute-start(bf16[3,3,1,1,80,640]{5,4,3,2,1,0:T(8,128)(2,1)S(1)} %fusion.11), channel_id=1, source_target_pairs={{0,4},{4,0},{1,5},{5,1},{2,6},{6,2},{3,7},{7,3},{8,12},{12,8},{9,1... | collective-permute-start | bytes 2764808 | tf_op jit(solution)/shard_map/ppermute | solution.py:36
  16.5 1.0 fusion.69
  17.4 1.9 collective-permute-start.2
  19.4 1.3 fusion.38
  20.6 4.9 %collective-permute-start.3 = (bf16[320,2,128]{2,1,0:T(2,128)(2,1)S(1)}, bf16[320,2,128]{2,1,0:T(2,128)(2,1)S(1)}, u32[]{:S(2)}, u32[]{:S(2)}) collective-permute-start(bf16[320,2,128]{2,1,0:T(2,128)(2,1)S(1)} %fusion.38), channel_id=1, source_target_pairs={{0,4},{4,0},{1,5},{5,1},{2,6},{6,2},{3,7},{7,3},{8,12},{12,8},{9,1... | collective-permute-start | bytes 491528 | tf_op jit(solution)/shard_map/ppermute | solution.py:36
  25.6 1.9 collective-permute-start.1
  36.1 13.9 %all_gather.33 = bf16[4,640,128]{2,0,1:T(4,128)(2,1)S(1)} all-gather(bf16[4,160,128]{2,0,1:T(4,128)(2,1)S(1)} %copy.251), channel_id=1, replica_groups=mesh['tz'=16,'tx'=4,'image'=2,'tensor'=4] {'tensor'}, dimensions={1}, use_global_device_ids=true | all-gather | bytes 819200 | tf_op jit(solution)/shard_map/all_gather | solution.py:110
  77.3 1.0 copy.281
  79.3 1.3 convert_element_type.116
  82.0 1.1 pad_maximum_fusion.2
  83.1 1.4 broadcast_select_fusion
  84.5 1.5 pad_maximum_fusion
  86.0 0.9 fusion.90
  87.7 3.5 %all-to-all-start = ((bf16[4,2,160,128]{3,2,1,0:T(8,128)(2,1)}), bf16[4,2,160,128]{3,2,1,0:T(8,128)(2,1)S(1)}, u32[]{:S(2)}, u32[]{:S(2)}) async-start(bf16[4,2,160,128]{3,2,1,0:T(8,128)(2,1)} %pad_maximum_fusion.1), calls=%async_computation | async-start | bytes 655360 | tf_op jit(solution)/shard_map/all_to_all | solution.py:60
  91.2 3.4 %convolution_select_fusion = f32[4,8,17,160]{3,1,2,0:T(8,128)S(1)} fusion(bf16[3,3,160,640]{3,2,1,0:T(8,128)(2,1)} %bitcast.200, bf16[4,640,1,7,2]{1,3,4,0,2:T(8,128)(2,1)} %slice.120, bf16[4,640,1,8,17]{1,3,4,0,2:T(8,128)(2,1)S(1)} %copy.254, pred[8,17]{0,1:T(8,128)(4,1)} %constant.296), kind=kOutput, calls=%fused_computation.28 | convolution fusion | flops 838005760 | bytes 2959496 | tf_op jit(solution)/shard_map/conv_general_dilated | solution.py:19
  95.1 1.0 fusion.29
  96.1 1.0 all-to-all-done
  97.1 9.3 %all_gather.36 = bf16[2,640,128]{2,1,0:T(8,128)(2,1)S(1)} all-gather(bf16[2,160,128]{2,1,0:T(8,128)(2,1)S(1)} %pad_maximum_fusion.4), channel_id=1, replica_groups=mesh['tz'=16,'tx'=4,'image'=2,'tensor'=4] {'tensor'}, dimensions={1}, use_global_device_ids=true | all-gather | bytes 409600 | tf_op jit(solution)/shard_map/all_gather | solution.py:112
  106.8 1.5 convolution_select_fusion.2
  110.1 6.2 %all-gather.1 = bf16[1,32,640]{1,0,2:T(2,128)(2,1)S(1)} all-gather(bf16[1,32,160]{1,0,2:T(2,128)(2,1)S(1)} %copy.272), channel_id=3, replica_groups=mesh['tz'=16,'tx'=4,'image'=2,'tensor'=4] {'tensor'}, dimensions={2}, use_global_device_ids=true | all-gather | bytes 51200 | tf_op jit(solution)/shard_map/all_gather | solution.py:136
  116.7 31.1 %all-gather.2 = bf16[512,256]{1,0:T(8,128)(2,1)} all-gather(bf16[32,256]{1,0:T(8,128)(2,1)S(1)} %convolution_convert_fusion), channel_id=4, replica_groups=mesh['tz'=16,'tx'=4,'image'=2,'tensor'=4] {'tz'}, dimensions={0}, use_global_device_ids=true | all-gather | bytes 278528 | tf_op jit(solution)/shard_map/all_gather | solution.py:139
  147.8 0.9 broadcast_select_fusion.7
  148.9 15.0 %all_gather.37 = bf16[4,640,128]{2,0,1:T(4,128)(2,1)S(1)} all-gather(bf16[4,160,128]{2,0,1:T(4,128)(2,1)S(1)} %copy.267), channel_id=1, replica_groups=mesh['tz'=16,'tx'=4,'image'=2,'tensor'=4] {'tensor'}, dimensions={1}, use_global_device_ids=true | all-gather | bytes 819200 | tf_op jit(solution)/shard_map/all_gather | solution.py:119
  165.6 12.4 %all-gather.9.cloned.1.call-done = bf16[64,32,256]{2,1,0:T(8,128)(2,1)} async-done(((bf16[16,32,256]{2,1,0:T(8,128)(2,1)}), bf16[64,32,256]{2,1,0:T(8,128)(2,1)}) %all-gather.9.cloned.1.call-update) | async-done | bytes 1048592 | tf_op jit(solution)/shard_map/all_gather | solution.py:140
  178.0 1.3 fusion.120
  180.5 1.1 select_reduce_fusion.1
  181.6 2.1 %fusion = (f32[512]{0:T(512)S(1)}, f32[512]{0:T(512)S(1)}) fusion(f32[512,2048]{1,0:T(8,128)S(1)} %get-tuple-element.53, f32[2048]{0:T(1024)S(1)} %get-tuple-element.19, f32[512]{0:T(512)S(1)} %get-tuple-element.7, pred[2048]{0:T(1024)(128)(4,1)S(1)} %get-tuple-element.20, f32[512]{0:T(512)S(1)} %get-tuple-element.8, f32[512,2048]{1,0:T(8,128)S(1)} %fusion.51), kind=kLoop, calls=%fused_computation.4 | loop fusion | flops 8387584 | bytes 8407040 | tf_op jit(solution)/shard_map/reduce_sum | solution.py:166
  183.7 1.0 fusion.17
  184.8 1.0 fusion.20
  185.9 8.8 %all_gather.43 = bf16[512,512]{0,1:T(8,128)(2,1)S(1)} all-gather(bf16[512,128]{0,1:T(8,128)(2,1)S(1)} %bitcast.217), channel_id=1, replica_groups=mesh['tz'=16,'tx'=4,'image'=2,'tensor'=4] {'tensor'}, dimensions={1}, use_global_device_ids=true | all-gather | bytes 655360 | tf_op jit(solution)/shard_map/all_gather | solution.py:177
  (99 shorter events, 14.2 us)
Async XLA Ops:
  6.5 19.0 %copy-start.4 = (bf16[160,256]{1,0:T(8,128)(2,1)S(1)}, bf16[160,256]{1,0:T(8,128)(2,1)}, u32[]{:S(2)}) copy-start(bf16[160,256]{1,0:T(8,128)(2,1)} %param.23) | copy-start | bytes 245764
  6.5 19.0 %copy-start.5 = (bf16[160,256]{1,0:T(8,128)(2,1)S(1)}, bf16[160,256]{1,0:T(8,128)(2,1)}, u32[]{:S(2)}) copy-start(bf16[160,256]{1,0:T(8,128)(2,1)} %param.24) | copy-start | bytes 245764
  6.5 21.0 %copy-start.7 = (s32[2,64]{1,0:T(2,128)S(1)}, s32[2,64]{1,0:T(2,128)}, u32[]{:S(2)}) copy-start(s32[2,64]{1,0:T(2,128)} %param.14) | copy-start | bytes 1540
  6.5 27.9 %copy-start.9 = (s32[2]{0:T(128)S(1)}, s32[2]{0:T(128)}, u32[]{:S(2)}) copy-start(s32[2]{0:T(128)} %param.15) | copy-start | bytes 28
  6.5 79.4 %all-gather.7.cloned.1.call-start = ((), (), s32[]{:S(2)}) async-start(), calls=%async_computation.1 | async-start | bytes 1392640 | tf_op jit(solution)/shard_map/all_gather | solution.py:48
  10.8 72.3 %collective-permute-start = (bf16[3,3,1,1,80,640]{5,4,3,2,1,0:T(8,128)(2,1)S(1)}, bf16[3,3,1,1,80,640]{5,4,3,2,1,0:T(8,128)(2,1)}, u32[]{:S(2)}, u32[]{:S(2)}) collective-permute-start(bf16[3,3,1,1,80,640]{5,4,3,2,1,0:T(8,128)(2,1)S(1)} %fusion.11), channel_id=1, source_target_pairs={{0,4},{4,0},{1,5},{5,1},{2,6},{6,2},{3,7},{7,3},{8,12},{12,8},{9,1... | collective-permute-start | bytes 2764808 | tf_op jit(solution)/shard_map/ppermute | solution.py:36
  17.4 63.9 %collective-permute-start.2 = (bf16[320,128]{1,0:T(8,128)(2,1)S(1)}, bf16[320,128]{1,0:T(8,128)(2,1)S(1)}, u32[]{:S(2)}, u32[]{:S(2)}) collective-permute-start(bf16[320,128]{1,0:T(8,128)(2,1)S(1)} %fusion.69), channel_id=1, source_target_pairs={{0,4},{4,0},{1,5},{5,1},{2,6},{6,2},{3,7},{7,3},{8,12},{12,8},{9,1... | collective-permute-start | bytes 245768 | tf_op jit(solution)/shard_map/ppermute | solution.py:36
  20.6 61.3 %collective-permute-start.3 = (bf16[320,2,128]{2,1,0:T(2,128)(2,1)S(1)}, bf16[320,2,128]{2,1,0:T(2,128)(2,1)S(1)}, u32[]{:S(2)}, u32[]{:S(2)}) collective-permute-start(bf16[320,2,128]{2,1,0:T(2,128)(2,1)S(1)} %fusion.38), channel_id=1, source_target_pairs={{0,4},{4,0},{1,5},{5,1},{2,6},{6,2},{3,7},{7,3},{8,12},{12,8},{9,1... | collective-permute-start | bytes 491528 | tf_op jit(solution)/shard_map/ppermute | solution.py:36
  25.6 122.2 %collective-permute-start.1 = (bf16[160,256]{1,0:T(8,128)(2,1)S(1)}, bf16[160,256]{1,0:T(8,128)(2,1)}, u32[]{:S(2)}, u32[]{:S(2)}) collective-permute-start(bf16[160,256]{1,0:T(8,128)(2,1)S(1)} %fusion.67), channel_id=1, source_target_pairs={{0,4},{4,0},{1,5},{5,1},{2,6},{6,2},{3,7},{7,3},{8,12},{12,8},{9,1... | collective-permute-start | bytes 245768 | tf_op jit(solution)/shard_map/ppermute | solution.py:36
  87.7 9.3 %all-to-all-start = ((bf16[4,2,160,128]{3,2,1,0:T(8,128)(2,1)}), bf16[4,2,160,128]{3,2,1,0:T(8,128)(2,1)S(1)}, u32[]{:S(2)}, u32[]{:S(2)}) async-start(bf16[4,2,160,128]{3,2,1,0:T(8,128)(2,1)} %pad_maximum_fusion.1), calls=%async_computation | async-start | bytes 655360 | tf_op jit(solution)/shard_map/all_to_all | solution.py:60
  91.2 86.8 %all-gather.9.cloned.1.call-start = ((), (), s32[]{:S(2)}) async-start(), calls=%async_computation.2 | async-start | bytes 1310720 | tf_op jit(solution)/shard_map/all_gather | solution.py:140
  94.9 12.0 %copy-start.10 = (pred[8,17]{0,1:T(8,128)(4,1)S(1)}, pred[8,17]{0,1:T(8,128)(4,1)}, u32[]{:S(2)}) copy-start(pred[8,17]{0,1:T(8,128)(4,1)} %constant.296) | copy-start | bytes 412
  97.1 12.5 %copy-start = (bf16[1,4,160,128]{3,2,1,0:T(8,128)(2,1)S(1)}, bf16[1,4,160,128]{3,2,1,0:T(8,128)(2,1)}, u32[]{:S(2)}) copy-start(bf16[1,4,160,128]{3,2,1,0:T(8,128)(2,1)} %param.13) | copy-start | bytes 491524
  97.1 12.5 %copy-start.8 = (f32[4]{0:T(128)S(1)}, f32[4]{0:T(128)}, u32[]{:S(2)}) copy-start(f32[4]{0:T(128)} %pad.20.clone) | copy-start | bytes 52
  106.8 9.7 %copy-start.1 = (bf16[640,2,128]{2,1,0:T(2,128)(2,1)S(1)}, bf16[640,2,128]{2,1,0:T(2,128)(2,1)}, u32[]{:S(2)}) copy-start(bf16[640,2,128]{2,1,0:T(2,128)(2,1)} %pad_maximum_fusion.2) | copy-start | bytes 983044
  109.3 55.7 %copy-start.6 = (f32[640]{0:T(1024)S(1)}, f32[640]{0:T(1024)}, u32[]{:S(2)}) copy-start(f32[640]{0:T(1024)} %convert_element_type.116) | copy-start | bytes 7684
  109.7 55.5 %copy-start.2 = (bf16[320,128]{1,0:T(8,128)(2,1)S(1)}, bf16[320,128]{1,0:T(8,128)(2,1)}, u32[]{:S(2)}) copy-start(bf16[320,128]{1,0:T(8,128)(2,1)} %get-tuple-element.44) | copy-start | bytes 245764
  109.7 55.5 %copy-start.3 = (bf16[320,128]{1,0:T(8,128)(2,1)S(1)}, bf16[320,128]{1,0:T(8,128)(2,1)}, u32[]{:S(2)}) copy-start(bf16[320,128]{1,0:T(8,128)(2,1)} %get-tuple-element.45) | copy-start | bytes 245764
Sparse Core Ops, SparseCore 0:
  9.5 68.4 all-gather.6
  147.9 30.0 all-gather.8

commit v9 on v8

--- a/solution.py
+++ b/solution.py
@@ -44,8 +44,9 @@
     return jnp.sum(jnp.where(slot_row == slot, tiles, 0))
 
 
-def halo_rows(rims, slot_row, my_slot, tz_i, tx_i, n_x):
+def halo_rows(rims, early, slot_row, my_slot, tz_i, tx_i, n_x):
     column = lax.all_gather(rims, "tz", axis=0, tiled=False)
+    column, early = lax.optimization_barrier((column, early))
     chunks = []
     for dest_x in range(n_x):
         dest_tile = tz_i * n_x + dest_x
@@ -62,7 +63,7 @@
     down_src = owner_of(my_slot + 1, slot_row)
     upper = lax.dynamic_index_in_dim(received, up_src % n_x, 0, keepdims=False)[0]
     lower = lax.dynamic_index_in_dim(received, down_src % n_x, 0, keepdims=False)[1]
-    return upper, lower
+    return upper, lower, early
 
 
 def on_device(
@@ -93,22 +94,22 @@
     activated = jax.nn.silu(feats.astype(jnp.float32)).astype(jnp.bfloat16)
     rim_rows = jnp.stack([activated[0], activated[-1]])
     n_x = lax.axis_size("tx")
-    upper, lower = halo_rows(
-        rim_rows, slot_row, my_slot, lax.axis_index("tz"), lax.axis_index("tx"), n_x
-    )
-
     conv_w = image_pair(blend(conv_ema, conv_adjusted, blend_ratio), image_index, 3)
     query_w = image_pair(blend(query_ema, query_adjusted, blend_ratio), image_index, 0)
     kv_w = image_pair(blend(kv_ema, kv_adjusted, blend_ratio), image_index, 0)
     out_w = image_pair(blend(out_ema, out_adjusted, blend_ratio), image_index, 1)
     conv_w = conv_w.reshape(3, 3, -1, conv_w.shape[-1])
 
+    block_full = lax.all_gather(activated, "tensor", axis=1, tiled=True)
+    conv_inner = convolve(block_full, conv_w, (1, 1))
+    upper, lower, conv_inner = halo_rows(
+        rim_rows, conv_inner, slot_row, my_slot, lax.axis_index("tz"), lax.axis_index("tx"), n_x
+    )
+
     has_upper = my_slot > 0
     has_lower = my_slot + 1 < live_count
     upper = jnp.where(has_upper, upper, jnp.zeros_like(upper))
     lower = jnp.where(has_lower, lower, jnp.zeros_like(lower))
-    block_full = lax.all_gather(activated, "tensor", axis=1, tiled=True)
-    conv_inner = convolve(block_full, conv_w, (1, 1))
     halo_full = lax.all_gather(jnp.stack([upper, lower]), "tensor", axis=1, tiled=True)
     up_term = convolve(halo_full[0:1], conv_w[0:1], (0, 0))
     down_term = convolve(halo_full[1:2], conv_w[2:3], (0, 0))

time: 204 us -> 204 us (level)
  waiting for transfers between devices: 13.4 us -> 16.7 us
  blocking collectives: 84.4 us -> 81.6 us
    all_gather x1, blocking collectives: 31.1 us -> 25 us  [on_device(): kv_column = lax.all_gather(kv_local, 'tz', axis=0, tiled=False)]
    all_to_all x1, waiting for transfers between devices: 0.97 us -> 4.48 us  [halo_rows(): received = lax.all_to_all(jnp.stack(chunks), 'tx', 0, 0, tiled=False)]
    all_gather x1, blocking collectives: 9.32 us -> 12.2 us  [on_device(): lax.all_gather(jnp.stack([upper, lower]), 'tensor', axis=1, tiled=True)]
    select_n x3 -> x4, other arithmetic: 1.61 us -> 3.97 us  [image_pair(): first = jnp.where(image_index == 0, part, other)]
where the time goes in v9:
time: 204 us; the launch traced here: 203 us
  blocking collectives  81.6 us (40%)
  between operations  47.7 us (23%)
  other arithmetic  20.3 us (10%)
  starting transfers between devices  18.5 us (9%)
  waiting for transfers between devices  16.7 us (8%)
  matrix products  8.93 us (4%)
  local copies, waits for them, and re-layouts  8.77 us (4%)
    all_gather x1, blocking collectives, on_device(): kv_column = lax.all_gather(kv_local, 'tz', axis=0, tiled=False)  25 us
    all_gather x1, blocking collectives, on_device(): section_full = lax.all_gather(section, 'tensor', axis=1, tiled=True)  15.2 us
    ppermute x4, starting transfers between devices, image_pair(): other = lax.ppermute(part, 'image', [(0, 1), (1, 0)])  14.4 us
    all_gather x1, blocking collectives, on_device(): block_full = lax.all_gather(activated, 'tensor', axis=1, tiled=True)  13.9 us
    all_gather x1, blocking collectives, on_device(): lax.all_gather(jnp.stack([upper, lower]), 'tensor', axis=1, tiled=True)  12.2 us
    all_gather x1, waiting for transfers between devices, on_device(): kv_all = lax.all_gather(kv_column, 'tx', axis=0, tiled=False)  12.2 us
    all_gather x1, blocking collectives, on_device(): attended_full = lax.all_gather(attended, 'tensor', axis=1, tiled=True)  9.11 us
    all_gather x1, blocking collectives, on_device(): pooled = lax.all_gather(pooled, 'tensor', axis=1, tiled=True)  6.22 us
  transfers between devices with their start and end apart: 7, of which 2 were waited for; matrix products, arithmetic and copies ran while one was open for 14% of the time, Pallas kernels for 0%

profile of v9, /device:TPU:1, one launch (start us, length us, event | category | flops | bytes accessed | tf_op | source)
XLA Modules:
  0.0 202.5 jit_solution(17570375019825511891)
XLA Ops:
  7.3 1.8 fusion.11
  9.1 5.7 %collective-permute-start = (bf16[3,3,1,1,80,640]{5,4,3,2,1,0:T(8,128)(2,1)S(1)}, bf16[3,3,1,1,80,640]{5,4,3,2,1,0:T(8,128)(2,1)}, u32[]{:S(2)}, u32[]{:S(2)}) collective-permute-start(bf16[3,3,1,1,80,640]{5,4,3,2,1,0:T(8,128)(2,1)S(1)} %fusion.11), channel_id=1, source_target_pairs={{0,4},{4,0},{1,5},{5,1},{2,6},{6,2},{3,7},{7,3},{8,12},{12,8},{9,1... | collective-permute-start | bytes 2764808 | tf_op jit(solution)/shard_map/ppermute | solution.py:36
  14.8 1.0 fusion.39
  16.5 1.0 fusion.64
  17.4 1.9 collective-permute-start.2
  19.4 1.3 fusion.35
  20.6 4.9 %collective-permute-start.3 = (bf16[320,2,128]{2,1,0:T(2,128)(2,1)S(1)}, bf16[320,2,128]{2,1,0:T(2,128)(2,1)S(1)}, u32[]{:S(2)}, u32[]{:S(2)}) collective-permute-start(bf16[320,2,128]{2,1,0:T(2,128)(2,1)S(1)} %fusion.35), channel_id=1, source_target_pairs={{0,4},{4,0},{1,5},{5,1},{2,6},{6,2},{3,7},{7,3},{8,12},{12,8},{9,1... | collective-permute-start | bytes 491528 | tf_op jit(solution)/shard_map/ppermute | solution.py:36
  26.2 1.9 collective-permute-start.1
  63.2 13.9 %all_gather.35 = bf16[4,640,128]{2,0,1:T(4,128)(2,1)S(1)} all-gather(bf16[4,160,128]{2,0,1:T(4,128)(2,1)S(1)} %copy.190), channel_id=1, replica_groups=mesh['tz'=16,'tx'=4,'image'=2,'tensor'=4] {'tensor'}, dimensions={1}, use_global_device_ids=true | all-gather | bytes 819200 | tf_op jit(solution)/shard_map/all_gather | solution.py:103
  77.1 1.0 copy.220
  82.0 1.4 broadcast_select_fusion.1
  83.6 2.5 %convolution_select_fusion = f32[4,8,17,160]{3,1,2,0:T(8,128)S(1)} fusion(bf16[3,3,160,640]{3,2,1,0:T(8,128)(2,1)S(1)} %bitcast.175, bf16[4,640,1,7,2]{1,3,4,0,2:T(8,128)(2,1)S(1)} %copy-done.3, bf16[4,640,1,8,17]{1,3,4,0,2:T(8,128)(2,1)S(1)} %copy.193, pred[8,17]{0,1:T(8,128)(4,1)} %constant.296), kind=kOutput, calls=%fused_computation.28 | convolution fusion | flops 838005760 | bytes 2959496 | tf_op jit(solution)/shard_map/conv_general_dilated | solution.py:19
  86.7 1.0 fusion.85
  88.5 4.1 %all-to-all-start = ((bf16[4,2,160,128]{3,2,1,0:T(8,128)(2,1)}), bf16[4,2,160,128]{3,2,1,0:T(8,128)(2,1)}, u32[]{:S(2)}, u32[]{:S(2)}) async-start(bf16[4,2,160,128]{3,2,1,0:T(8,128)(2,1)} %pad_maximum_fusion.1), calls=%async_computation | async-start | bytes 655360 | tf_op jit(solution)/shard_map/all_to_all | solution.py:61
  93.1 1.0 fusion.29
  94.1 4.5 %all-to-all-done = bf16[4,2,160,128]{3,2,1,0:T(8,128)(2,1)} async-done(((bf16[4,2,160,128]{3,2,1,0:T(8,128)(2,1)}), bf16[4,2,160,128]{3,2,1,0:T(8,128)(2,1)}, u32[]{:S(2)}, u32[]{:S(2)}) %all-to-all-start) | async-done | bytes 327712 | tf_op jit(solution)/shard_map/all_to_all | solution.py:61
  98.6 0.8 fusion.77
  99.4 12.2 %all_gather.36 = bf16[2,640,128]{2,1,0:T(8,128)(2,1)S(1)} all-gather(bf16[2,160,128]{2,1,0:T(8,128)(2,1)S(1)} %pad_maximum_fusion.4), channel_id=1, replica_groups=mesh['tz'=16,'tx'=4,'image'=2,'tensor'=4] {'tensor'}, dimensions={1}, use_global_device_ids=true | all-gather | bytes 409600 | tf_op jit(solution)/shard_map/all_gather | solution.py:113
  112.0 1.4 convolution_select_fusion.2
  115.3 6.2 %all-gather.1 = bf16[1,32,640]{1,0,2:T(2,128)(2,1)S(1)} all-gather(bf16[1,32,160]{1,0,2:T(2,128)(2,1)S(1)} %copy.211), channel_id=3, replica_groups=mesh['tz'=16,'tx'=4,'image'=2,'tensor'=4] {'tensor'}, dimensions={2}, use_global_device_ids=true | all-gather | bytes 51200 | tf_op jit(solution)/shard_map/all_gather | solution.py:137
  121.8 25.0 %all-gather.2 = bf16[512,256]{1,0:T(8,128)(2,1)} all-gather(bf16[32,256]{1,0:T(8,128)(2,1)S(1)} %convolution_convert_fusion), channel_id=4, replica_groups=mesh['tz'=16,'tx'=4,'image'=2,'tensor'=4] {'tz'}, dimensions={0}, use_global_device_ids=true | all-gather | bytes 278528 | tf_op jit(solution)/shard_map/all_gather | solution.py:140
  146.8 0.9 broadcast_select_fusion.5
  147.7 0.9 broadcast_select_fusion.7
  148.8 15.2 %all_gather.37 = bf16[4,640,128]{2,0,1:T(4,128)(2,1)S(1)} all-gather(bf16[4,160,128]{2,0,1:T(4,128)(2,1)S(1)} %copy.206), channel_id=1, replica_groups=mesh['tz'=16,'tx'=4,'image'=2,'tensor'=4] {'tensor'}, dimensions={1}, use_global_device_ids=true | all-gather | bytes 819200 | tf_op jit(solution)/shard_map/all_gather | solution.py:120
  163.9 0.9 copy.207
  165.6 12.2 %all-gather.9.cloned.1.call-done = bf16[64,32,256]{2,1,0:T(8,128)(2,1)} async-done(((bf16[16,32,256]{2,1,0:T(8,128)(2,1)}), bf16[64,32,256]{2,1,0:T(8,128)(2,1)}) %all-gather.9.cloned.1.call-update) | async-done | bytes 1048592 | tf_op jit(solution)/shard_map/all_gather | solution.py:141
  177.8 1.3 fusion.116
  180.2 1.1 select_reduce_fusion.1
  181.3 2.2 %fusion = (f32[512]{0:T(512)S(1)}, f32[512]{0:T(512)S(1)}) fusion(f32[512,2048]{1,0:T(8,128)S(1)} %get-tuple-element.59, f32[2048]{0:T(1024)S(1)} %get-tuple-element.23, f32[512]{0:T(512)S(1)} %get-tuple-element.11, pred[2048]{0:T(1024)(128)(4,1)S(1)} %get-tuple-element.24, f32[512]{0:T(512)S(1)} %get-tuple-element.12, f32[512,2048]{1,0:T(8,128)S(1)} %fusion.46), kind=kLoop, calls=%fused_computation.4 | loop fusion | flops 8387584 | bytes 8407040 | tf_op jit(solution)/shard_map/reduce_sum | solution.py:167
  183.5 1.0 fusion.17
  184.5 1.0 fusion.20
  185.6 9.1 %all_gather.43 = bf16[512,512]{0,1:T(8,128)(2,1)S(1)} all-gather(bf16[512,128]{0,1:T(8,128)(2,1)S(1)} %bitcast.187), channel_id=1, replica_groups=mesh['tz'=16,'tx'=4,'image'=2,'tensor'=4] {'tensor'}, dimensions={1}, use_global_device_ids=true | all-gather | bytes 655360 | tf_op jit(solution)/shard_map/all_gather | solution.py:178
  (101 shorter events, 14.7 us)
Async XLA Ops:
  6.5 19.0 %copy-start.4 = (bf16[160,256]{1,0:T(8,128)(2,1)S(1)}, bf16[160,256]{1,0:T(8,128)(2,1)}, u32[]{:S(2)}) copy-start(bf16[160,256]{1,0:T(8,128)(2,1)} %param.23) | copy-start | bytes 245764
  6.5 19.0 %copy-start.5 = (bf16[160,256]{1,0:T(8,128)(2,1)S(1)}, bf16[160,256]{1,0:T(8,128)(2,1)}, u32[]{:S(2)}) copy-start(bf16[160,256]{1,0:T(8,128)(2,1)} %param.24) | copy-start | bytes 245764
  6.5 21.6 %copy-start.7 = (s32[2,64]{1,0:T(2,128)S(1)}, s32[2,64]{1,0:T(2,128)}, u32[]{:S(2)}) copy-start(s32[2,64]{1,0:T(2,128)} %param.14) | copy-start | bytes 1540
  6.5 54.0 %copy-start.10 = (s32[2]{0:T(128)S(1)}, s32[2]{0:T(128)}, u32[]{:S(2)}) copy-start(s32[2]{0:T(128)} %param.15) | copy-start | bytes 28
  6.5 80.2 %all-gather.7.cloned.1.call-start = ((), (), s32[]{:S(2)}) async-start(), calls=%async_computation.1 | async-start | bytes 1392640 | tf_op jit(solution)/shard_map/all_gather | solution.py:48
  9.1 70.0 %copy-start.8 = (bf16[640]{0:T(1024)(128)(2,1)S(1)}, bf16[640]{0:T(1024)(128)(2,1)}, u32[]{:S(2)}) copy-start(bf16[640]{0:T(1024)(128)(2,1)} %param.25) | copy-start | bytes 3844
  9.1 72.9 %collective-permute-start = (bf16[3,3,1,1,80,640]{5,4,3,2,1,0:T(8,128)(2,1)S(1)}, bf16[3,3,1,1,80,640]{5,4,3,2,1,0:T(8,128)(2,1)}, u32[]{:S(2)}, u32[]{:S(2)}) collective-permute-start(bf16[3,3,1,1,80,640]{5,4,3,2,1,0:T(8,128)(2,1)S(1)} %fusion.11), channel_id=1, source_target_pairs={{0,4},{4,0},{1,5},{5,1},{2,6},{6,2},{3,7},{7,3},{8,12},{12,8},{9,1... | collective-permute-start | bytes 2764808 | tf_op jit(solution)/shard_map/ppermute | solution.py:36
  17.4 129.4 %collective-permute-start.2 = (bf16[320,128]{1,0:T(8,128)(2,1)S(1)}, bf16[320,128]{1,0:T(8,128)(2,1)}, u32[]{:S(2)}, u32[]{:S(2)}) collective-permute-start(bf16[320,128]{1,0:T(8,128)(2,1)S(1)} %fusion.64), channel_id=1, source_target_pairs={{0,4},{4,0},{1,5},{5,1},{2,6},{6,2},{3,7},{7,3},{8,12},{12,8},{9,1... | collective-permute-start | bytes 245768 | tf_op jit(solution)/shard_map/ppermute | solution.py:36
  20.6 60.7 %collective-permute-start.3 = (bf16[320,2,128]{2,1,0:T(2,128)(2,1)S(1)}, bf16[320,2,128]{2,1,0:T(2,128)(2,1)S(1)}, u32[]{:S(2)}, u32[]{:S(2)}) collective-permute-start(bf16[320,2,128]{2,1,0:T(2,128)(2,1)S(1)} %fusion.35), channel_id=1, source_target_pairs={{0,4},{4,0},{1,5},{5,1},{2,6},{6,2},{3,7},{7,3},{8,12},{12,8},{9,1... | collective-permute-start | bytes 491528 | tf_op jit(solution)/shard_map/ppermute | solution.py:36
  26.2 121.5 %collective-permute-start.1 = (bf16[160,256]{1,0:T(8,128)(2,1)}, bf16[160,256]{1,0:T(8,128)(2,1)}, u32[]{:S(2)}, u32[]{:S(2)}) collective-permute-start(bf16[160,256]{1,0:T(8,128)(2,1)} %fusion.62), channel_id=1, source_target_pairs={{0,4},{4,0},{1,5},{5,1},{2,6},{6,2},{3,7},{7,3},{8,12},{12,8},{9,1... | collective-permute-start | bytes 245768 | tf_op jit(solution)/shard_map/ppermute | solution.py:36
  79.9 3.8 %copy-start.3 = (bf16[4,640,1,7,2]{1,3,4,0,2:T(8,128)(2,1)S(1)}, bf16[4,640,1,7,2]{1,3,4,0,2:T(8,128)(2,1)}, u32[]{:S(2)}) copy-start(bf16[4,640,1,7,2]{1,3,4,0,2:T(8,128)(2,1)} %slice.122) | copy-start | bytes 215044
  86.2 6.5 %copy-start = (bf16[80,8,128]{2,1,0:T(8,128)(2,1)S(1)}, bf16[80,8,128]{2,1,0:T(8,128)(2,1)}, u32[]{:S(2)}) copy-start(bf16[80,8,128]{2,1,0:T(8,128)(2,1)} %get-tuple-element.64) | copy-start | bytes 491524
  86.2 6.5 %copy-start.1 = (bf16[80,8,128]{2,1,0:T(8,128)(2,1)S(1)}, bf16[80,8,128]{2,1,0:T(8,128)(2,1)}, u32[]{:S(2)}) copy-start(bf16[80,8,128]{2,1,0:T(8,128)(2,1)} %get-tuple-element.65) | copy-start | bytes 491524
  87.7 24.3 %copy-start.11 = (pred[8,17]{0,1:T(8,128)(4,1)S(1)}, pred[8,17]{0,1:T(8,128)(4,1)}, u32[]{:S(2)}) copy-start(pred[8,17]{0,1:T(8,128)(4,1)} %constant.296) | copy-start | bytes 412
  88.5 10.0 %all-to-all-start = ((bf16[4,2,160,128]{3,2,1,0:T(8,128)(2,1)}), bf16[4,2,160,128]{3,2,1,0:T(8,128)(2,1)}, u32[]{:S(2)}, u32[]{:S(2)}) async-start(bf16[4,2,160,128]{3,2,1,0:T(8,128)(2,1)} %pad_maximum_fusion.1), calls=%async_computation | async-start | bytes 655360 | tf_op jit(solution)/shard_map/all_to_all | solution.py:61
  92.6 85.2 %all-gather.9.cloned.1.call-start = ((), (), s32[]{:S(2)}) async-start(), calls=%async_computation.2 | async-start | bytes 1310720 | tf_op jit(solution)/shard_map/all_gather | solution.py:141
  99.4 15.3 %copy-start.2 = (bf16[1,4,160,128]{3,2,1,0:T(8,128)(2,1)S(1)}, bf16[1,4,160,128]{3,2,1,0:T(8,128)(2,1)}, u32[]{:S(2)}) copy-start(bf16[1,4,160,128]{3,2,1,0:T(8,128)(2,1)} %param.13) | copy-start | bytes 491524
  99.4 15.3 %copy-start.9 = (f32[4]{0:T(128)S(1)}, f32[4]{0:T(128)}, u32[]{:S(2)}) copy-start(f32[4]{0:T(128)} %pad.17.clone) | copy-start | bytes 52
  114.6 50.5 %copy-start.6 = (f32[640]{0:T(1024)S(1)}, f32[640]{0:T(1024)}, u32[]{:S(2)}) copy-start(f32[640]{0:T(1024)} %convert_element_type.112) | copy-start | bytes 7684
Sparse Core Ops, SparseCore 0:
  16.6 65.0 all-gather.6
  146.9 30.8 all-gather.8

commit v10 on v7

--- a/solution.py
+++ b/solution.py
@@ -97,7 +97,7 @@
     feats = latent[0]
     tile_rows, chan_shard, tile_cols = feats.shape
     activated = jax.nn.silu(feats.astype(jnp.float32)).astype(jnp.bfloat16)
-    rim_rows = jnp.stack([activated[0], activated[-1]])
+    rim_rows = jnp.stack([feats[0], feats[-1]])
     n_x = lax.axis_size("tx")
     upper, lower = halo_rows(
         rim_rows, slot_row, my_slot, lax.axis_index("tz"), lax.axis_index("tx"), n_x
@@ -111,6 +111,8 @@
 
     has_upper = my_slot > 0
     has_lower = my_slot + 1 < live_count
+    upper = jax.nn.silu(upper.astype(jnp.float32)).astype(jnp.bfloat16)
+    lower = jax.nn.silu(lower.astype(jnp.float32)).astype(jnp.bfloat16)
     upper = jnp.where(has_upper, upper, jnp.zeros_like(upper))
     lower = jnp.where(has_lower, lower, jnp.zeros_like(lower))
     block_full = lax.all_gather(activated, "tensor", axis=1, tiled=True)

time: 203 us -> 202 us (level)
  transfers between devices with their start and end apart: 9 -> 9, of which waited for: 2 -> 2; matrix products, arithmetic and copies ran while one was open for 11% -> 12% of each run, Pallas kernels for 0% -> 0%
where the time goes in v10:
time: 202 us; the launch traced here: 201 us
  blocking collectives  83.1 us (41%)
  between operations  42.4 us (21%)
  starting transfers between devices  23.8 us (12%)
  other arithmetic  18.9 us (9%)
  waiting for transfers between devices  15.8 us (8%)
  local copies, waits for them, and re-layouts  10 us (5%)
  matrix products  7.17 us (4%)
    all_gather x1, blocking collectives, on_device(): kv_column = lax.all_gather(kv_local, 'tz', axis=0, tiled=False)  25.8 us
    all_gather x1, blocking collectives, on_device(): section_full = lax.all_gather(section, 'tensor', axis=1, tiled=True)  15 us
    ppermute x4, starting transfers between devices, image_pair(): other = lax.ppermute(part, 'image', [(0, 1), (1, 0)])  14.3 us
    all_gather x1, waiting for transfers between devices, on_device(): kv_all = lax.all_gather(kv_column, 'tx', axis=0, tiled=False)  14.3 us
    all_gather x1, blocking collectives, on_device(): block_full = lax.all_gather(activated, 'tensor', axis=1, tiled=True)  13.9 us
    all_gather x1, blocking collectives, on_device(): lax.all_gather(jnp.stack([upper, lower]), 'tensor', axis=1, tiled=True)  13.6 us
    ppermute x3, starting transfers between devices, halo_rows(): lax.ppermute(chunk, 'tx', [(i, (i + shift) % n_x) for i in range(n_x)])  9.4 us
    all_gather x1, blocking collectives, on_device(): attended_full = lax.all_gather(attended, 'tensor', axis=1, tiled=True)  8.57 us
  transfers between devices with their start and end apart: 9, of which 2 were waited for; matrix products, arithmetic and copies ran while one was open for 12% of the time, Pallas kernels for 0%

profile of v10, /device:TPU:1, one launch (start us, length us, event | category | flops | bytes accessed | tf_op | source)
XLA Modules:
  0.0 201.2 jit_solution(6264497843553617407)
XLA Ops:
  8.8 1.8 fusion.11
  10.6 5.7 %collective-permute-start = (bf16[3,3,1,1,80,640]{5,4,3,2,1,0:T(8,128)(2,1)S(1)}, bf16[3,3,1,1,80,640]{5,4,3,2,1,0:T(8,128)(2,1)}, u32[]{:S(2)}, u32[]{:S(2)}) collective-permute-start(bf16[3,3,1,1,80,640]{5,4,3,2,1,0:T(8,128)(2,1)S(1)} %fusion.11), channel_id=1, source_target_pairs={{0,4},{4,0},{1,5},{5,1},{2,6},{6,2},{3,7},{7,3},{8,12},{12,8},{9,1... | collective-permute-start | bytes 2764808 | tf_op jit(solution)/shard_map/ppermute | solution.py:36
  16.2 1.0 fusion.69
  17.2 1.9 collective-permute-start.5
  19.1 1.3 fusion.38
  20.4 4.9 %collective-permute-start.6 = (bf16[320,2,128]{2,1,0:T(2,128)(2,1)S(1)}, bf16[320,2,128]{2,1,0:T(2,128)(2,1)S(1)}, u32[]{:S(2)}, u32[]{:S(2)}) collective-permute-start(bf16[320,2,128]{2,1,0:T(2,128)(2,1)S(1)} %fusion.38), channel_id=1, source_target_pairs={{0,4},{4,0},{1,5},{5,1},{2,6},{6,2},{3,7},{7,3},{8,12},{12,8},{9,1... | collective-permute-start | bytes 491528 | tf_op jit(solution)/shard_map/ppermute | solution.py:36
  25.3 1.6 fusion.67
  26.9 1.9 collective-permute-start.4
  36.5 13.9 %all_gather.33 = bf16[4,640,128]{2,0,1:T(4,128)(2,1)S(1)} all-gather(bf16[4,160,128]{2,0,1:T(4,128)(2,1)S(1)} %copy.274), channel_id=1, replica_groups=mesh['tz'=16,'tx'=4,'image'=2,'tensor'=4] {'tensor'}, dimensions={1}, use_global_device_ids=true | all-gather | bytes 819200 | tf_op jit(solution)/shard_map/all_gather | solution.py:118
  73.7 1.0 copy.309
  76.8 1.2 pad_maximum_fusion.1
  78.0 1.4 broadcast_select_fusion
  79.6 1.8 convolution_select_fusion
  81.9 0.9 fusion.98
  82.9 2.0 collective-permute-start.1
  84.9 4.4 %collective-permute-start.2 = (bf16[2,160,128]{2,1,0:T(8,128)(2,1)S(1)}, bf16[2,160,128]{2,1,0:T(8,128)(2,1)S(1)}, u32[]{:S(2)}, u32[]{:S(2)}) collective-permute-start(bf16[2,160,128]{2,1,0:T(8,128)(2,1)S(1)} %pad_maximum_fusion.4), channel_id=1, source_target_pairs={{0,16},{8,24},{16,0},{24,8},{1,17},{9,25},{17,1},{25,9},{2,18},{10... | collective-permute-start | bytes 245768 | tf_op jit(solution)/shard_map/ppermute | solution.py:61
  89.3 3.1 %collective-permute-start.3 = (bf16[2,160,128]{2,1,0:T(8,128)(2,1)S(1)}, bf16[2,160,128]{2,1,0:T(8,128)(2,1)S(1)}, u32[]{:S(2)}, u32[]{:S(2)}) collective-permute-start(bf16[2,160,128]{2,1,0:T(8,128)(2,1)S(1)} %pad_maximum_fusion.5), channel_id=1, source_target_pairs={{0,24},{8,0},{16,8},{24,16},{1,25},{9,1},{17,9},{25,17},{2,26},{10... | collective-permute-start | bytes 245768 | tf_op jit(solution)/shard_map/ppermute | solution.py:61
  92.3 1.0 fusion.29
  93.3 1.4 collective-permute-done.3
  94.7 0.9 fusion.90
  95.7 13.6 %all_gather.36 = bf16[2,640,128]{2,0,1:T(2,128)(2,1)S(1)} all-gather(bf16[2,160,128]{2,0,1:T(2,128)(2,1)S(1)} %copy.280), channel_id=1, replica_groups=mesh['tz'=16,'tx'=4,'image'=2,'tensor'=4] {'tensor'}, dimensions={1}, use_global_device_ids=true | all-gather | bytes 409600 | tf_op jit(solution)/shard_map/all_gather | solution.py:120
  112.4 6.2 %all-gather.1 = bf16[1,32,640]{1,0,2:T(2,128)(2,1)S(1)} all-gather(bf16[1,32,160]{1,0,2:T(2,128)(2,1)S(1)} %copy.298), channel_id=3, replica_groups=mesh['tz'=16,'tx'=4,'image'=2,'tensor'=4] {'tensor'}, dimensions={2}, use_global_device_ids=true | all-gather | bytes 51200 | tf_op jit(solution)/shard_map/all_gather | solution.py:144
  118.9 25.8 %all-gather.2 = bf16[512,256]{1,0:T(8,128)(2,1)} all-gather(bf16[32,256]{1,0:T(8,128)(2,1)S(1)} %convolution_convert_fusion), channel_id=4, replica_groups=mesh['tz'=16,'tx'=4,'image'=2,'tensor'=4] {'tz'}, dimensions={0}, use_global_device_ids=true | all-gather | bytes 278528 | tf_op jit(solution)/shard_map/all_gather | solution.py:147
  144.8 0.9 broadcast_select_fusion.7
  145.9 15.0 %all_gather.37 = bf16[4,640,128]{2,0,1:T(4,128)(2,1)S(1)} all-gather(bf16[4,160,128]{2,0,1:T(4,128)(2,1)S(1)} %copy.293), channel_id=1, replica_groups=mesh['tz'=16,'tx'=4,'image'=2,'tensor'=4] {'tensor'}, dimensions={1}, use_global_device_ids=true | all-gather | bytes 819200 | tf_op jit(solution)/shard_map/all_gather | solution.py:127
  162.6 14.3 %all-gather.9.cloned.1.call-done = bf16[64,32,256]{2,1,0:T(8,128)(2,1)} async-done(((bf16[16,32,256]{2,1,0:T(8,128)(2,1)}), bf16[64,32,256]{2,1,0:T(8,128)(2,1)}) %all-gather.9.cloned.1.call-update) | async-done | bytes 1048592 | tf_op jit(solution)/shard_map/all_gather | solution.py:148
  177.0 1.3 fusion.126
  179.4 1.1 select_reduce_fusion.1
  180.5 2.1 %fusion = (f32[512]{0:T(512)S(1)}, f32[512]{0:T(512)S(1)}) fusion(f32[512,2048]{1,0:T(8,128)S(1)} %get-tuple-element.48, f32[2048]{0:T(1024)S(1)} %get-tuple-element.17, f32[512]{0:T(512)S(1)} %get-tuple-element.7, pred[2048]{0:T(1024)(128)(4,1)S(1)} %get-tuple-element.18, f32[512]{0:T(512)S(1)} %get-tuple-element.8, f32[512,2048]{1,0:T(8,128)S(1)} %fusion.51), kind=kLoop, calls=%fused_computation.4 | loop fusion | flops 8387584 | bytes 8407040 | tf_op jit(solution)/shard_map/reduce_sum | solution.py:174
  182.6 1.0 fusion.17
  183.7 1.0 fusion.20
  184.8 8.6 %all_gather.43 = bf16[512,512]{0,1:T(8,128)(2,1)S(1)} all-gather(bf16[512,128]{0,1:T(8,128)(2,1)S(1)} %bitcast.211), channel_id=1, replica_groups=mesh['tz'=16,'tx'=4,'image'=2,'tensor'=4] {'tensor'}, dimensions={1}, use_global_device_ids=true | all-gather | bytes 655360 | tf_op jit(solution)/shard_map/all_gather | solution.py:185
  (105 shorter events, 15.0 us)
Async XLA Ops:
  6.5 22.2 %copy-start = (bf16[1,4,160,128]{3,2,1,0:T(8,128)(2,1)S(1)}, bf16[1,4,160,128]{3,2,1,0:T(8,128)(2,1)}, u32[]{:S(2)}) copy-start(bf16[1,4,160,128]{3,2,1,0:T(8,128)(2,1)} %param.13) | copy-start | bytes 491524
  6.5 22.4 %copy-start.7 = (s32[2,64]{1,0:T(2,128)S(1)}, s32[2,64]{1,0:T(2,128)}, u32[]{:S(2)}) copy-start(s32[2,64]{1,0:T(2,128)} %param.14) | copy-start | bytes 1540
  6.5 28.2 %copy-start.9 = (s32[2]{0:T(128)S(1)}, s32[2]{0:T(128)}, u32[]{:S(2)}) copy-start(s32[2]{0:T(128)} %param.15) | copy-start | bytes 28
  6.5 75.4 %all-gather.7.cloned.1.call-start = ((), (), s32[]{:S(2)}) async-start(), calls=%async_computation | async-start | bytes 1392640 | tf_op jit(solution)/shard_map/all_gather | solution.py:48
  8.1 168.9 %all-gather.9.cloned.1.call-start = ((), (), s32[]{:S(2)}) async-start(), calls=%async_computation.1 | async-start | bytes 1310720 | tf_op jit(solution)/shard_map/all_gather | solution.py:148
  10.6 65.4 %copy-start.8 = (bf16[640]{0:T(1024)(128)(2,1)S(1)}, bf16[640]{0:T(1024)(128)(2,1)}, u32[]{:S(2)}) copy-start(bf16[640]{0:T(1024)(128)(2,1)} %param.25) | copy-start | bytes 3844
  10.6 67.4 %collective-permute-start = (bf16[3,3,1,1,80,640]{5,4,3,2,1,0:T(8,128)(2,1)S(1)}, bf16[3,3,1,1,80,640]{5,4,3,2,1,0:T(8,128)(2,1)}, u32[]{:S(2)}, u32[]{:S(2)}) collective-permute-start(bf16[3,3,1,1,80,640]{5,4,3,2,1,0:T(8,128)(2,1)S(1)} %fusion.11), channel_id=1, source_target_pairs={{0,4},{4,0},{1,5},{5,1},{2,6},{6,2},{3,7},{7,3},{8,12},{12,8},{9,1... | collective-permute-start | bytes 2764808 | tf_op jit(solution)/shard_map/ppermute | solution.py:36
  17.2 58.9 %collective-permute-start.5 = (bf16[320,128]{1,0:T(8,128)(2,1)S(1)}, bf16[320,128]{1,0:T(8,128)(2,1)S(1)}, u32[]{:S(2)}, u32[]{:S(2)}) collective-permute-start(bf16[320,128]{1,0:T(8,128)(2,1)S(1)} %fusion.69), channel_id=1, source_target_pairs={{0,4},{4,0},{1,5},{5,1},{2,6},{6,2},{3,7},{7,3},{8,12},{12,8},{9,1... | collective-permute-start | bytes 245768 | tf_op jit(solution)/shard_map/ppermute | solution.py:36
  20.4 56.4 %collective-permute-start.6 = (bf16[320,2,128]{2,1,0:T(2,128)(2,1)S(1)}, bf16[320,2,128]{2,1,0:T(2,128)(2,1)S(1)}, u32[]{:S(2)}, u32[]{:S(2)}) collective-permute-start(bf16[320,2,128]{2,1,0:T(2,128)(2,1)S(1)} %fusion.38), channel_id=1, source_target_pairs={{0,4},{4,0},{1,5},{5,1},{2,6},{6,2},{3,7},{7,3},{8,12},{12,8},{9,1... | collective-permute-start | bytes 491528 | tf_op jit(solution)/shard_map/ppermute | solution.py:36
  26.9 117.9 %collective-permute-start.4 = (bf16[160,256]{1,0:T(8,128)(2,1)}, bf16[160,256]{1,0:T(8,128)(2,1)}, u32[]{:S(2)}, u32[]{:S(2)}) collective-permute-start(bf16[160,256]{1,0:T(8,128)(2,1)} %fusion.67), channel_id=1, source_target_pairs={{0,4},{4,0},{1,5},{5,1},{2,6},{6,2},{3,7},{7,3},{8,12},{12,8},{9,1... | collective-permute-start | bytes 245768 | tf_op jit(solution)/shard_map/ppermute | solution.py:36
  75.1 0.9 copy-start.2
  76.8 2.8 %copy-start.3 = (bf16[4,640,1,8,17]{1,3,4,0,2:T(8,128)(2,1)S(1)}, bf16[4,640,1,8,17]{1,3,4,0,2:T(8,128)(2,1)}, u32[]{:S(2)}) copy-start(bf16[4,640,1,8,17]{1,3,4,0,2:T(8,128)(2,1)} %copy-done.2) | copy-start | bytes 2088964
  76.8 2.8 %copy-start.10 = (pred[8,17]{0,1:T(8,128)(4,1)S(1)}, pred[8,17]{0,1:T(8,128)(4,1)}, u32[]{:S(2)}) copy-start(pred[8,17]{0,1:T(8,128)(4,1)} %constant.283) | copy-start | bytes 412
  82.9 10.5 %collective-permute-start.1 = (bf16[2,160,128]{2,1,0:T(8,128)(2,1)S(1)}, bf16[2,160,128]{2,1,0:T(8,128)(2,1)S(1)}, u32[]{:S(2)}, u32[]{:S(2)}) collective-permute-start(bf16[2,160,128]{2,1,0:T(8,128)(2,1)S(1)} %pad_maximum_fusion.3), channel_id=1, source_target_pairs={{0,8},{8,16},{16,24},{24,0},{1,9},{9,17},{17,25},{25,1},{2,10},{10... | collective-permute-start | bytes 245768 | tf_op jit(solution)/shard_map/ppermute | solution.py:61
  84.9 8.5 %collective-permute-start.2 = (bf16[2,160,128]{2,1,0:T(8,128)(2,1)S(1)}, bf16[2,160,128]{2,1,0:T(8,128)(2,1)S(1)}, u32[]{:S(2)}, u32[]{:S(2)}) collective-permute-start(bf16[2,160,128]{2,1,0:T(8,128)(2,1)S(1)} %pad_maximum_fusion.4), channel_id=1, source_target_pairs={{0,16},{8,24},{16,0},{24,8},{1,17},{9,25},{17,1},{25,9},{2,18},{10... | collective-permute-start | bytes 245768 | tf_op jit(solution)/shard_map/ppermute | solution.py:61
  89.3 5.5 %collective-permute-start.3 = (bf16[2,160,128]{2,1,0:T(8,128)(2,1)S(1)}, bf16[2,160,128]{2,1,0:T(8,128)(2,1)S(1)}, u32[]{:S(2)}, u32[]{:S(2)}) collective-permute-start(bf16[2,160,128]{2,1,0:T(8,128)(2,1)S(1)} %pad_maximum_fusion.5), channel_id=1, source_target_pairs={{0,24},{8,0},{16,8},{24,16},{1,25},{9,1},{17,9},{25,17},{2,26},{10... | collective-permute-start | bytes 245768 | tf_op jit(solution)/shard_map/ppermute | solution.py:61
  93.3 16.9 %copy-start.4 = (bf16[1,3,1,2,80,640]{5,4,3,2,1,0:T(8,128)(2,1)S(1)}, bf16[1,3,1,2,80,640]{5,4,3,2,1,0:T(8,128)(2,1)}, u32[]{:S(2)}) copy-start(bf16[1,3,1,2,80,640]{5,4,3,2,1,0:T(8,128)(2,1)} %get-tuple-element.20) | copy-start | bytes 1843204
  110.2 8.5 %copy-start.1 = (bf16[640,2,128]{2,1,0:T(2,128)(2,1)S(1)}, bf16[640,2,128]{2,1,0:T(2,128)(2,1)}, u32[]{:S(2)}) copy-start(bf16[640,2,128]{2,1,0:T(2,128)(2,1)} %pad_maximum_fusion.1) | copy-start | bytes 983044
  112.0 50.3 %copy-start.5 = (bf16[320,128]{1,0:T(8,128)(2,1)S(1)}, bf16[320,128]{1,0:T(8,128)(2,1)}, u32[]{:S(2)}) copy-start(bf16[320,128]{1,0:T(8,128)(2,1)} %get-tuple-element.40) | copy-start | bytes 245764
  112.0 50.3 %copy-start.6 = (bf16[320,128]{1,0:T(8,128)(2,1)S(1)}, bf16[320,128]{1,0:T(8,128)(2,1)}, u32[]{:S(2)}) copy-start(bf16[320,128]{1,0:T(8,128)(2,1)} %get-tuple-element.41) | copy-start | bytes 245764
Sparse Core Ops, SparseCore 0:
  9.4 68.0 all-gather.6
  144.9 32.0 all-gather.8

commit v11 on v10

--- a/solution.py
+++ b/solution.py
@@ -56,10 +56,12 @@
         down_part = lax.dynamic_index_in_dim(column, down_src // n_x, 0, keepdims=False)[0]
         up_part = jnp.where(up_src % n_x == tx_i, up_part, jnp.zeros_like(up_part))
         down_part = jnp.where(down_src % n_x == tx_i, down_part, jnp.zeros_like(down_part))
-        chunk = jnp.stack([up_part, down_part])
-        received.append(
-            lax.ppermute(chunk, "tx", [(i, (i + shift) % n_x) for i in range(n_x)])
-        )
+        received.append(jnp.stack([up_part, down_part]))
+    sent = lax.all_gather(jnp.stack(received[1:]), "tx", axis=0, tiled=False)
+    received = [None] + [
+        lax.dynamic_index_in_dim(sent, (tx_i - shift) % n_x, 0, keepdims=False)[shift - 1]
+        for shift in range(1, n_x)
+    ]
     up_src = owner_of(my_slot - 1, slot_row)
     down_src = owner_of(my_slot + 1, slot_row)
     up_shift = (tx_i - up_src % n_x) % n_x

time: 202 us -> 204 us (level)
  blocking collectives: 83.1 us -> 95.7 us
  starting transfers between devices: 23.8 us -> 14.4 us
    all_gather x0 -> x1, blocking collectives: none -> 11.8 us  [halo_rows(): sent = lax.all_gather(jnp.stack(received[1:]), 'tx', axis=0, tiled=False)]
    ppermute x3 -> x0, starting transfers between devices: 9.4 us -> none  [halo_rows(): lax.ppermute(chunk, 'tx', [(i, (i + shift) % n_x) for i in range(n_x)])]
  transfers between devices with their start and end apart: 9 -> 6, of which waited for: 2 -> 1; matrix products, arithmetic and copies ran while one was open for 12% -> 12% of each run, Pallas kernels for 0% -> 0%
where the time goes in v11:
time: 204 us; the launch traced here: 203 us
  blocking collectives  95.7 us (47%)
  between operations  42.4 us (21%)
  other arithmetic  19 us (9%)
  waiting for transfers between devices  14.5 us (7%)
  starting transfers between devices  14.4 us (7%)
  local copies, waits for them, and re-layouts  9.99 us (5%)
  matrix products  7.18 us (4%)
    all_gather x1, blocking collectives, on_device(): kv_column = lax.all_gather(kv_local, 'tz', axis=0, tiled=False)  26.6 us
    all_gather x1, blocking collectives, on_device(): section_full = lax.all_gather(section, 'tensor', axis=1, tiled=True)  15 us
    all_gather x1, waiting for transfers between devices, on_device(): kv_all = lax.all_gather(kv_column, 'tx', axis=0, tiled=False)  14.5 us
    ppermute x4, starting transfers between devices, image_pair(): other = lax.ppermute(part, 'image', [(0, 1), (1, 0)])  14.3 us
    all_gather x1, blocking collectives, on_device(): block_full = lax.all_gather(activated, 'tensor', axis=1, tiled=True)  13.9 us
    all_gather x1, blocking collectives, on_device(): lax.all_gather(jnp.stack([upper, lower]), 'tensor', axis=1, tiled=True)  13.3 us
    all_gather x1, blocking collectives, halo_rows(): sent = lax.all_gather(jnp.stack(received[1:]), 'tx', axis=0, tiled=False)  11.8 us
    all_gather x1, blocking collectives, on_device(): attended_full = lax.all_gather(attended, 'tensor', axis=1, tiled=True)  8.84 us
  transfers between devices with their start and end apart: 6, of which 1 were waited for; matrix products, arithmetic and copies ran while one was open for 12% of the time, Pallas kernels for 0%

profile of v11, /device:TPU:1, one launch (start us, length us, event | category | flops | bytes accessed | tf_op | source)
XLA Modules:
  0.0 203.2 jit_solution(10716342854657555270)
XLA Ops:
  6.5 0.9 slice_bitcast_fusion.9
  8.8 1.8 fusion.11
  10.6 5.7 %collective-permute-start = (bf16[3,3,1,1,80,640]{5,4,3,2,1,0:T(8,128)(2,1)S(1)}, bf16[3,3,1,1,80,640]{5,4,3,2,1,0:T(8,128)(2,1)}, u32[]{:S(2)}, u32[]{:S(2)}) collective-permute-start(bf16[3,3,1,1,80,640]{5,4,3,2,1,0:T(8,128)(2,1)S(1)} %fusion.11), channel_id=1, source_target_pairs={{0,4},{4,0},{1,5},{5,1},{2,6},{6,2},{3,7},{7,3},{8,12},{12,8},{9,1... | collective-permute-start | bytes 2764808 | tf_op jit(solution)/shard_map/ppermute | solution.py:36
  16.2 1.0 fusion.69
  17.2 1.9 collective-permute-start.2
  19.1 1.3 fusion.38
  20.4 4.9 %collective-permute-start.3 = (bf16[320,2,128]{2,1,0:T(2,128)(2,1)S(1)}, bf16[320,2,128]{2,1,0:T(2,128)(2,1)S(1)}, u32[]{:S(2)}, u32[]{:S(2)}) collective-permute-start(bf16[320,2,128]{2,1,0:T(2,128)(2,1)S(1)} %fusion.38), channel_id=1, source_target_pairs={{0,4},{4,0},{1,5},{5,1},{2,6},{6,2},{3,7},{7,3},{8,12},{12,8},{9,1... | collective-permute-start | bytes 491528 | tf_op jit(solution)/shard_map/ppermute | solution.py:36
  25.3 1.6 fusion.67
  26.9 1.9 collective-permute-start.1
  36.5 13.9 %all_gather.39 = bf16[4,640,128]{2,0,1:T(4,128)(2,1)S(1)} all-gather(bf16[4,160,128]{2,0,1:T(4,128)(2,1)S(1)} %copy.260), channel_id=1, replica_groups=mesh['tz'=16,'tx'=4,'image'=2,'tensor'=4] {'tensor'}, dimensions={1}, use_global_device_ids=true | all-gather | bytes 819200 | tf_op jit(solution)/shard_map/all_gather | solution.py:120
  73.8 1.0 copy.295
  75.1 0.8 copy-done.2
  76.9 1.2 pad_maximum_fusion.1
  78.1 1.4 broadcast_select_fusion
  79.6 1.8 convolution_select_fusion
  82.0 1.0 fusion.29
  83.0 1.0 fusion.102
  84.0 11.8 %all-gather.1 = bf16[12,2,160,128]{3,2,1,0:T(8,128)(2,1)S(1)} all-gather(bf16[3,2,160,128]{3,2,1,0:T(8,128)(2,1)S(1)} %pad_maximum_fusion.2), channel_id=3, replica_groups=mesh['tz'=16,'tx'=4,'image'=2,'tensor'=4] {'tx'}, dimensions={0}, use_global_device_ids=true | all-gather | bytes 1228800 | tf_op jit(solution)/shard_map/all_gather | solution.py:60
  95.8 0.9 fusion.90
  96.8 13.3 %all_gather.44 = bf16[2,640,128]{2,0,1:T(2,128)(2,1)S(1)} all-gather(bf16[2,160,128]{2,0,1:T(2,128)(2,1)S(1)} %copy.266), channel_id=1, replica_groups=mesh['tz'=16,'tx'=4,'image'=2,'tensor'=4] {'tensor'}, dimensions={1}, use_global_device_ids=true | all-gather | bytes 409600 | tf_op jit(solution)/shard_map/all_gather | solution.py:122
  113.2 6.2 %all-gather.2 = bf16[1,32,640]{1,0,2:T(2,128)(2,1)S(1)} all-gather(bf16[1,32,160]{1,0,2:T(2,128)(2,1)S(1)} %copy.284), channel_id=4, replica_groups=mesh['tz'=16,'tx'=4,'image'=2,'tensor'=4] {'tensor'}, dimensions={2}, use_global_device_ids=true | all-gather | bytes 51200 | tf_op jit(solution)/shard_map/all_gather | solution.py:146
  119.7 26.6 %all-gather.3 = bf16[512,256]{1,0:T(8,128)(2,1)} all-gather(bf16[32,256]{1,0:T(8,128)(2,1)S(1)} %convolution_convert_fusion), channel_id=5, replica_groups=mesh['tz'=16,'tx'=4,'image'=2,'tensor'=4] {'tz'}, dimensions={0}, use_global_device_ids=true | all-gather | bytes 278528 | tf_op jit(solution)/shard_map/all_gather | solution.py:149
  146.3 0.9 broadcast_select_fusion.7
  147.5 15.0 %all_gather.45 = bf16[4,640,128]{2,0,1:T(4,128)(2,1)S(1)} all-gather(bf16[4,160,128]{2,0,1:T(4,128)(2,1)S(1)} %copy.279), channel_id=1, replica_groups=mesh['tz'=16,'tx'=4,'image'=2,'tensor'=4] {'tensor'}, dimensions={1}, use_global_device_ids=true | all-gather | bytes 819200 | tf_op jit(solution)/shard_map/all_gather | solution.py:129
  162.5 0.9 copy.280
  164.2 14.5 %all-gather.10.cloned.1.call-done = bf16[64,32,256]{2,1,0:T(8,128)(2,1)} async-done(((bf16[16,32,256]{2,1,0:T(8,128)(2,1)}), bf16[64,32,256]{2,1,0:T(8,128)(2,1)}) %all-gather.10.cloned.1.call-update) | async-done | bytes 1048592 | tf_op jit(solution)/shard_map/all_gather | solution.py:150
  178.6 1.3 fusion.130
  181.1 1.1 select_reduce_fusion.1
  182.2 2.1 %fusion = (f32[512]{0:T(512)S(1)}, f32[512]{0:T(512)S(1)}) fusion(f32[512,2048]{1,0:T(8,128)S(1)} %get-tuple-element.48, f32[2048]{0:T(1024)S(1)} %get-tuple-element.17, f32[512]{0:T(512)S(1)} %get-tuple-element.7, pred[2048]{0:T(1024)(128)(4,1)S(1)} %get-tuple-element.18, f32[512]{0:T(512)S(1)} %get-tuple-element.8, f32[512,2048]{1,0:T(8,128)S(1)} %fusion.51), kind=kLoop, calls=%fused_computation.4 | loop fusion | flops 8387584 | bytes 8407040 | tf_op jit(solution)/shard_map/reduce_sum | solution.py:176
  184.3 1.0 fusion.17
  185.3 1.0 fusion.20
  186.4 8.8 %all_gather.51 = bf16[512,512]{0,1:T(8,128)(2,1)S(1)} all-gather(bf16[512,128]{0,1:T(8,128)(2,1)S(1)} %bitcast.247), channel_id=1, replica_groups=mesh['tz'=16,'tx'=4,'image'=2,'tensor'=4] {'tensor'}, dimensions={1}, use_global_device_ids=true | all-gather | bytes 655360 | tf_op jit(solution)/shard_map/all_gather | solution.py:187
  (101 shorter events, 12.4 us)
Async XLA Ops:
  6.5 27.0 %copy-start = (bf16[1,4,160,128]{3,2,1,0:T(8,128)(2,1)S(1)}, bf16[1,4,160,128]{3,2,1,0:T(8,128)(2,1)}, u32[]{:S(2)}) copy-start(bf16[1,4,160,128]{3,2,1,0:T(8,128)(2,1)} %param.13) | copy-start | bytes 491524
  6.5 22.3 %copy-start.7 = (s32[2,64]{1,0:T(2,128)S(1)}, s32[2,64]{1,0:T(2,128)}, u32[]{:S(2)}) copy-start(s32[2,64]{1,0:T(2,128)} %param.14) | copy-start | bytes 1540
  6.5 28.2 %copy-start.9 = (s32[2]{0:T(128)S(1)}, s32[2]{0:T(128)}, u32[]{:S(2)}) copy-start(s32[2]{0:T(128)} %param.15) | copy-start | bytes 28
  6.5 76.4 %all-gather.8.cloned.1.call-start = ((), (), s32[]{:S(2)}) async-start(), calls=%async_computation | async-start | bytes 1392640 | tf_op jit(solution)/shard_map/all_gather | solution.py:48
  8.1 170.6 %all-gather.10.cloned.1.call-start = ((), (), s32[]{:S(2)}) async-start(), calls=%async_computation.1 | async-start | bytes 1310720 | tf_op jit(solution)/shard_map/all_gather | solution.py:150
  10.6 65.4 %copy-start.8 = (bf16[640]{0:T(1024)(128)(2,1)S(1)}, bf16[640]{0:T(1024)(128)(2,1)}, u32[]{:S(2)}) copy-start(bf16[640]{0:T(1024)(128)(2,1)} %param.25) | copy-start | bytes 3844
  10.6 67.5 %collective-permute-start = (bf16[3,3,1,1,80,640]{5,4,3,2,1,0:T(8,128)(2,1)S(1)}, bf16[3,3,1,1,80,640]{5,4,3,2,1,0:T(8,128)(2,1)}, u32[]{:S(2)}, u32[]{:S(2)}) collective-permute-start(bf16[3,3,1,1,80,640]{5,4,3,2,1,0:T(8,128)(2,1)S(1)} %fusion.11), channel_id=1, source_target_pairs={{0,4},{4,0},{1,5},{5,1},{2,6},{6,2},{3,7},{7,3},{8,12},{12,8},{9,1... | collective-permute-start | bytes 2764808 | tf_op jit(solution)/shard_map/ppermute | solution.py:36
  17.2 59.0 %collective-permute-start.2 = (bf16[320,128]{1,0:T(8,128)(2,1)S(1)}, bf16[320,128]{1,0:T(8,128)(2,1)S(1)}, u32[]{:S(2)}, u32[]{:S(2)}) collective-permute-start(bf16[320,128]{1,0:T(8,128)(2,1)S(1)} %fusion.69), channel_id=1, source_target_pairs={{0,4},{4,0},{1,5},{5,1},{2,6},{6,2},{3,7},{7,3},{8,12},{12,8},{9,1... | collective-permute-start | bytes 245768 | tf_op jit(solution)/shard_map/ppermute | solution.py:36
  20.4 56.5 %collective-permute-start.3 = (bf16[320,2,128]{2,1,0:T(2,128)(2,1)S(1)}, bf16[320,2,128]{2,1,0:T(2,128)(2,1)S(1)}, u32[]{:S(2)}, u32[]{:S(2)}) collective-permute-start(bf16[320,2,128]{2,1,0:T(2,128)(2,1)S(1)} %fusion.38), channel_id=1, source_target_pairs={{0,4},{4,0},{1,5},{5,1},{2,6},{6,2},{3,7},{7,3},{8,12},{12,8},{9,1... | collective-permute-start | bytes 491528 | tf_op jit(solution)/shard_map/ppermute | solution.py:36
  26.9 119.4 %collective-permute-start.1 = (bf16[160,256]{1,0:T(8,128)(2,1)}, bf16[160,256]{1,0:T(8,128)(2,1)}, u32[]{:S(2)}, u32[]{:S(2)}) collective-permute-start(bf16[160,256]{1,0:T(8,128)(2,1)} %fusion.67), channel_id=1, source_target_pairs={{0,4},{4,0},{1,5},{5,1},{2,6},{6,2},{3,7},{7,3},{8,12},{12,8},{9,1... | collective-permute-start | bytes 245768 | tf_op jit(solution)/shard_map/ppermute | solution.py:36
  75.1 0.9 copy-start.2
  76.9 2.8 %copy-start.3 = (bf16[4,640,1,8,17]{1,3,4,0,2:T(8,128)(2,1)S(1)}, bf16[4,640,1,8,17]{1,3,4,0,2:T(8,128)(2,1)}, u32[]{:S(2)}) copy-start(bf16[4,640,1,8,17]{1,3,4,0,2:T(8,128)(2,1)} %copy-done.2) | copy-start | bytes 2088964
  76.9 2.8 %copy-start.10 = (pred[8,17]{0,1:T(8,128)(4,1)S(1)}, pred[8,17]{0,1:T(8,128)(4,1)}, u32[]{:S(2)}) copy-start(pred[8,17]{0,1:T(8,128)(4,1)} %constant.308) | copy-start | bytes 412
  83.0 28.0 %copy-start.4 = (bf16[1,3,1,2,80,640]{5,4,3,2,1,0:T(8,128)(2,1)S(1)}, bf16[1,3,1,2,80,640]{5,4,3,2,1,0:T(8,128)(2,1)}, u32[]{:S(2)}) copy-start(bf16[1,3,1,2,80,640]{5,4,3,2,1,0:T(8,128)(2,1)} %get-tuple-element.22) | copy-start | bytes 1843204
  111.0 8.6 %copy-start.1 = (bf16[640,2,128]{2,1,0:T(2,128)(2,1)S(1)}, bf16[640,2,128]{2,1,0:T(2,128)(2,1)}, u32[]{:S(2)}) copy-start(bf16[640,2,128]{2,1,0:T(2,128)(2,1)} %pad_maximum_fusion.1) | copy-start | bytes 983044
  112.8 51.0 %copy-start.5 = (bf16[320,128]{1,0:T(8,128)(2,1)S(1)}, bf16[320,128]{1,0:T(8,128)(2,1)}, u32[]{:S(2)}) copy-start(bf16[320,128]{1,0:T(8,128)(2,1)} %get-tuple-element.40) | copy-start | bytes 245764
  112.8 51.0 %copy-start.6 = (bf16[320,128]{1,0:T(8,128)(2,1)S(1)}, bf16[320,128]{1,0:T(8,128)(2,1)}, u32[]{:S(2)}) copy-start(bf16[320,128]{1,0:T(8,128)(2,1)} %get-tuple-element.41) | copy-start | bytes 245764
Sparse Core Ops, SparseCore 0:
  9.4 67.9 all-gather.7
  146.4 32.1 all-gather.9

commit v12 on v10

--- a/solution.py
+++ b/solution.py
@@ -182,11 +182,15 @@
     totals = jnp.stack(total_list, axis=1)
     accum = jnp.stack(accum_list, axis=1)
     attended = (accum / totals[..., None]).astype(jnp.bfloat16).reshape(cells, att_shard)
-    attended_full = lax.all_gather(attended, "tensor", axis=1, tiled=True)
-    projected = lax.dot_general(
-        out_w, attended_full, (((1,), (1,)), ((), ())), preferred_element_type=jnp.float32
-    )
-    projected = jnp.transpose(projected.reshape(chan_shard, tile_rows, tile_cols), (1, 0, 2))
+    attended_stack = lax.all_gather(
+        attended.reshape(tile_rows, tile_cols, att_shard), "tensor", axis=0, tiled=False
+    )
+    projected = jnp.einsum(
+        "okj,krwj->row",
+        out_w.reshape(chan_shard, -1, att_shard),
+        attended_stack,
+        preferred_element_type=jnp.float32,
+    )
     final = (section_r + projected) * live_flag
     return final.astype(jnp.bfloat16).reshape(1, tile_rows, chan_shard, tile_cols)
 

time: 202 us -> 203 us (level)
  other arithmetic: 18.9 us -> 16.8 us
  transfers between devices with their start and end apart: 9 -> 9, of which waited for: 2 -> 2; matrix products, arithmetic and copies ran while one was open for 12% -> 9% of each run, Pallas kernels for 0% -> 0%
where the time goes in v12:
time: 203 us; the launch traced here: 202 us
  blocking collectives  83.3 us (41%)
  between operations  42.3 us (21%)
  starting transfers between devices  24.7 us (12%)
  other arithmetic  16.8 us (8%)
  waiting for transfers between devices  16.4 us (8%)
  local copies, waits for them, and re-layouts  9.27 us (5%)
  matrix products  8.84 us (4%)
    all_gather x1, blocking collectives, on_device(): kv_column = lax.all_gather(kv_local, 'tz', axis=0, tiled=False)  25.6 us
    all_gather x1, waiting for transfers between devices, on_device(): kv_all = lax.all_gather(kv_column, 'tx', axis=0, tiled=False)  15.1 us
    all_gather x1, blocking collectives, on_device(): section_full = lax.all_gather(section, 'tensor', axis=1, tiled=True)  15 us
    ppermute x4, starting transfers between devices, image_pair(): other = lax.ppermute(part, 'image', [(0, 1), (1, 0)])  14.4 us
    all_gather x1, blocking collectives, on_device(): lax.all_gather(jnp.stack([upper, lower]), 'tensor', axis=1, tiled=True)  14 us
    all_gather x1, blocking collectives, on_device(): block_full = lax.all_gather(activated, 'tensor', axis=1, tiled=True)  13.9 us
    ppermute x3, starting transfers between devices, halo_rows(): lax.ppermute(chunk, 'tx', [(i, (i + shift) % n_x) for i in range(n_x)])  10.3 us
    all_gather x1, blocking collectives, on_device(): lax.all_gather(attended.reshape(tile_rows, tile_cols, att_shard), 'tensor...  8.56 us
  transfers between devices with their start and end apart: 9, of which 2 were waited for; matrix products, arithmetic and copies ran while one was open for 9% of the time, Pallas kernels for 0%

profile of v12, /device:TPU:1, one launch (start us, length us, event | category | flops | bytes accessed | tf_op | source)
XLA Modules:
  0.0 201.6 jit_solution(12034732506798984949)
XLA Ops:
  8.8 1.8 fusion.11
  10.6 5.7 %collective-permute-start = (bf16[3,3,1,1,80,640]{5,4,3,2,1,0:T(8,128)(2,1)S(1)}, bf16[3,3,1,1,80,640]{5,4,3,2,1,0:T(8,128)(2,1)}, u32[]{:S(2)}, u32[]{:S(2)}) collective-permute-start(bf16[3,3,1,1,80,640]{5,4,3,2,1,0:T(8,128)(2,1)S(1)} %fusion.11), channel_id=1, source_target_pairs={{0,4},{4,0},{1,5},{5,1},{2,6},{6,2},{3,7},{7,3},{8,12},{12,8},{9,1... | collective-permute-start | bytes 2764808 | tf_op jit(solution)/shard_map/ppermute | solution.py:36
  16.2 1.0 fusion.67
  17.2 1.9 collective-permute-start.4
  19.1 1.3 fusion.41
  20.4 4.9 %collective-permute-start.5 = (bf16[320,2,128]{2,1,0:T(2,128)(2,1)S(1)}, bf16[320,2,128]{2,1,0:T(2,128)(2,1)S(1)}, u32[]{:S(2)}, u32[]{:S(2)}) collective-permute-start(bf16[320,2,128]{2,1,0:T(2,128)(2,1)S(1)} %fusion.41), channel_id=1, source_target_pairs={{0,4},{4,0},{1,5},{5,1},{2,6},{6,2},{3,7},{7,3},{8,12},{12,8},{9,1... | collective-permute-start | bytes 491528 | tf_op jit(solution)/shard_map/ppermute | solution.py:36
  25.3 1.0 fusion.69
  26.2 1.9 collective-permute-start.6
  35.6 13.9 %all_gather.33 = bf16[4,640,128]{2,1,0:T(8,128)(2,1)S(1)} all-gather(bf16[4,160,128]{2,1,0:T(8,128)(2,1)S(1)} %fusion.45), channel_id=1, replica_groups=mesh['tz'=16,'tx'=4,'image'=2,'tensor'=4] {'tensor'}, dimensions={1}, use_global_device_ids=true | all-gather | bytes 819200 | tf_op jit(solution)/shard_map/all_gather | solution.py:118
  74.0 0.9 copy-done.3
  76.9 1.4 broadcast_select_fusion
  78.5 1.8 convolution_select_fusion
  80.9 1.0 fusion.95
  81.9 2.8 %collective-permute-start.1 = (bf16[2,160,128]{2,1,0:T(8,128)(2,1)S(1)}, bf16[2,160,128]{2,1,0:T(8,128)(2,1)S(1)}, u32[]{:S(2)}, u32[]{:S(2)}) collective-permute-start(bf16[2,160,128]{2,1,0:T(8,128)(2,1)S(1)} %pad_maximum_fusion.3), channel_id=1, source_target_pairs={{0,8},{8,16},{16,24},{24,0},{1,9},{9,17},{17,25},{25,1},{2,10},{10... | collective-permute-start | bytes 245768 | tf_op jit(solution)/shard_map/ppermute | solution.py:61
  84.8 4.4 %collective-permute-start.2 = (bf16[2,160,128]{2,1,0:T(8,128)(2,1)S(1)}, bf16[2,160,128]{2,1,0:T(8,128)(2,1)S(1)}, u32[]{:S(2)}, u32[]{:S(2)}) collective-permute-start(bf16[2,160,128]{2,1,0:T(8,128)(2,1)S(1)} %pad_maximum_fusion.4), channel_id=1, source_target_pairs={{0,16},{8,24},{16,0},{24,8},{1,17},{9,25},{17,1},{25,9},{2,18},{10... | collective-permute-start | bytes 245768 | tf_op jit(solution)/shard_map/ppermute | solution.py:61
  89.1 3.1 %collective-permute-start.3 = (bf16[2,160,128]{2,1,0:T(8,128)(2,1)S(1)}, bf16[2,160,128]{2,1,0:T(8,128)(2,1)S(1)}, u32[]{:S(2)}, u32[]{:S(2)}) collective-permute-start(bf16[2,160,128]{2,1,0:T(8,128)(2,1)S(1)} %pad_maximum_fusion.5), channel_id=1, source_target_pairs={{0,24},{8,0},{16,8},{24,16},{1,25},{9,1},{17,9},{25,17},{2,26},{10... | collective-permute-start | bytes 245768 | tf_op jit(solution)/shard_map/ppermute | solution.py:61
  92.2 1.2 fusion.32
  93.4 1.2 collective-permute-done.3
  94.6 0.9 fusion.87
  95.6 14.0 %all_gather.36 = bf16[2,640,128]{2,0,1:T(2,128)(2,1)S(1)} all-gather(bf16[2,160,128]{2,0,1:T(2,128)(2,1)S(1)} %copy.172), channel_id=1, replica_groups=mesh['tz'=16,'tx'=4,'image'=2,'tensor'=4] {'tensor'}, dimensions={1}, use_global_device_ids=true | all-gather | bytes 409600 | tf_op jit(solution)/shard_map/all_gather | solution.py:120
  112.6 6.2 %all-gather.1 = bf16[1,32,640]{1,0,2:T(2,128)(2,1)S(1)} all-gather(bf16[1,32,160]{1,0,2:T(2,128)(2,1)S(1)} %copy.187), channel_id=3, replica_groups=mesh['tz'=16,'tx'=4,'image'=2,'tensor'=4] {'tensor'}, dimensions={2}, use_global_device_ids=true | all-gather | bytes 51200 | tf_op jit(solution)/shard_map/all_gather | solution.py:144
  119.1 25.6 %all-gather.2 = bf16[512,256]{1,0:T(8,128)(2,1)} all-gather(bf16[32,256]{1,0:T(8,128)(2,1)S(1)} %convolution_convert_fusion), channel_id=4, replica_groups=mesh['tz'=16,'tx'=4,'image'=2,'tensor'=4] {'tz'}, dimensions={0}, use_global_device_ids=true | all-gather | bytes 278528 | tf_op jit(solution)/shard_map/all_gather | solution.py:147
  144.9 15.0 %all_gather.37 = bf16[4,640,128]{2,1,0:T(8,128)(2,1)S(1)} all-gather(bf16[4,160,128]{2,1,0:T(8,128)(2,1)S(1)} %fusion.119), channel_id=1, replica_groups=mesh['tz'=16,'tx'=4,'image'=2,'tensor'=4] {'tensor'}, dimensions={1}, use_global_device_ids=true | all-gather | bytes 819200 | tf_op jit(solution)/shard_map/all_gather | solution.py:127
  160.7 1.3 fusion.18
  162.0 15.1 %all-gather.9.cloned.1.call-done = bf16[64,32,256]{2,1,0:T(8,128)(2,1)} async-done(((bf16[16,32,256]{2,1,0:T(8,128)(2,1)}), bf16[64,32,256]{2,1,0:T(8,128)(2,1)}) %all-gather.9.cloned.1.call-update) | async-done | bytes 1048592 | tf_op jit(solution)/shard_map/all_gather | solution.py:148
  177.1 1.3 fusion.122
  179.6 1.1 select_reduce_fusion.1
  180.6 2.1 %fusion = (f32[512]{0:T(512)S(1)}, f32[512]{0:T(512)S(1)}) fusion(f32[512,2048]{1,0:T(8,128)S(1)} %get-tuple-element.48, f32[2048]{0:T(1024)S(1)} %get-tuple-element.17, f32[512]{0:T(512)S(1)} %get-tuple-element.7, pred[2048]{0:T(1024)(128)(4,1)S(1)} %get-tuple-element.18, f32[512]{0:T(512)S(1)} %get-tuple-element.8, f32[512,2048]{1,0:T(8,128)S(1)} %fusion.51), kind=kLoop, calls=%fused_computation.4 | loop fusion | flops 8387584 | bytes 8407040 | tf_op jit(solution)/shard_map/reduce_sum | solution.py:174
  182.8 1.0 fusion.20
  183.9 1.0 fusion.23
  185.1 8.6 %all_gather.43 = bf16[4,4,128,128]{3,2,0,1:T(8,128)(2,1)S(1)} all-gather(bf16[1,4,128,128]{3,2,0,1:T(8,128)(2,1)S(1)} %copy.191), channel_id=1, replica_groups=mesh['tz'=16,'tx'=4,'image'=2,'tensor'=4] {'tensor'}, dimensions={0}, use_global_device_ids=true | all-gather | bytes 655360 | tf_op jit(solution)/shard_map/all_gather | solution.py:185
  193.7 1.0 fusion.19
  (113 shorter events, 14.1 us)
Async XLA Ops:
  6.5 29.0 %copy-start.2 = (bf16[1,4,160,128]{3,2,1,0:T(8,128)(2,1)S(1)}, bf16[1,4,160,128]{3,2,1,0:T(8,128)(2,1)}, u32[]{:S(2)}) copy-start(bf16[1,4,160,128]{3,2,1,0:T(8,128)(2,1)} %param.13) | copy-start | bytes 491524
  6.5 21.7 %copy-start.11 = (s32[2,64]{1,0:T(2,128)S(1)}, s32[2,64]{1,0:T(2,128)}, u32[]{:S(2)}) copy-start(s32[2,64]{1,0:T(2,128)} %param.14) | copy-start | bytes 1540
  6.5 27.2 %copy-start.13 = (s32[2]{0:T(128)S(1)}, s32[2]{0:T(128)}, u32[]{:S(2)}) copy-start(s32[2]{0:T(128)} %param.15) | copy-start | bytes 28
  6.5 74.3 %all-gather.7.cloned.1.call-start = ((), (), s32[]{:S(2)}) async-start(), calls=%async_computation | async-start | bytes 1392640 | tf_op jit(solution)/shard_map/all_gather | solution.py:48
  8.1 169.1 %all-gather.9.cloned.1.call-start = ((), (), s32[]{:S(2)}) async-start(), calls=%async_computation.1 | async-start | bytes 1310720 | tf_op jit(solution)/shard_map/all_gather | solution.py:148
  10.6 64.3 %copy-start.12 = (bf16[640]{0:T(1024)(128)(2,1)S(1)}, bf16[640]{0:T(1024)(128)(2,1)}, u32[]{:S(2)}) copy-start(bf16[640]{0:T(1024)(128)(2,1)} %param.25) | copy-start | bytes 3844
  10.6 66.3 %collective-permute-start = (bf16[3,3,1,1,80,640]{5,4,3,2,1,0:T(8,128)(2,1)S(1)}, bf16[3,3,1,1,80,640]{5,4,3,2,1,0:T(8,128)(2,1)}, u32[]{:S(2)}, u32[]{:S(2)}) collective-permute-start(bf16[3,3,1,1,80,640]{5,4,3,2,1,0:T(8,128)(2,1)S(1)} %fusion.11), channel_id=1, source_target_pairs={{0,4},{4,0},{1,5},{5,1},{2,6},{6,2},{3,7},{7,3},{8,12},{12,8},{9,1... | collective-permute-start | bytes 2764808 | tf_op jit(solution)/shard_map/ppermute | solution.py:36
  17.2 57.8 %collective-permute-start.4 = (bf16[320,128]{1,0:T(8,128)(2,1)S(1)}, bf16[320,128]{1,0:T(8,128)(2,1)S(1)}, u32[]{:S(2)}, u32[]{:S(2)}) collective-permute-start(bf16[320,128]{1,0:T(8,128)(2,1)S(1)} %fusion.67), channel_id=1, source_target_pairs={{0,4},{4,0},{1,5},{5,1},{2,6},{6,2},{3,7},{7,3},{8,12},{12,8},{9,1... | collective-permute-start | bytes 245768 | tf_op jit(solution)/shard_map/ppermute | solution.py:36
  20.4 56.0 %collective-permute-start.5 = (bf16[320,2,128]{2,1,0:T(2,128)(2,1)S(1)}, bf16[320,2,128]{2,1,0:T(2,128)(2,1)S(1)}, u32[]{:S(2)}, u32[]{:S(2)}) collective-permute-start(bf16[320,2,128]{2,1,0:T(2,128)(2,1)S(1)} %fusion.41), channel_id=1, source_target_pairs={{0,4},{4,0},{1,5},{5,1},{2,6},{6,2},{3,7},{7,3},{8,12},{12,8},{9,1... | collective-permute-start | bytes 491528 | tf_op jit(solution)/shard_map/ppermute | solution.py:36
  26.2 49.5 %collective-permute-start.6 = (bf16[160,256]{1,0:T(8,128)(2,1)S(1)}, bf16[160,256]{1,0:T(8,128)(2,1)S(1)}, u32[]{:S(2)}, u32[]{:S(2)}) collective-permute-start(bf16[160,256]{1,0:T(8,128)(2,1)S(1)} %fusion.69), channel_id=1, source_target_pairs={{0,4},{4,0},{1,5},{5,1},{2,6},{6,2},{3,7},{7,3},{8,12},{12,8},{9,1... | collective-permute-start | bytes 245768 | tf_op jit(solution)/shard_map/ppermute | solution.py:36
  74.0 0.9 copy-start.3
  76.4 2.1 %copy-start.4 = (bf16[4,640,1,8,17]{1,3,4,0,2:T(8,128)(2,1)S(1)}, bf16[4,640,1,8,17]{1,3,4,0,2:T(8,128)(2,1)}, u32[]{:S(2)}) copy-start(bf16[4,640,1,8,17]{1,3,4,0,2:T(8,128)(2,1)} %copy-done.3) | copy-start | bytes 2088964
  76.4 2.1 %copy-start.14 = (pred[8,17]{0,1:T(8,128)(4,1)S(1)}, pred[8,17]{0,1:T(8,128)(4,1)}, u32[]{:S(2)}) copy-start(pred[8,17]{0,1:T(8,128)(4,1)} %constant.283) | copy-start | bytes 412
  80.8 63.9 %copy-start = (f32[4,1,128,160]{2,3,0,1:T(8,128)}, f32[4,1,128,160]{2,3,0,1:T(8,128)S(1)}, u32[]{:S(2)}) copy-start(f32[4,1,128,160]{2,3,0,1:T(8,128)S(1)} %copy.194) | copy-start | bytes 983044
  81.9 11.5 %collective-permute-start.1 = (bf16[2,160,128]{2,1,0:T(8,128)(2,1)S(1)}, bf16[2,160,128]{2,1,0:T(8,128)(2,1)S(1)}, u32[]{:S(2)}, u32[]{:S(2)}) collective-permute-start(bf16[2,160,128]{2,1,0:T(8,128)(2,1)S(1)} %pad_maximum_fusion.3), channel_id=1, source_target_pairs={{0,8},{8,16},{16,24},{24,0},{1,9},{9,17},{17,25},{25,1},{2,10},{10... | collective-permute-start | bytes 245768 | tf_op jit(solution)/shard_map/ppermute | solution.py:61
  84.8 8.6 %collective-permute-start.2 = (bf16[2,160,128]{2,1,0:T(8,128)(2,1)S(1)}, bf16[2,160,128]{2,1,0:T(8,128)(2,1)S(1)}, u32[]{:S(2)}, u32[]{:S(2)}) collective-permute-start(bf16[2,160,128]{2,1,0:T(8,128)(2,1)S(1)} %pad_maximum_fusion.4), channel_id=1, source_target_pairs={{0,16},{8,24},{16,0},{24,8},{1,17},{9,25},{17,1},{25,9},{2,18},{10... | collective-permute-start | bytes 245768 | tf_op jit(solution)/shard_map/ppermute | solution.py:61
  89.1 5.5 %collective-permute-start.3 = (bf16[2,160,128]{2,1,0:T(8,128)(2,1)S(1)}, bf16[2,160,128]{2,1,0:T(8,128)(2,1)S(1)}, u32[]{:S(2)}, u32[]{:S(2)}) collective-permute-start(bf16[2,160,128]{2,1,0:T(8,128)(2,1)S(1)} %pad_maximum_fusion.5), channel_id=1, source_target_pairs={{0,24},{8,0},{16,8},{24,16},{1,25},{9,1},{17,9},{25,17},{2,26},{10... | collective-permute-start | bytes 245768 | tf_op jit(solution)/shard_map/ppermute | solution.py:61
  93.4 17.1 %copy-start.8 = (bf16[1,3,1,2,80,640]{5,4,3,2,1,0:T(8,128)(2,1)S(1)}, bf16[1,3,1,2,80,640]{5,4,3,2,1,0:T(8,128)(2,1)}, u32[]{:S(2)}) copy-start(bf16[1,3,1,2,80,640]{5,4,3,2,1,0:T(8,128)(2,1)} %get-tuple-element.20) | copy-start | bytes 1843204
  95.5 15.9 %copy-start.7 = (bf16[1,3,1,2,80,640]{5,4,3,2,1,0:T(8,128)(2,1)S(1)}, bf16[1,3,1,2,80,640]{5,4,3,2,1,0:T(8,128)(2,1)}, u32[]{:S(2)}) copy-start(bf16[1,3,1,2,80,640]{5,4,3,2,1,0:T(8,128)(2,1)} %get-tuple-element.21) | copy-start | bytes 1843204
  112.1 32.8 %copy-start.5 = (f32[1,1,128,160]{2,3,0,1:T(8,128)}, f32[1,1,128,160]{2,3,0,1:T(8,128)S(1)}, u32[]{:S(2)}) copy-start(f32[1,1,128,160]{2,3,0,1:T(8,128)S(1)} %copy.198) | copy-start | bytes 245764
  183.8 9.9 %copy-start.1 = (f32[4,1,128,160]{2,3,0,1:T(8,128)S(1)}, f32[4,1,128,160]{2,3,0,1:T(8,128)}, u32[]{:S(2)}) copy-start(f32[4,1,128,160]{2,3,0,1:T(8,128)} %copy-done) | copy-start | bytes 983044
  183.8 9.9 %copy-start.6 = (f32[1,1,128,160]{2,3,0,1:T(8,128)S(1)}, f32[1,1,128,160]{2,3,0,1:T(8,128)}, u32[]{:S(2)}) copy-start(f32[1,1,128,160]{2,3,0,1:T(8,128)} %copy-done.5) | copy-start | bytes 245764
  183.8 9.9 %copy-start.9 = (bf16[160,256]{1,0:T(8,128)(2,1)S(1)}, bf16[160,256]{1,0:T(8,128)(2,1)}, u32[]{:S(2)}) copy-start(bf16[160,256]{1,0:T(8,128)(2,1)} %get-tuple-element.38) | copy-start | bytes 245764
  183.9 9.9 %copy-start.10 = (bf16[160,256]{1,0:T(8,128)(2,1)S(1)}, bf16[160,256]{1,0:T(8,128)(2,1)}, u32[]{:S(2)}) copy-start(bf16[160,256]{1,0:T(8,128)(2,1)} %get-tuple-element.39) | copy-start | bytes 245764
Sparse Core Ops, SparseCore 0:
  9.4 68.5 all-gather.6
  144.8 32.2 all-gather.8

commit v13 on v10

--- a/solution.py
+++ b/solution.py
@@ -117,9 +117,18 @@
     lower = jnp.where(has_lower, lower, jnp.zeros_like(lower))
     block_full = lax.all_gather(activated, "tensor", axis=1, tiled=True)
     conv_inner = convolve(block_full, conv_w, (1, 1))
-    halo_full = lax.all_gather(jnp.stack([upper, lower]), "tensor", axis=1, tiled=True)
-    up_term = convolve(halo_full[0:1], conv_w[0:1], (0, 0))
-    down_term = convolve(halo_full[1:2], conv_w[2:3], (0, 0))
+    halo_stack = lax.all_gather(jnp.stack([upper, lower]), "tensor", axis=0, tiled=False)
+    w_halo = conv_w[0::2].reshape(2, 3, chan_shard, halo_stack.shape[0], halo_stack.shape[2])
+    taps = jnp.einsum(
+        "sbokc,kscw->sbow", w_halo, halo_stack, preferred_element_type=jnp.float32
+    )
+    edge = jnp.zeros(taps.shape[:1] + taps.shape[2:3] + (1,), jnp.float32)
+    halo_terms = (
+        jnp.concatenate([edge, taps[:, 0, :, :-1]], axis=-1)
+        + taps[:, 1]
+        + jnp.concatenate([taps[:, 2, :, 1:], edge], axis=-1)
+    )
+    up_term, down_term = halo_terms[0:1], halo_terms[1:2]
     middle = jnp.zeros((tile_rows - 2,) + up_term.shape[1:], jnp.float32)
     conv_out = conv_inner + jnp.concatenate([up_term, middle, down_term], axis=0)
     section_r = lax.reduce_precision(feats.astype(jnp.float32) + conv_out, exponent_bits=8, mantissa_bits=7)

time: 202 us -> 206 us (1.020)
  waiting for transfers between devices: 15.8 us -> 13 us
  matrix products: 7.17 us -> 9.4 us
    reshape x0 -> x1, local copies, waits for them, and re-layouts: none -> 2.6 us  [on_device(): conv_w[0::2]]
    dot_general x0 -> x1, matrix products: none -> 2.13 us  [on_device(): jnp.einsum('sbokc,kscw->sbow', w_halo, halo_stack, preferred_element_type...]
  transfers between devices with their start and end apart: 9 -> 9, of which waited for: 2 -> 1; matrix products, arithmetic and copies ran while one was open for 12% -> 15% of each run, Pallas kernels for 0% -> 0%
where the time goes in v13:
time: 206 us; the launch traced here: 205 us
  blocking collectives  84.1 us (41%)
  between operations  42.4 us (21%)
  starting transfers between devices  24.7 us (12%)
  other arithmetic  19.6 us (10%)
  waiting for transfers between devices  13 us (6%)
  local copies, waits for them, and re-layouts  11.8 us (6%)
  matrix products  9.4 us (5%)
    all_gather x1, blocking collectives, on_device(): kv_column = lax.all_gather(kv_local, 'tz', axis=0, tiled=False)  25 us
    all_gather x1, blocking collectives, on_device(): lax.all_gather(jnp.stack([upper, lower]), 'tensor', axis=0, tiled=False)  15.2 us
    all_gather x1, blocking collectives, on_device(): section_full = lax.all_gather(section, 'tensor', axis=1, tiled=True)  15.2 us
    ppermute x4, starting transfers between devices, image_pair(): other = lax.ppermute(part, 'image', [(0, 1), (1, 0)])  14.4 us
    all_gather x1, blocking collectives, on_device(): block_full = lax.all_gather(activated, 'tensor', axis=1, tiled=True)  13.9 us
    all_gather x1, waiting for transfers between devices, on_device(): kv_all = lax.all_gather(kv_column, 'tx', axis=0, tiled=False)  12.9 us
    ppermute x3, starting transfers between devices, halo_rows(): lax.ppermute(chunk, 'tx', [(i, (i + shift) % n_x) for i in range(n_x)])  10.3 us
    all_gather x1, blocking collectives, on_device(): attended_full = lax.all_gather(attended, 'tensor', axis=1, tiled=True)  8.57 us
  transfers between devices with their start and end apart: 9, of which 1 were waited for; matrix products, arithmetic and copies ran while one was open for 15% of the time, Pallas kernels for 0%

profile of v13, /device:TPU:1, one launch (start us, length us, event | category | flops | bytes accessed | tf_op | source)
XLA Modules:
  0.0 205.0 jit_solution(295922575203560631)
XLA Ops:
  8.8 1.8 fusion.13
  10.6 5.7 %collective-permute-start = (bf16[3,3,1,1,80,640]{5,4,3,2,1,0:T(8,128)(2,1)S(1)}, bf16[3,3,1,1,80,640]{5,4,3,2,1,0:T(8,128)(2,1)}, u32[]{:S(2)}, u32[]{:S(2)}) collective-permute-start(bf16[3,3,1,1,80,640]{5,4,3,2,1,0:T(8,128)(2,1)S(1)} %fusion.13), channel_id=1, source_target_pairs={{0,4},{4,0},{1,5},{5,1},{2,6},{6,2},{3,7},{7,3},{8,12},{12,8},{9,1... | collective-permute-start | bytes 2764808 | tf_op jit(solution)/shard_map/ppermute | solution.py:36
  16.2 1.0 fusion.60
  17.2 1.9 collective-permute-start.5
  19.1 1.3 fusion.39
  20.4 4.9 %collective-permute-start.6 = (bf16[320,2,128]{2,1,0:T(2,128)(2,1)S(1)}, bf16[320,2,128]{2,1,0:T(2,128)(2,1)}, u32[]{:S(2)}, u32[]{:S(2)}) collective-permute-start(bf16[320,2,128]{2,1,0:T(2,128)(2,1)S(1)} %fusion.39), channel_id=1, source_target_pairs={{0,4},{4,0},{1,5},{5,1},{2,6},{6,2},{3,7},{7,3},{8,12},{12,8},{9,1... | collective-permute-start | bytes 491528 | tf_op jit(solution)/shard_map/ppermute | solution.py:36
  25.3 1.0 fusion.58
  26.2 1.9 collective-permute-start.4
  35.6 13.9 %all_gather.36 = bf16[4,640,128]{2,0,1:T(4,128)(2,1)S(1)} all-gather(bf16[4,160,128]{2,0,1:T(4,128)(2,1)S(1)} %copy.204), channel_id=1, replica_groups=mesh['tz'=16,'tx'=4,'image'=2,'tensor'=4] {'tensor'}, dimensions={1}, use_global_device_ids=true | all-gather | bytes 819200 | tf_op jit(solution)/shard_map/all_gather | solution.py:118
  73.2 1.0 copy.233
  75.3 0.9 broadcast_select_fusion.3
  76.2 1.2 pad_maximum_fusion.1
  77.4 1.4 broadcast_select_fusion.1
  80.6 2.9 %collective-permute-start.1 = (bf16[2,160,128]{2,1,0:T(8,128)(2,1)}, bf16[2,160,128]{2,1,0:T(8,128)(2,1)}, u32[]{:S(2)}, u32[]{:S(2)}) collective-permute-start(bf16[2,160,128]{2,1,0:T(8,128)(2,1)} %pad_maximum_fusion.3), channel_id=1, source_target_pairs={{0,8},{8,16},{16,24},{24,0},{1,9},{9,17},{17,25},{25,1},{2,10},{10... | collective-permute-start | bytes 245768 | tf_op jit(solution)/shard_map/ppermute | solution.py:61
  84.1 4.3 %collective-permute-start.2 = (bf16[2,160,128]{2,1,0:T(8,128)(2,1)}, bf16[2,160,128]{2,1,0:T(8,128)(2,1)}, u32[]{:S(2)}, u32[]{:S(2)}) collective-permute-start(bf16[2,160,128]{2,1,0:T(8,128)(2,1)} %pad_maximum_fusion.4), channel_id=1, source_target_pairs={{0,16},{8,24},{16,0},{24,8},{1,17},{9,25},{17,1},{25,9},{2,18},{10... | collective-permute-start | bytes 245768 | tf_op jit(solution)/shard_map/ppermute | solution.py:61
  89.1 3.0 %collective-permute-start.3 = (bf16[2,160,128]{2,1,0:T(8,128)(2,1)}, bf16[2,160,128]{2,1,0:T(8,128)(2,1)}, u32[]{:S(2)}, u32[]{:S(2)}) collective-permute-start(bf16[2,160,128]{2,1,0:T(8,128)(2,1)} %pad_maximum_fusion.5), channel_id=1, source_target_pairs={{0,24},{8,0},{16,8},{24,16},{1,25},{9,1},{17,9},{25,17},{2,26},{10... | collective-permute-start | bytes 245768 | tf_op jit(solution)/shard_map/ppermute | solution.py:61
  92.2 2.6 %convolution_select_fusion = f32[4,8,17,160]{3,1,2,0:T(8,128)} fusion(bf16[3,3,160,640]{3,2,1,0:T(8,128)(2,1)S(1)} %bitcast.184, bf16[4,640,1,7,2]{1,3,4,0,2:T(8,128)(2,1)S(1)} %copy-done.2, bf16[4,640,1,8,17]{1,3,4,0,2:T(8,128)(2,1)S(1)} %copy.207, pred[8,17]{0,1:T(8,128)(4,1)S(1)} %copy-done.6), kind=kOutput, calls=%fused_computation.27 | convolution fusion | flops 838005760 | bytes 2959496 | tf_op jit(solution)/shard_map/conv_general_dilated | solution.py:19
  95.0 2.6 %reshape.238 = bf16[2,3,160,4,160]{4,3,2,1,0:T(4,128)(2,1)} reshape(bf16[2,3,160,640]{3,2,1,0:T(8,128)(2,1)S(1)} %slice.104) | data formatting | bytes 2457600 | tf_op jit(solution)/shard_map/reshape | solution.py:121
  97.6 1.3 copy.208
  99.1 1.0 fusion.81
  100.2 15.2 %all-gather.1 = bf16[8,160,128]{2,1,0:T(8,128)(2,1)S(1)} all-gather(bf16[2,160,128]{2,1,0:T(8,128)(2,1)S(1)} %pad_maximum_fusion.6), channel_id=3, replica_groups=mesh['tz'=16,'tx'=4,'image'=2,'tensor'=4] {'tensor'}, dimensions={0}, use_global_device_ids=true | all-gather | bytes 409600 | tf_op jit(solution)/shard_map/all_gather | solution.py:120
  115.4 2.1 %fusion.18 = f32[2,3,160,128]{3,2,0,1:T(8,128)S(1)} fusion(bf16[2,3,160,4,160]{4,3,2,1,0:T(4,128)(2,1)} %reshape.238, bf16[4,2,160,128]{3,2,1,0:T(8,128)(2,1)S(1)} %bitcast.200), kind=kOutput, calls=%fused_computation.26 | convolution fusion | flops 157286400 | bytes 2048000 | tf_op jit(solution)/shard_map/sbokc,kscw->sbow/dot_general | solution.py:122
  118.3 6.2 %all-gather.2 = bf16[1,32,640]{1,0,2:T(2,128)(2,1)S(1)} all-gather(bf16[1,32,160]{1,0,2:T(2,128)(2,1)S(1)} %copy.220), channel_id=4, replica_groups=mesh['tz'=16,'tx'=4,'image'=2,'tensor'=4] {'tensor'}, dimensions={2}, use_global_device_ids=true | all-gather | bytes 51200 | tf_op jit(solution)/shard_map/all_gather | solution.py:153
  124.9 25.0 %all-gather.3 = bf16[512,256]{1,0:T(8,128)(2,1)} all-gather(bf16[32,256]{1,0:T(8,128)(2,1)S(1)} %convolution_convert_fusion), channel_id=5, replica_groups=mesh['tz'=16,'tx'=4,'image'=2,'tensor'=4] {'tz'}, dimensions={0}, use_global_device_ids=true | all-gather | bytes 278528 | tf_op jit(solution)/shard_map/all_gather | solution.py:156
  151.1 15.2 %all_gather.41 = bf16[4,640,128]{2,0,1:T(4,128)(2,1)S(1)} all-gather(bf16[4,160,128]{2,0,1:T(4,128)(2,1)S(1)} %copy.215), channel_id=1, replica_groups=mesh['tz'=16,'tx'=4,'image'=2,'tensor'=4] {'tensor'}, dimensions={1}, use_global_device_ids=true | all-gather | bytes 819200 | tf_op jit(solution)/shard_map/all_gather | solution.py:136
  167.9 12.9 %all-gather.10.cloned.1.call-done = bf16[64,32,256]{2,1,0:T(8,128)(2,1)} async-done(((bf16[16,32,256]{2,1,0:T(8,128)(2,1)}), bf16[64,32,256]{2,1,0:T(8,128)(2,1)}) %all-gather.10.cloned.1.call-update) | async-done | bytes 1048592 | tf_op jit(solution)/shard_map/all_gather | solution.py:157
  180.8 1.3 fusion.111
  183.2 1.1 select_reduce_fusion.1
  184.3 2.1 %fusion = (f32[512]{0:T(512)S(1)}, f32[512]{0:T(512)S(1)}) fusion(f32[512,2048]{1,0:T(8,128)S(1)} %get-tuple-element.50, f32[2048]{0:T(1024)S(1)} %get-tuple-element.17, f32[512]{0:T(512)S(1)} %get-tuple-element.7, pred[2048]{0:T(1024)(128)(4,1)S(1)} %get-tuple-element.18, f32[512]{0:T(512)S(1)} %get-tuple-element.8, f32[512,2048]{1,0:T(8,128)S(1)} %fusion.54), kind=kLoop, calls=%fused_computation.4 | loop fusion | flops 8387584 | bytes 8407040 | tf_op jit(solution)/shard_map/reduce_sum | solution.py:183
  186.4 1.0 fusion.22
  187.5 1.0 fusion.25
  188.5 8.6 %all_gather.47 = bf16[512,512]{0,1:T(8,128)(2,1)S(1)} all-gather(bf16[512,128]{0,1:T(8,128)(2,1)S(1)} %bitcast.197), channel_id=1, replica_groups=mesh['tz'=16,'tx'=4,'image'=2,'tensor'=4] {'tensor'}, dimensions={1}, use_global_device_ids=true | all-gather | bytes 655360 | tf_op jit(solution)/shard_map/all_gather | solution.py:194
  (81 shorter events, 15.3 us)
Async XLA Ops:
  6.5 27.8 %copy-start = (bf16[1,4,160,128]{3,2,1,0:T(8,128)(2,1)S(1)}, bf16[1,4,160,128]{3,2,1,0:T(8,128)(2,1)}, u32[]{:S(2)}) copy-start(bf16[1,4,160,128]{3,2,1,0:T(8,128)(2,1)} %param.13) | copy-start | bytes 491524
  6.5 21.7 %copy-start.3 = (s32[2,64]{1,0:T(2,128)S(1)}, s32[2,64]{1,0:T(2,128)}, u32[]{:S(2)}) copy-start(s32[2,64]{1,0:T(2,128)} %param.14) | copy-start | bytes 1540
  6.5 27.3 %copy-start.5 = (s32[2]{0:T(128)S(1)}, s32[2]{0:T(128)}, u32[]{:S(2)}) copy-start(s32[2]{0:T(128)} %param.15) | copy-start | bytes 28
  6.5 72.5 %all-gather.8.cloned.1.call-start = ((), (), s32[]{:S(2)}) async-start(), calls=%async_computation | async-start | bytes 1392640 | tf_op jit(solution)/shard_map/all_gather | solution.py:48
  8.1 172.7 %all-gather.10.cloned.1.call-start = ((), (), s32[]{:S(2)}) async-start(), calls=%async_computation.1 | async-start | bytes 1310720 | tf_op jit(solution)/shard_map/all_gather | solution.py:157
  10.6 64.6 %copy-start.4 = (bf16[640]{0:T(1024)(128)(2,1)S(1)}, bf16[640]{0:T(1024)(128)(2,1)}, u32[]{:S(2)}) copy-start(bf16[640]{0:T(1024)(128)(2,1)} %param.25) | copy-start | bytes 3844
  10.6 66.8 %collective-permute-start = (bf16[3,3,1,1,80,640]{5,4,3,2,1,0:T(8,128)(2,1)S(1)}, bf16[3,3,1,1,80,640]{5,4,3,2,1,0:T(8,128)(2,1)}, u32[]{:S(2)}, u32[]{:S(2)}) collective-permute-start(bf16[3,3,1,1,80,640]{5,4,3,2,1,0:T(8,128)(2,1)S(1)} %fusion.13), channel_id=1, source_target_pairs={{0,4},{4,0},{1,5},{5,1},{2,6},{6,2},{3,7},{7,3},{8,12},{12,8},{9,1... | collective-permute-start | bytes 2764808 | tf_op jit(solution)/shard_map/ppermute | solution.py:36
  17.2 58.0 %collective-permute-start.5 = (bf16[320,128]{1,0:T(8,128)(2,1)S(1)}, bf16[320,128]{1,0:T(8,128)(2,1)S(1)}, u32[]{:S(2)}, u32[]{:S(2)}) collective-permute-start(bf16[320,128]{1,0:T(8,128)(2,1)S(1)} %fusion.60), channel_id=1, source_target_pairs={{0,4},{4,0},{1,5},{5,1},{2,6},{6,2},{3,7},{7,3},{8,12},{12,8},{9,1... | collective-permute-start | bytes 245768 | tf_op jit(solution)/shard_map/ppermute | solution.py:36
  20.4 54.9 %collective-permute-start.6 = (bf16[320,2,128]{2,1,0:T(2,128)(2,1)S(1)}, bf16[320,2,128]{2,1,0:T(2,128)(2,1)}, u32[]{:S(2)}, u32[]{:S(2)}) collective-permute-start(bf16[320,2,128]{2,1,0:T(2,128)(2,1)S(1)} %fusion.39), channel_id=1, source_target_pairs={{0,4},{4,0},{1,5},{5,1},{2,6},{6,2},{3,7},{7,3},{8,12},{12,8},{9,1... | collective-permute-start | bytes 491528 | tf_op jit(solution)/shard_map/ppermute | solution.py:36
  26.2 123.7 %collective-permute-start.4 = (bf16[160,256]{1,0:T(8,128)(2,1)S(1)}, bf16[160,256]{1,0:T(8,128)(2,1)}, u32[]{:S(2)}, u32[]{:S(2)}) collective-permute-start(bf16[160,256]{1,0:T(8,128)(2,1)S(1)} %fusion.58), channel_id=1, source_target_pairs={{0,4},{4,0},{1,5},{5,1},{2,6},{6,2},{3,7},{7,3},{8,12},{12,8},{9,1... | collective-permute-start | bytes 245768 | tf_op jit(solution)/shard_map/ppermute | solution.py:36
  77.4 14.8 %copy-start.2 = (bf16[4,640,1,7,2]{1,3,4,0,2:T(8,128)(2,1)S(1)}, bf16[4,640,1,7,2]{1,3,4,0,2:T(8,128)(2,1)}, u32[]{:S(2)}) copy-start(bf16[4,640,1,7,2]{1,3,4,0,2:T(8,128)(2,1)} %slice.138) | copy-start | bytes 215044
  77.4 14.8 %copy-start.6 = (pred[8,17]{0,1:T(8,128)(4,1)S(1)}, pred[8,17]{0,1:T(8,128)(4,1)}, u32[]{:S(2)}) copy-start(pred[8,17]{0,1:T(8,128)(4,1)} %constant.280) | copy-start | bytes 412
  80.6 18.5 %collective-permute-start.1 = (bf16[2,160,128]{2,1,0:T(8,128)(2,1)}, bf16[2,160,128]{2,1,0:T(8,128)(2,1)}, u32[]{:S(2)}, u32[]{:S(2)}) collective-permute-start(bf16[2,160,128]{2,1,0:T(8,128)(2,1)} %pad_maximum_fusion.3), channel_id=1, source_target_pairs={{0,8},{8,16},{16,24},{24,0},{1,9},{9,17},{17,25},{25,1},{2,10},{10... | collective-permute-start | bytes 245768 | tf_op jit(solution)/shard_map/ppermute | solution.py:61
  84.1 15.0 %collective-permute-start.2 = (bf16[2,160,128]{2,1,0:T(8,128)(2,1)}, bf16[2,160,128]{2,1,0:T(8,128)(2,1)}, u32[]{:S(2)}, u32[]{:S(2)}) collective-permute-start(bf16[2,160,128]{2,1,0:T(8,128)(2,1)} %pad_maximum_fusion.4), channel_id=1, source_target_pairs={{0,16},{8,24},{16,0},{24,8},{1,17},{9,25},{17,1},{25,9},{2,18},{10... | collective-permute-start | bytes 245768 | tf_op jit(solution)/shard_map/ppermute | solution.py:61
  89.1 10.0 %collective-permute-start.3 = (bf16[2,160,128]{2,1,0:T(8,128)(2,1)}, bf16[2,160,128]{2,1,0:T(8,128)(2,1)}, u32[]{:S(2)}, u32[]{:S(2)}) collective-permute-start(bf16[2,160,128]{2,1,0:T(8,128)(2,1)} %pad_maximum_fusion.5), channel_id=1, source_target_pairs={{0,24},{8,0},{16,8},{24,16},{1,25},{9,1},{17,9},{25,17},{2,26},{10... | collective-permute-start | bytes 245768 | tf_op jit(solution)/shard_map/ppermute | solution.py:61
  100.2 24.5 %copy-start.1 = (bf16[640,2,128]{2,1,0:T(2,128)(2,1)S(1)}, bf16[640,2,128]{2,1,0:T(2,128)(2,1)}, u32[]{:S(2)}) copy-start(bf16[640,2,128]{2,1,0:T(2,128)(2,1)} %pad_maximum_fusion.1) | copy-start | bytes 983044
Sparse Core Ops, SparseCore 0:
  9.4 68.1 all-gather.7
  150.0 30.6 all-gather.9

commit v14 on v10

--- a/solution.py
+++ b/solution.py
@@ -141,9 +141,14 @@
     ).mean(axis=(1, 4))
     tok_count = pooled.shape[0] * pooled.shape[2]
     pooled = jnp.transpose(pooled, (0, 2, 1)).astype(jnp.bfloat16).reshape(tok_count, chan_shard)
-    pooled = lax.all_gather(pooled, "tensor", axis=1, tiled=True)
+    pooled = lax.all_gather(pooled, "tensor", axis=0, tiled=False)
     kv_flat = kv_w.reshape(channels, 2 * att_shard)
-    kv_local = jnp.dot(pooled, kv_flat, preferred_element_type=jnp.float32).astype(jnp.bfloat16)
+    kv_local = jnp.einsum(
+        "ktc,kcj->tj",
+        pooled,
+        kv_flat.reshape(pooled.shape[0], chan_shard, -1),
+        preferred_element_type=jnp.float32,
+    ).astype(jnp.bfloat16)
     kv_column = lax.all_gather(kv_local, "tz", axis=0, tiled=False)
     kv_all = lax.all_gather(kv_column, "tx", axis=0, tiled=False)
     n_z = kv_all.shape[1]

time: 202 us -> 202 us (level)
  transfers between devices with their start and end apart: 9 -> 9, of which waited for: 2 -> 2; matrix products, arithmetic and copies ran while one was open for 12% -> 13% of each run, Pallas kernels for 0% -> 0%
where the time goes in v14:
time: 202 us; the launch traced here: 201 us
  blocking collectives  82.7 us (41%)
  between operations  42.4 us (21%)
  starting transfers between devices  23.8 us (12%)
  other arithmetic  18.2 us (9%)
  waiting for transfers between devices  15.1 us (7%)
  local copies, waits for them, and re-layouts  10.7 us (5%)
  matrix products  8.31 us (4%)
    all_gather x1, blocking collectives, on_device(): kv_column = lax.all_gather(kv_local, 'tz', axis=0, tiled=False)  27.1 us
    all_gather x1, blocking collectives, on_device(): section_full = lax.all_gather(section, 'tensor', axis=1, tiled=True)  15 us
    ppermute x4, starting transfers between devices, image_pair(): other = lax.ppermute(part, 'image', [(0, 1), (1, 0)])  14.3 us
    all_gather x1, blocking collectives, on_device(): block_full = lax.all_gather(activated, 'tensor', axis=1, tiled=True)  13.9 us
    all_gather x1, waiting for transfers between devices, on_device(): kv_all = lax.all_gather(kv_column, 'tx', axis=0, tiled=False)  13.9 us
    all_gather x1, blocking collectives, on_device(): lax.all_gather(jnp.stack([upper, lower]), 'tensor', axis=1, tiled=True)  12.6 us
    ppermute x3, starting transfers between devices, halo_rows(): lax.ppermute(chunk, 'tx', [(i, (i + shift) % n_x) for i in range(n_x)])  9.4 us
    all_gather x1, blocking collectives, on_device(): attended_full = lax.all_gather(attended, 'tensor', axis=1, tiled=True)  8.84 us
  transfers between devices with their start and end apart: 9, of which 2 were waited for; matrix products, arithmetic and copies ran while one was open for 13% of the time, Pallas kernels for 0%

profile of v14, /device:TPU:1, one launch (start us, length us, event | category | flops | bytes accessed | tf_op | source)
XLA Modules:
  0.0 201.2 jit_solution(9910030086505995123)
XLA Ops:
  8.8 1.8 fusion.11
  10.6 5.7 %collective-permute-start = (bf16[3,3,1,1,80,640]{5,4,3,2,1,0:T(8,128)(2,1)S(1)}, bf16[3,3,1,1,80,640]{5,4,3,2,1,0:T(8,128)(2,1)}, u32[]{:S(2)}, u32[]{:S(2)}) collective-permute-start(bf16[3,3,1,1,80,640]{5,4,3,2,1,0:T(8,128)(2,1)S(1)} %fusion.11), channel_id=1, source_target_pairs={{0,4},{4,0},{1,5},{5,1},{2,6},{6,2},{3,7},{7,3},{8,12},{12,8},{9,1... | collective-permute-start | bytes 2764808 | tf_op jit(solution)/shard_map/ppermute | solution.py:36
  16.2 1.0 fusion.68
  17.2 1.9 collective-permute-start.5
  19.1 1.3 fusion.39
  20.4 4.9 %collective-permute-start.6 = (bf16[320,2,128]{2,1,0:T(2,128)(2,1)S(1)}, bf16[320,2,128]{2,1,0:T(2,128)(2,1)S(1)}, u32[]{:S(2)}, u32[]{:S(2)}) collective-permute-start(bf16[320,2,128]{2,1,0:T(2,128)(2,1)S(1)} %fusion.39), channel_id=1, source_target_pairs={{0,4},{4,0},{1,5},{5,1},{2,6},{6,2},{3,7},{7,3},{8,12},{12,8},{9,1... | collective-permute-start | bytes 491528 | tf_op jit(solution)/shard_map/ppermute | solution.py:36
  25.3 1.6 fusion.66
  26.9 1.9 collective-permute-start.4
  36.5 13.9 %all_gather.33 = bf16[4,640,128]{2,0,1:T(4,128)(2,1)S(1)} all-gather(bf16[4,160,128]{2,0,1:T(4,128)(2,1)S(1)} %copy.207), channel_id=1, replica_groups=mesh['tz'=16,'tx'=4,'image'=2,'tensor'=4] {'tensor'}, dimensions={1}, use_global_device_ids=true | all-gather | bytes 819200 | tf_op jit(solution)/shard_map/all_gather | solution.py:118
  73.7 1.0 copy.240
  77.3 0.9 reshape_reshape.3
  78.2 1.4 broadcast_select_fusion
  79.8 2.9 %convolution_select_fusion = f32[4,8,17,160]{3,1,2,0:T(8,128)S(1)} fusion(bf16[3,3,160,640]{3,2,1,0:T(8,128)(2,1)S(1)} %bitcast.193, bf16[4,640,1,7,2]{1,3,4,0,2:T(8,128)(2,1)S(1)} %slice.142, bf16[4,640,1,8,17]{1,3,4,0,2:T(8,128)(2,1)} %copy-done.2, pred[8,17]{0,1:T(8,128)(4,1)S(1)} %copy-done.9), kind=kOutput, calls=%fused_computation.28 | convolution fusion | flops 838005760 | bytes 2959496 | tf_op jit(solution)/shard_map/conv_general_dilated | solution.py:19
  83.2 0.9 fusion.97
  84.2 2.0 collective-permute-start.1
  86.2 4.4 %collective-permute-start.2 = (bf16[2,160,128]{2,1,0:T(8,128)(2,1)S(1)}, bf16[2,160,128]{2,1,0:T(8,128)(2,1)S(1)}, u32[]{:S(2)}, u32[]{:S(2)}) collective-permute-start(bf16[2,160,128]{2,1,0:T(8,128)(2,1)S(1)} %pad_maximum_fusion.4), channel_id=1, source_target_pairs={{0,16},{8,24},{16,0},{24,8},{1,17},{9,25},{17,1},{25,9},{2,18},{10... | collective-permute-start | bytes 245768 | tf_op jit(solution)/shard_map/ppermute | solution.py:61
  90.6 3.1 %collective-permute-start.3 = (bf16[2,160,128]{2,1,0:T(8,128)(2,1)S(1)}, bf16[2,160,128]{2,1,0:T(8,128)(2,1)S(1)}, u32[]{:S(2)}, u32[]{:S(2)}) collective-permute-start(bf16[2,160,128]{2,1,0:T(8,128)(2,1)S(1)} %pad_maximum_fusion.5), channel_id=1, source_target_pairs={{0,24},{8,0},{16,8},{24,16},{1,25},{9,1},{17,9},{25,17},{2,26},{10... | collective-permute-start | bytes 245768 | tf_op jit(solution)/shard_map/ppermute | solution.py:61
  93.6 1.0 fusion.30
  94.7 1.1 collective-permute-done.3
  95.8 0.9 fusion.89
  96.8 12.6 %all_gather.36 = bf16[2,640,128]{2,0,1:T(2,128)(2,1)S(1)} all-gather(bf16[2,160,128]{2,0,1:T(2,128)(2,1)S(1)} %copy.213), channel_id=1, replica_groups=mesh['tz'=16,'tx'=4,'image'=2,'tensor'=4] {'tensor'}, dimensions={1}, use_global_device_ids=true | all-gather | bytes 409600 | tf_op jit(solution)/shard_map/all_gather | solution.py:120
  112.2 5.2 %all_gather.38 = bf16[4,32,160]{2,1,0:T(8,128)(2,1)S(1)} all-gather(bf16[1,32,160]{2,1,0:T(8,128)(2,1)S(1)} %fusion.98), channel_id=1, replica_groups=mesh['tz'=16,'tx'=4,'image'=2,'tensor'=4] {'tensor'}, dimensions={0}, use_global_device_ids=true | all-gather | bytes 51200 | tf_op jit(solution)/shard_map/all_gather | solution.py:144
  117.7 27.1 %all-gather.1 = bf16[512,256]{1,0:T(8,128)(2,1)} all-gather(bf16[32,256]{1,0:T(8,128)(2,1)S(1)} %fusion.23), channel_id=3, replica_groups=mesh['tz'=16,'tx'=4,'image'=2,'tensor'=4] {'tz'}, dimensions={0}, use_global_device_ids=true | all-gather | bytes 278528 | tf_op jit(solution)/shard_map/all_gather | solution.py:152
  144.9 0.9 broadcast_select_fusion.7
  146.0 15.0 %all_gather.37 = bf16[4,640,128]{2,0,1:T(4,128)(2,1)S(1)} all-gather(bf16[4,160,128]{2,0,1:T(4,128)(2,1)S(1)} %copy.226), channel_id=1, replica_groups=mesh['tz'=16,'tx'=4,'image'=2,'tensor'=4] {'tensor'}, dimensions={1}, use_global_device_ids=true | all-gather | bytes 819200 | tf_op jit(solution)/shard_map/all_gather | solution.py:127
  162.7 13.9 %all-gather.8.cloned.1.call-done = bf16[64,32,256]{2,1,0:T(8,128)(2,1)} async-done(((bf16[16,32,256]{2,1,0:T(8,128)(2,1)}), bf16[64,32,256]{2,1,0:T(8,128)(2,1)}) %all-gather.8.cloned.1.call-update) | async-done | bytes 1048592 | tf_op jit(solution)/shard_map/all_gather | solution.py:153
  176.6 1.3 fusion.124
  179.1 1.1 select_reduce_fusion.1
  180.1 2.1 %fusion = (f32[512]{0:T(512)S(1)}, f32[512]{0:T(512)S(1)}) fusion(f32[512,2048]{1,0:T(8,128)S(1)} %get-tuple-element.48, f32[2048]{0:T(1024)S(1)} %get-tuple-element.17, f32[512]{0:T(512)S(1)} %get-tuple-element.7, pred[2048]{0:T(1024)(128)(4,1)S(1)} %get-tuple-element.18, f32[512]{0:T(512)S(1)} %get-tuple-element.8, f32[512,2048]{1,0:T(8,128)S(1)} %fusion.50), kind=kLoop, calls=%fused_computation.4 | loop fusion | flops 8387584 | bytes 8407040 | tf_op jit(solution)/shard_map/reduce_sum | solution.py:179
  182.3 1.0 fusion.17
  183.3 1.0 fusion.20
  184.4 8.8 %all_gather.43 = bf16[512,512]{0,1:T(8,128)(2,1)S(1)} all-gather(bf16[512,128]{0,1:T(8,128)(2,1)S(1)} %bitcast.209), channel_id=1, replica_groups=mesh['tz'=16,'tx'=4,'image'=2,'tensor'=4] {'tensor'}, dimensions={1}, use_global_device_ids=true | all-gather | bytes 655360 | tf_op jit(solution)/shard_map/all_gather | solution.py:190
  (102 shorter events, 15.2 us)
Async XLA Ops:
  6.5 22.2 %copy-start = (bf16[1,4,160,128]{3,2,1,0:T(8,128)(2,1)S(1)}, bf16[1,4,160,128]{3,2,1,0:T(8,128)(2,1)}, u32[]{:S(2)}) copy-start(bf16[1,4,160,128]{3,2,1,0:T(8,128)(2,1)} %param.13) | copy-start | bytes 491524
  6.5 22.4 %copy-start.6 = (s32[2,64]{1,0:T(2,128)S(1)}, s32[2,64]{1,0:T(2,128)}, u32[]{:S(2)}) copy-start(s32[2,64]{1,0:T(2,128)} %param.14) | copy-start | bytes 1540
  6.5 28.2 %copy-start.8 = (s32[2]{0:T(128)S(1)}, s32[2]{0:T(128)}, u32[]{:S(2)}) copy-start(s32[2]{0:T(128)} %param.15) | copy-start | bytes 28
  6.5 76.7 %all-gather.6.cloned.1.call-start = ((), (), s32[]{:S(2)}) async-start(), calls=%async_computation | async-start | bytes 1392640 | tf_op jit(solution)/shard_map/all_gather | solution.py:48
  8.1 168.5 %all-gather.8.cloned.1.call-start = ((), (), s32[]{:S(2)}) async-start(), calls=%async_computation.1 | async-start | bytes 1310720 | tf_op jit(solution)/shard_map/all_gather | solution.py:153
  10.6 65.4 %copy-start.7 = (bf16[640]{0:T(1024)(128)(2,1)S(1)}, bf16[640]{0:T(1024)(128)(2,1)}, u32[]{:S(2)}) copy-start(bf16[640]{0:T(1024)(128)(2,1)} %param.25) | copy-start | bytes 3844
  10.6 67.6 %collective-permute-start = (bf16[3,3,1,1,80,640]{5,4,3,2,1,0:T(8,128)(2,1)S(1)}, bf16[3,3,1,1,80,640]{5,4,3,2,1,0:T(8,128)(2,1)}, u32[]{:S(2)}, u32[]{:S(2)}) collective-permute-start(bf16[3,3,1,1,80,640]{5,4,3,2,1,0:T(8,128)(2,1)S(1)} %fusion.11), channel_id=1, source_target_pairs={{0,4},{4,0},{1,5},{5,1},{2,6},{6,2},{3,7},{7,3},{8,12},{12,8},{9,1... | collective-permute-start | bytes 2764808 | tf_op jit(solution)/shard_map/ppermute | solution.py:36
  17.2 58.9 %collective-permute-start.5 = (bf16[320,128]{1,0:T(8,128)(2,1)S(1)}, bf16[320,128]{1,0:T(8,128)(2,1)S(1)}, u32[]{:S(2)}, u32[]{:S(2)}) collective-permute-start(bf16[320,128]{1,0:T(8,128)(2,1)S(1)} %fusion.68), channel_id=1, source_target_pairs={{0,4},{4,0},{1,5},{5,1},{2,6},{6,2},{3,7},{7,3},{8,12},{12,8},{9,1... | collective-permute-start | bytes 245768 | tf_op jit(solution)/shard_map/ppermute | solution.py:36
  20.4 56.4 %collective-permute-start.6 = (bf16[320,2,128]{2,1,0:T(2,128)(2,1)S(1)}, bf16[320,2,128]{2,1,0:T(2,128)(2,1)S(1)}, u32[]{:S(2)}, u32[]{:S(2)}) collective-permute-start(bf16[320,2,128]{2,1,0:T(2,128)(2,1)S(1)} %fusion.39), channel_id=1, source_target_pairs={{0,4},{4,0},{1,5},{5,1},{2,6},{6,2},{3,7},{7,3},{8,12},{12,8},{9,1... | collective-permute-start | bytes 491528 | tf_op jit(solution)/shard_map/ppermute | solution.py:36
  26.9 118.0 %collective-permute-start.4 = (bf16[160,256]{1,0:T(8,128)(2,1)}, bf16[160,256]{1,0:T(8,128)(2,1)}, u32[]{:S(2)}, u32[]{:S(2)}) collective-permute-start(bf16[160,256]{1,0:T(8,128)(2,1)} %fusion.66), channel_id=1, source_target_pairs={{0,4},{4,0},{1,5},{5,1},{2,6},{6,2},{3,7},{7,3},{8,12},{12,8},{9,1... | collective-permute-start | bytes 245768 | tf_op jit(solution)/shard_map/ppermute | solution.py:36
  75.1 0.9 copy-start.2
  76.8 3.0 %copy-start.9 = (pred[8,17]{0,1:T(8,128)(4,1)S(1)}, pred[8,17]{0,1:T(8,128)(4,1)}, u32[]{:S(2)}) copy-start(pred[8,17]{0,1:T(8,128)(4,1)} %constant.283) | copy-start | bytes 412
  84.2 10.5 %collective-permute-start.1 = (bf16[2,160,128]{2,1,0:T(8,128)(2,1)S(1)}, bf16[2,160,128]{2,1,0:T(8,128)(2,1)S(1)}, u32[]{:S(2)}, u32[]{:S(2)}) collective-permute-start(bf16[2,160,128]{2,1,0:T(8,128)(2,1)S(1)} %pad_maximum_fusion.3), channel_id=1, source_target_pairs={{0,8},{8,16},{16,24},{24,0},{1,9},{9,17},{17,25},{25,1},{2,10},{10... | collective-permute-start | bytes 245768 | tf_op jit(solution)/shard_map/ppermute | solution.py:61
  86.2 8.5 %collective-permute-start.2 = (bf16[2,160,128]{2,1,0:T(8,128)(2,1)S(1)}, bf16[2,160,128]{2,1,0:T(8,128)(2,1)S(1)}, u32[]{:S(2)}, u32[]{:S(2)}) collective-permute-start(bf16[2,160,128]{2,1,0:T(8,128)(2,1)S(1)} %pad_maximum_fusion.4), channel_id=1, source_target_pairs={{0,16},{8,24},{16,0},{24,8},{1,17},{9,25},{17,1},{25,9},{2,18},{10... | collective-permute-start | bytes 245768 | tf_op jit(solution)/shard_map/ppermute | solution.py:61
  90.6 5.2 %collective-permute-start.3 = (bf16[2,160,128]{2,1,0:T(8,128)(2,1)S(1)}, bf16[2,160,128]{2,1,0:T(8,128)(2,1)S(1)}, u32[]{:S(2)}, u32[]{:S(2)}) collective-permute-start(bf16[2,160,128]{2,1,0:T(8,128)(2,1)S(1)} %pad_maximum_fusion.5), channel_id=1, source_target_pairs={{0,24},{8,0},{16,8},{24,16},{1,25},{9,1},{17,9},{25,17},{2,26},{10... | collective-permute-start | bytes 245768 | tf_op jit(solution)/shard_map/ppermute | solution.py:61
  94.6 15.6 %copy-start.3 = (bf16[1,3,1,2,80,640]{5,4,3,2,1,0:T(8,128)(2,1)S(1)}, bf16[1,3,1,2,80,640]{5,4,3,2,1,0:T(8,128)(2,1)}, u32[]{:S(2)}) copy-start(bf16[1,3,1,2,80,640]{5,4,3,2,1,0:T(8,128)(2,1)} %get-tuple-element.20) | copy-start | bytes 1843204
  110.1 7.4 %copy-start.1 = (bf16[4,160,256]{2,1,0:T(8,128)(2,1)S(1)}, bf16[4,160,256]{2,1,0:T(8,128)(2,1)}, u32[]{:S(2)}) copy-start(bf16[4,160,256]{2,1,0:T(8,128)(2,1)} %reshape_reshape.3) | copy-start | bytes 983044
  111.7 50.6 %copy-start.4 = (bf16[320,128]{1,0:T(8,128)(2,1)S(1)}, bf16[320,128]{1,0:T(8,128)(2,1)}, u32[]{:S(2)}) copy-start(bf16[320,128]{1,0:T(8,128)(2,1)} %get-tuple-element.40) | copy-start | bytes 245764
  111.7 50.6 %copy-start.5 = (bf16[320,128]{1,0:T(8,128)(2,1)S(1)}, bf16[320,128]{1,0:T(8,128)(2,1)}, u32[]{:S(2)}) copy-start(bf16[320,128]{1,0:T(8,128)(2,1)} %get-tuple-element.41) | copy-start | bytes 245764
Sparse Core Ops, SparseCore 0:
  9.4 68.0 all-gather.5
  145.0 31.5 all-gather.7
